TPU v7x, 256 devices: a whole 4x4x8 slice. The times are simulated.
256 devices in a mesh: span: 8 (over y, x_hi), tm: 32 (over x_lo, z, core).
Axes of the slice: x: 4 (x_hi: 2, x_lo: 2; x = x_hi * 2 + x_lo), y: 4, z: 8, core: 2. Of those that a mesh axis runs over, the one named last changes fastest.
Arguments:
- launched: float32 [8, 2, 110, 8192], P(None, None, None, 'tm'), may hold values from -1.5 to 1.5
- coupling: float32 [8, 2, 2, 2, 110, 110], P('span'), may hold values from -2 to 2
- impulse: float32 [8, 2, 2, 2, 129], P('span'), may hold values from -1.5 to 1.5
- amplifier: float32 [8, 2, 110], P('span'), may hold values from 0.9 to 1.11
- nonlinear: float32 [8, 2, 2], P('span'), may hold values from 0.002 to 0.008
Outputs:
- monitored: float32 [8, 8, 2, 110, 8192], P('span', None, None, None, 'tm')
All inputs are finite; a program needn't handle non-finite values.
Results may differ from a plain program's by a relative error of at most 0.0004.
Values sent between devices are 32-bit elements; how exact they have to be, the bound alone decides.
No kernel may reach another device: no remote copies, remote signals or barrier semaphores. Data moves between devices by JAX's collectives and lax.ppermute only.
A program may use at most 64 MiB of HBM per device.

v0:
```python
import jax
import jax.numpy as jnp
from jax import lax
from jax.sharding import PartitionSpec as P


def padded_2(block, sides, width):
    for axis, dim in sides:
        count = lax.axis_size(axis)
        forward = [(i, i + 1) for i in range(count - 1)]
        backward = [(target, source) for source, target in forward]
        low = lax.ppermute(
            lax.slice_in_dim(block, block.shape[dim] - width, None, axis=dim), axis, forward
        )
        high = lax.ppermute(lax.slice_in_dim(block, 0, width, axis=dim), axis, backward)
        block = jnp.concatenate([low, block, high], axis=dim)
    return block


def passed_along(value, axis, by):
    length = lax.axis_size(axis)
    pairs = [(i, i + by) for i in range(length) if 0 <= i + by < length]
    return lax.ppermute(value, axis, pairs)


def band(values, width):
    padded = jnp.concatenate([values, jnp.zeros((width,), jnp.float32)])
    tiled = jnp.tile(padded, width)[: width * 2 * width]
    return tiled.reshape(width, 2 * width).T


def prepare(coupling_group, impulse_group):
    half_taps = (impulse_group.shape[-1] - 1) // 2
    width = 2 * half_taps

    def toeplitz(pair):
        real_band = band(pair[0], width)
        imag_band = band(pair[1], width)
        upper = jnp.concatenate([real_band, imag_band], axis=1)
        lower = jnp.concatenate([-imag_band, real_band], axis=1)
        return jnp.concatenate([upper, lower], axis=0)

    filters = jax.vmap(jax.vmap(toeplitz))(impulse_group)
    real_part = coupling_group[:, :, 0]
    imag_part = coupling_group[:, :, 1]
    upper = jnp.concatenate([real_part, -imag_part], axis=-1)
    lower = jnp.concatenate([imag_part, real_part], axis=-1)
    return (filters, jnp.concatenate([upper, lower], axis=-2))


def disperse(extended, matrix, half_taps):
    width = 2 * half_taps
    frames, _, channels, extent = extended.shape
    block_count = extent // width - 1
    blocks = extended.reshape(frames, 2, channels, block_count + 1, width)
    windows = jnp.concatenate([blocks[..., :-1, :], blocks[..., 1:, :]], axis=-1)
    stacked = jnp.concatenate([windows[:, 0], windows[:, 1]], axis=-1)
    product = jnp.einsum("fcbu,uv->fcbv", stacked, matrix, precision=lax.Precision.HIGHEST)
    real_part = product[..., :width].reshape(frames, channels, block_count * width)
    imag_part = product[..., width:].reshape(frames, channels, block_count * width)
    return jnp.stack([real_part, imag_part], axis=1)


def couple(signal, mixer, coefficient):
    frames, _, channels, extent = signal.shape
    flat = signal.reshape(frames, 2 * channels, extent)
    mixed = jnp.einsum("de,fel->fdl", mixer, flat, precision=lax.Precision.HIGHEST).reshape(
        frames, 2, channels, extent
    )
    power = jnp.sum(mixed * mixed, axis=(1, 2))
    phase = coefficient * power[:, None, :]
    cosine = jnp.cos(phase)
    sine = jnp.sin(phase)
    real_part = mixed[:, 0]
    imag_part = mixed[:, 1]
    return jnp.stack(
        [real_part * cosine - imag_part * sine, real_part * sine + imag_part * cosine], axis=1
    )


def propagate(signal, filters, mixers, amplifier_group, nonlinear_group):
    span_count, step_count = nonlinear_group.shape
    half_taps = filters.shape[-1] // 4
    margin = 0
    for span_index in range(span_count):
        for step_index in range(step_count):
            signal = padded_2(signal, (("tm", 3),), half_taps)
            margin = half_taps
            signal = disperse(signal, filters[span_index, step_index], half_taps)
            margin = margin - half_taps
            signal = couple(
                signal, mixers[span_index, step_index], nonlinear_group[span_index, step_index]
            )
        signal = signal * amplifier_group[span_index][None, None, :, None]
    return signal


def shards(launched, coupling, impulse, amplifier, nonlinear):
    frames_count = launched.shape[0]
    sections = lax.axis_size("span")
    section_index = lax.axis_index("span")
    filters, mixers = prepare(coupling[0], impulse[0])
    amplifier_group = amplifier[0]
    nonlinear_group = nonlinear[0]

    def advance(carry, moment):
        received, stored = carry
        source = lax.dynamic_index_in_dim(
            launched, jnp.minimum(moment, frames_count - 1), 0, keepdims=True
        )
        incoming = jnp.where(section_index == 0, source, received)
        result = propagate(incoming, filters, mixers, amplifier_group, nonlinear_group)
        frame_slot = moment - section_index
        usable = (frame_slot >= 0) & (frame_slot < frames_count)
        position = jnp.clip(frame_slot, 0, frames_count - 1)
        previous = lax.dynamic_index_in_dim(stored, position, 0, keepdims=True)
        stored = lax.dynamic_update_index_in_dim(
            stored, jnp.where(usable, result, previous), position, 0
        )
        passed = passed_along(result, "span", 1)
        return ((passed, stored), None)

    start = (jnp.zeros_like(launched[:1]), jnp.zeros_like(launched))
    moments = jnp.arange(frames_count + sections - 1, dtype=jnp.int32)
    (_, stored), _ = lax.scan(advance, start, moments)
    return stored[None]


def solution(mesh):
    placed = (
        P(None, None, None, "tm"),
        P("span", None, None, None, None, None),
        P("span", None, None, None, None),
        P("span", None, None),
        P("span", None, None),
    )
    return jax.shard_map(
        shards,
        mesh=mesh,
        in_specs=placed,
        out_specs=P("span", None, None, None, "tm"),
        check_vma=False,
    )
```

profile of v0, /device:TPU:2, one launch (start us, length us, event | category | flops | bytes accessed | tf_op | source)
XLA Modules:
  0.0 1096.4 jit_solution(11867473501314037659)
XLA Ops:
  11.9 1084.5 %while.13 = (s32[]{:T(128)}, f32[1,2,110,256]{3,2,1,0:T(8,128)S(1)}, f32[8,2,110,256]{3,1,2,0:T(2,128)}, pred[]{:T(512)}, s32[15]{0:T(128)}, /*index=5*/f32[8,2,...) while((s32[]{:T(128)}, ...), condition=%wide.region_5.6_spmd, body=%wide.region_0.5_spmd.sunk | while | flops 1982351360 | bytes 41830600 | solution.py:125
  15.9 7.2 collective-permute-start
  54.5 5.8 collective-permute-done.5
  69.0 5.9 collective-permute-done.7
  124.3 5.8 collective-permute-done.5
  148.9 5.9 collective-permute-start.8
  195.7 5.9 collective-permute-done.5
  220.4 5.9 collective-permute-start.8
  267.2 5.8 collective-permute-done.5
  291.8 5.9 collective-permute-start.8
  338.6 5.8 collective-permute-done.5
  363.3 6.8 collective-permute-start.8
  410.9 5.8 collective-permute-done.5
  435.6 6.7 collective-permute-start.8
  483.1 5.8 collective-permute-done.5
  507.7 6.8 collective-permute-start.8
  555.4 5.8 collective-permute-done.5
  580.1 6.9 collective-permute-start.8
  628.0 5.8 collective-permute-done.5
  652.6 6.8 collective-permute-start.8
  700.3 5.8 collective-permute-done.5
  725.0 6.6 collective-permute-start.8
  772.4 5.8 collective-permute-done.5
  797.0 6.8 collective-permute-start.8
  844.7 5.8 collective-permute-done.5
  869.3 6.8 collective-permute-start.8
  916.9 5.8 collective-permute-done.5
  941.6 6.8 collective-permute-start.8
  989.2 5.8 collective-permute-done.5
  1013.8 6.8 collective-permute-start.8
  1061.5 5.8 collective-permute-done.5
  1086.1 6.8 collective-permute-start.8
  (1493 shorter events, 874.7 us)
Async XLA Ops:
  15.9 9.8 collective-permute-start
  66.5 8.3 collective-permute-start.7
  92.9 8.2 collective-permute-start.1
  136.3 8.2 collective-permute-start.7
  148.9 9.4 collective-permute-start.8
  193.3 8.3 collective-permute-start.5
  220.4 9.4 collective-permute-start.8
  250.1 8.2 collective-permute-start.3
  264.7 8.2 collective-permute-start.5
  291.8 9.4 collective-permute-start.8
  307.1 8.2 collective-permute-start.1
  321.5 8.3 collective-permute-start.3
  363.3 10.3 collective-permute-start.8
  379.6 8.2 collective-permute-start.1
  408.5 8.2 collective-permute-start.5
  435.6 10.2 collective-permute-start.8
  451.7 8.2 collective-permute-start.1
  507.7 10.3 collective-permute-start.8
  524.0 8.3 collective-permute-start.1
  567.5 8.2 collective-permute-start.7
  580.1 10.5 collective-permute-start.8
  596.5 8.3 collective-permute-start.1
  652.6 10.3 collective-permute-start.8
  668.8 8.3 collective-permute-start.1
  683.3 8.2 collective-permute-start.3
  697.9 8.2 collective-permute-start.5
  725.0 10.1 collective-permute-start.8
  797.0 10.3 collective-permute-start.8
  869.3 10.3 collective-permute-start.8
  941.6 10.3 collective-permute-start.8
  1013.8 10.3 collective-permute-start.8
  1086.1 10.3 collective-permute-start.8
  (149 other events, 852.9 us)
where the time goes:
time: 1110 us; the launch traced here: 1100 us
  waiting for transfers between devices  370 us (33%)
  starting transfers between devices  361 us (33%)
  local copies, waits for them, and re-layouts  122 us (11%)
  matrix products  112 us (10%)
  other arithmetic  103 us (9%)
  loops' own time  29.1 us (3%)
    ppermute x60, waiting for transfers between devices, padded_2(): lax.ppermute(lax.slice_in_dim(block, block.shape[dim] - width, None, axis...  331 us
    ppermute x60, starting transfers between devices, padded_2(): lax.ppermute(lax.slice_in_dim(block, block.shape[dim] - width, None, axis...  144 us
    ppermute x60, starting transfers between devices, padded_2(): lax.ppermute(lax.slice_in_dim(block, 0, width, axis=dim), axis, backward)  120 us
    ppermute x15, starting transfers between devices, passed_along(): return lax.ppermute(value, axis, pairs)  96.6 us
    dot_general x60, matrix products, couple(): jnp.einsum('de,fel->fdl', mixer, flat, precision=lax.Precision.HIGHEST)  79.2 us
    cos x60, other arithmetic, couple(): cosine = jnp.cos(phase)  41.7 us
    ppermute x15, waiting for transfers between devices, passed_along(): return lax.ppermute(value, axis, pairs)  39.6 us
    another operation x60, other arithmetic, disperse(): return jnp.stack([real_part, imag_part], axis=1)  37 us
  transfers between devices with their start and end apart: 135, of which 75 were waited for; matrix products, arithmetic and copies ran while one was open for 3% of the time, Pallas kernels for 0%

commit v1 on v0

--- a/solution.py
+++ b/solution.py
@@ -2,25 +2,6 @@
 import jax.numpy as jnp
 from jax import lax
 from jax.sharding import PartitionSpec as P
-
-
-def padded_2(block, sides, width):
-    for axis, dim in sides:
-        count = lax.axis_size(axis)
-        forward = [(i, i + 1) for i in range(count - 1)]
-        backward = [(target, source) for source, target in forward]
-        low = lax.ppermute(
-            lax.slice_in_dim(block, block.shape[dim] - width, None, axis=dim), axis, forward
-        )
-        high = lax.ppermute(lax.slice_in_dim(block, 0, width, axis=dim), axis, backward)
-        block = jnp.concatenate([low, block, high], axis=dim)
-    return block
-
-
-def passed_along(value, axis, by):
-    length = lax.axis_size(axis)
-    pairs = [(i, i + by) for i in range(length) if 0 <= i + by < length]
-    return lax.ppermute(value, axis, pairs)
 
 
 def band(values, width):
@@ -78,52 +59,63 @@
     )
 
 
-def propagate(signal, filters, mixers, amplifier_group, nonlinear_group):
+def neighbours(block, halo):
+    count = lax.axis_size("tm")
+    forward = [(i, i + 1) for i in range(count - 1)]
+    backward = [(i + 1, i) for i in range(count - 1)]
+    extent = block.shape[-1]
+    low = lax.ppermute(lax.slice_in_dim(block, extent - halo, None, axis=3), "tm", forward)
+    high = lax.ppermute(lax.slice_in_dim(block, 0, halo, axis=3), "tm", backward)
+    return jnp.concatenate([low, block, high], axis=3)
+
+
+def group_pass(signal, filters, mixers, amplifier_group, nonlinear_group, origin, length):
     span_count, step_count = nonlinear_group.shape
     half_taps = filters.shape[-1] // 4
-    margin = 0
+    halo = span_count * step_count * half_taps
+    extent = signal.shape[-1]
+    signal = neighbours(signal, halo)
+    offset = -halo
     for span_index in range(span_count):
         for step_index in range(step_count):
-            signal = padded_2(signal, (("tm", 3),), half_taps)
-            margin = half_taps
             signal = disperse(signal, filters[span_index, step_index], half_taps)
-            margin = margin - half_taps
+            offset = offset + half_taps
+            where = origin + offset + jnp.arange(signal.shape[-1], dtype=jnp.int32)
+            inside = ((where >= 0) & (where < length)).astype(jnp.float32)
+            signal = signal * inside
             signal = couple(
                 signal, mixers[span_index, step_index], nonlinear_group[span_index, step_index]
             )
         signal = signal * amplifier_group[span_index][None, None, :, None]
+    assert signal.shape[-1] == extent
     return signal
 
 
 def shards(launched, coupling, impulse, amplifier, nonlinear):
-    frames_count = launched.shape[0]
     sections = lax.axis_size("span")
     section_index = lax.axis_index("span")
-    filters, mixers = prepare(coupling[0], impulse[0])
-    amplifier_group = amplifier[0]
-    nonlinear_group = nonlinear[0]
+    frames_count, _, _, extent = launched.shape
+    per_section = frames_count // sections
+    length = extent * lax.axis_size("tm")
+    origin = lax.axis_index("tm") * extent
 
-    def advance(carry, moment):
-        received, stored = carry
-        source = lax.dynamic_index_in_dim(
-            launched, jnp.minimum(moment, frames_count - 1), 0, keepdims=True
+    coupling_all = lax.all_gather(coupling, "span", axis=0, tiled=True)
+    impulse_all = lax.all_gather(impulse, "span", axis=0, tiled=True)
+    amplifier_all = lax.all_gather(amplifier, "span", axis=0, tiled=True)
+    nonlinear_all = lax.all_gather(nonlinear, "span", axis=0, tiled=True)
+
+    signal = lax.dynamic_slice_in_dim(launched, section_index * per_section, per_section, 0)
+
+    def advance(signal, params):
+        coupling_group, impulse_group, amplifier_group, nonlinear_group = params
+        filters, mixers = prepare(coupling_group, impulse_group)
+        signal = group_pass(
+            signal, filters, mixers, amplifier_group, nonlinear_group, origin, length
         )
-        incoming = jnp.where(section_index == 0, source, received)
-        result = propagate(incoming, filters, mixers, amplifier_group, nonlinear_group)
-        frame_slot = moment - section_index
-        usable = (frame_slot >= 0) & (frame_slot < frames_count)
-        position = jnp.clip(frame_slot, 0, frames_count - 1)
-        previous = lax.dynamic_index_in_dim(stored, position, 0, keepdims=True)
-        stored = lax.dynamic_update_index_in_dim(
-            stored, jnp.where(usable, result, previous), position, 0
-        )
-        passed = passed_along(result, "span", 1)
-        return ((passed, stored), None)
+        return signal, signal
 
-    start = (jnp.zeros_like(launched[:1]), jnp.zeros_like(launched))
-    moments = jnp.arange(frames_count + sections - 1, dtype=jnp.int32)
-    (_, stored), _ = lax.scan(advance, start, moments)
-    return stored[None]
+    _, stacked = lax.scan(advance, signal, (coupling_all, impulse_all, amplifier_all, nonlinear_all))
+    return lax.all_to_all(stacked, "span", 0, 1, tiled=True)
 
 
 def solution(mesh):

time: 1110 us -> 698 us (0.63)
  waiting for transfers between devices: 370 us -> 0.75 us
  starting transfers between devices: 361 us -> 60.5 us
  local copies, waits for them, and re-layouts: 122 us -> 275 us
  blocking collectives: 0 us -> 105 us
  other arithmetic: 103 us -> 132 us
  loops' own time: 29.1 us -> 3.87 us
  matrix products: 112 us -> 98.7 us
  between operations: 0.13 us -> 13.4 us
    ppermute x135 -> x16, waiting for transfers between devices: 370 us -> 0.04 us  [the longest x8 0.02 us: neighbours(): lax.ppermute(lax.slice_in_dim(block, 0, halo, axis=3), 'tm', backward)]
    ppermute x135 -> x16, starting transfers between devices: 361 us -> 60.5 us  [the longest x8 44.6 us: neighbours(): lax.ppermute(lax.slice_in_dim(block, 0, halo, axis=3), 'tm', backward)]
    all_gather x0 -> x3, blocking collectives: none -> 78.3 us  [the longest x1 37 us: shards(): impulse_all = lax.all_gather(impulse, 'span', axis=0, tiled=True)]
    dot_general x60 -> x32, matrix products: 79.2 us -> 39.6 us  [couple(): jnp.einsum('de,fel->fdl', mixer, flat, precision=lax.Precision.HIGHEST)]
    reshape x2 -> x32, local copies, waits for them, and re-layouts: 0.9 us -> 40 us  [band(): return tiled.reshape(width, 2 * width).T]
    another operation x60 -> x0, other arithmetic: 37 us -> none  [disperse(): return jnp.stack([real_part, imag_part], axis=1)]
    mul x15 -> x56, other arithmetic: 1.22 us -> 33.8 us  [the longest x32 26.3 us: group_pass(): signal = signal * inside]
    dot_general x60 -> x32, matrix products: 32.5 us -> 59.1 us  [disperse(): jnp.einsum('fcbu,uv->fcbv', stacked, matrix, precision=lax.Precision.HIGH...]
  transfers between devices with their start and end apart: 135 -> 17, of which waited for: 75 -> 0; matrix products, arithmetic and copies ran while one was open for 3% -> 20% of each run, Pallas kernels for 0% -> 0%
where the time goes in v1:
time: 698 us; the launch traced here: 690 us
  local copies, waits for them, and re-layouts  275 us (39%)
  other arithmetic  132 us (19%)
  blocking collectives  105 us (15%)
  matrix products  98.7 us (14%)
  starting transfers between devices  60.5 us (9%)
  between operations  13.4 us (2%)
    dot_general x32, matrix products, disperse(): jnp.einsum('fcbu,uv->fcbv', stacked, matrix, precision=lax.Precision.HIGH...  59.1 us
    ppermute x8, starting transfers between devices, neighbours(): lax.ppermute(lax.slice_in_dim(block, 0, halo, axis=3), 'tm', backward)  44.6 us
    reshape x32, local copies, waits for them, and re-layouts, band(): return tiled.reshape(width, 2 * width).T  40 us
    dot_general x32, matrix products, couple(): jnp.einsum('de,fel->fdl', mixer, flat, precision=lax.Precision.HIGHEST)  39.6 us
    all_gather x1, blocking collectives, shards(): impulse_all = lax.all_gather(impulse, 'span', axis=0, tiled=True)  37 us
    while x80, local copies, waits for them, and re-layouts  28.2 us
    all_to_all x1, blocking collectives, shards(): return lax.all_to_all(stacked, 'span', 0, 1, tiled=True)  26.3 us
    mul x32, other arithmetic, group_pass(): signal = signal * inside  26.3 us
  transfers between devices with their start and end apart: 17, of which 0 were waited for; matrix products, arithmetic and copies ran while one was open for 20% of the time, Pallas kernels for 0%

profile of v1, /device:TPU:2, one launch (start us, length us, event | category | flops | bytes accessed | tf_op | source)
XLA Modules:
  0.0 689.6 jit_solution(1994653478486105164)
XLA Ops:
  8.7 22.9 %all_gather.14 = f32[8,2,2]{2,1,0:T(2,128)S(1)} all-gather(f32[1,2,2]{2,1,0:T(2,128)} %param.11), channel_id=1, replica_groups=mesh['span'=8,'tm'=32] {'span'}, dimensions={0}, use_global_device_ids=true | all-gather | bytes 144 | tf_op jit(solution)/shard_map/all_gather | solution.py:105
  31.7 18.4 %all_gather.15 = f32[8,2,110]{2,1,0:T(2,128)S(1)} all-gather(f32[1,2,110]{2,1,0:T(2,128)} %param.10), channel_id=1, replica_groups=mesh['span'=8,'tm'=32] {'span'}, dimensions={0}, use_global_device_ids=true | all-gather | bytes 7920 | tf_op jit(solution)/shard_map/all_gather | solution.py:104
  50.1 37.0 %all_gather.12 = f32[8,2,2,2,129]{4,3,2,1,0:T(2,128)} all-gather(f32[1,2,2,2,129]{4,3,2,1,0:T(2,128)} %param.9), channel_id=1, replica_groups=mesh['span'=8,'tm'=32] {'span'}, dimensions={0}, use_global_device_ids=true | all-gather | bytes 37152 | tf_op jit(solution)/shard_map/all_gather | solution.py:103
  87.1 568.2 %while.13 = (s32[]{:T(128)}, f32[1,2,110,256]{3,2,1,0:T(8,128)}, f32[8,1,2,110,256]{4,2,3,1,0:T(2,128)}, f32[8,2,2,2,129]{4,3,2,1,0:T(2,128)}, s32[]{:T(128)}, /...) while((s32[]{:T(128)}, f32[1,2,110,256]{3,2,1,0:T(8,128)}, ...), condition=%wide.region_5.6_spmd, body=%wide.region_0.5_spmd.sunk | while | flops 3470978304 | bytes 83243504 | solution.py:117
  89.0 2.4 collective-permute-start.1
  106.0 2.7 maximum_maximum_fusion.4
  138.9 2.4 multiply_reduce_fusion.9
  154.8 8.4 %collective-permute-start = (f32[1,2,110,256]{3,2,1,0:T(8,128)}, f32[1,2,110,256]{3,2,1,0:T(8,128)}, u32[]{:S(2)}, u32[]{:S(2)}) collective-permute-start(f32[1,2,110,256]{3,2,1,0:T(8,128)} %get-tuple-element.367), channel_id=1, source_target_pairs={{1,0},{2,1},{3,2},{4,3},{5,4},{6,5},{7,6},{8,7},{9,8},{10,9},{11,1... | collective-permute-start | bytes 675848 | tf_op jit(solution)/shard_map/while/body/eval_jaxpr/ppermute | solution.py:68
  179.8 2.7 maximum_maximum_fusion.4
  212.6 2.4 multiply_reduce_fusion.9
  228.6 5.7 collective-permute-start
  245.8 2.3 reshape.881
  250.9 2.7 maximum_maximum_fusion.4
  283.7 2.4 multiply_reduce_fusion.9
  299.7 5.7 collective-permute-start
  322.0 2.7 maximum_maximum_fusion.4
  354.8 2.4 multiply_reduce_fusion.9
  370.8 5.7 collective-permute-start
  388.0 2.3 reshape.881
  393.1 2.7 maximum_maximum_fusion.4
  426.0 2.4 multiply_reduce_fusion.9
  441.9 5.7 collective-permute-start
  459.1 2.3 reshape.881
  464.2 2.7 maximum_maximum_fusion.4
  497.1 2.4 multiply_reduce_fusion.9
  513.0 5.7 collective-permute-start
  535.3 2.7 maximum_maximum_fusion.4
  568.2 2.4 multiply_reduce_fusion.9
  584.1 5.7 collective-permute-start
  606.4 2.7 maximum_maximum_fusion.4
  639.3 2.4 multiply_reduce_fusion.9
  655.2 26.3 %all_to_all.12 = f32[8,1,2,110,256]{4,2,3,1,0:T(2,128)S(1)} all-to-all(f32[8,1,2,110,256]{4,2,3,1,0:T(2,128)} %get-tuple-element.90), channel_id=1, replica_groups=mesh['span'=8,'tm'=32] {'span'}, dimensions={0} | all-to-all | bytes 3604480 | tf_op jit(solution)/shard_map/all_to_all | solution.py:118
  (894 shorter events, 475.0 us)
Async XLA Ops:
  6.5 80.5 %all-gather.2.cloned.1.call-start = ((), (), s32[]{:S(2)}) async-start(), calls=%async_computation.1 | async-start | bytes 4055040 | tf_op jit(solution)/shard_map/all_gather | solution.py:102
  87.1 22.0 %collective-permute-start = (f32[1,2,110,256]{3,2,1,0:T(8,128)}, f32[1,2,110,256]{3,2,1,0:T(8,128)}, u32[]{:S(2)}, u32[]{:S(2)}) collective-permute-start(f32[1,2,110,256]{3,2,1,0:T(8,128)} %get-tuple-element.367), channel_id=1, source_target_pairs={{1,0},{2,1},{3,2},{4,3},{5,4},{6,5},{7,6},{8,7},{9,8},{10,9},{11,1... | collective-permute-start | bytes 675848 | tf_op jit(solution)/shard_map/while/body/eval_jaxpr/ppermute | solution.py:68
  89.0 20.1 %collective-permute-start.1 = (f32[1,2,110,256]{3,2,1,0:T(8,128)}, f32[1,2,110,256]{3,2,1,0:T(8,128)}, u32[]{:S(2)}, u32[]{:S(2)}) collective-permute-start(f32[1,2,110,256]{3,2,1,0:T(8,128)} %get-tuple-element.367), channel_id=1, source_target_pairs={{0,1},{1,2},{2,3},{3,4},{4,5},{5,6},{6,7},{7,8},{8,9},{9,10},{10,1... | collective-permute-start | bytes 675848 | tf_op jit(solution)/shard_map/while/body/eval_jaxpr/ppermute | solution.py:67
  99.1 7.0 %copy-start.1 = (f32[2,2,256,128]{3,2,1,0:T(8,128)S(1)}, f32[2,2,256,128]{3,2,1,0:T(8,128)}, u32[]{:S(2)}) copy-start(f32[2,2,256,128]{3,2,1,0:T(8,128)} %bitcast_negate_fusion.2) | copy-start | bytes 1572868 | tf_op jit(solution)/shard_map/while
  105.4 3.3 copy-start.4
  154.8 27.9 %collective-permute-start = (f32[1,2,110,256]{3,2,1,0:T(8,128)}, f32[1,2,110,256]{3,2,1,0:T(8,128)}, u32[]{:S(2)}, u32[]{:S(2)}) collective-permute-start(f32[1,2,110,256]{3,2,1,0:T(8,128)} %get-tuple-element.367), channel_id=1, source_target_pairs={{1,0},{2,1},{3,2},{4,3},{5,4},{6,5},{7,6},{8,7},{9,8},{10,9},{11,1... | collective-permute-start | bytes 675848 | tf_op jit(solution)/shard_map/while/body/eval_jaxpr/ppermute | solution.py:68
  163.2 19.6 %collective-permute-start.1 = (f32[1,2,110,256]{3,2,1,0:T(8,128)}, f32[1,2,110,256]{3,2,1,0:T(8,128)}, u32[]{:S(2)}, u32[]{:S(2)}) collective-permute-start(f32[1,2,110,256]{3,2,1,0:T(8,128)} %get-tuple-element.367), channel_id=1, source_target_pairs={{0,1},{1,2},{2,3},{3,4},{4,5},{5,6},{6,7},{7,8},{8,9},{9,10},{10,1... | collective-permute-start | bytes 675848 | tf_op jit(solution)/shard_map/while/body/eval_jaxpr/ppermute | solution.py:67
  172.8 7.0 %copy-start.1 = (f32[2,2,256,128]{3,2,1,0:T(8,128)S(1)}, f32[2,2,256,128]{3,2,1,0:T(8,128)}, u32[]{:S(2)}) copy-start(f32[2,2,256,128]{3,2,1,0:T(8,128)} %bitcast_negate_fusion.2) | copy-start | bytes 1572868 | tf_op jit(solution)/shard_map/while
  179.1 3.3 copy-start.4
  228.6 25.3 %collective-permute-start = (f32[1,2,110,256]{3,2,1,0:T(8,128)}, f32[1,2,110,256]{3,2,1,0:T(8,128)}, u32[]{:S(2)}, u32[]{:S(2)}) collective-permute-start(f32[1,2,110,256]{3,2,1,0:T(8,128)} %get-tuple-element.367), channel_id=1, source_target_pairs={{1,0},{2,1},{3,2},{4,3},{5,4},{6,5},{7,6},{8,7},{9,8},{10,9},{11,1... | collective-permute-start | bytes 675848 | tf_op jit(solution)/shard_map/while/body/eval_jaxpr/ppermute | solution.py:68
  234.3 19.6 %collective-permute-start.1 = (f32[1,2,110,256]{3,2,1,0:T(8,128)}, f32[1,2,110,256]{3,2,1,0:T(8,128)}, u32[]{:S(2)}, u32[]{:S(2)}) collective-permute-start(f32[1,2,110,256]{3,2,1,0:T(8,128)} %get-tuple-element.367), channel_id=1, source_target_pairs={{0,1},{1,2},{2,3},{3,4},{4,5},{5,6},{6,7},{7,8},{8,9},{9,10},{10,1... | collective-permute-start | bytes 675848 | tf_op jit(solution)/shard_map/while/body/eval_jaxpr/ppermute | solution.py:67
  243.9 7.0 %copy-start.1 = (f32[2,2,256,128]{3,2,1,0:T(8,128)S(1)}, f32[2,2,256,128]{3,2,1,0:T(8,128)}, u32[]{:S(2)}) copy-start(f32[2,2,256,128]{3,2,1,0:T(8,128)} %bitcast_negate_fusion.2) | copy-start | bytes 1572868 | tf_op jit(solution)/shard_map/while
  250.2 3.3 copy-start.4
  299.7 25.3 %collective-permute-start = (f32[1,2,110,256]{3,2,1,0:T(8,128)}, f32[1,2,110,256]{3,2,1,0:T(8,128)}, u32[]{:S(2)}, u32[]{:S(2)}) collective-permute-start(f32[1,2,110,256]{3,2,1,0:T(8,128)} %get-tuple-element.367), channel_id=1, source_target_pairs={{1,0},{2,1},{3,2},{4,3},{5,4},{6,5},{7,6},{8,7},{9,8},{10,9},{11,1... | collective-permute-start | bytes 675848 | tf_op jit(solution)/shard_map/while/body/eval_jaxpr/ppermute | solution.py:68
  305.4 19.6 %collective-permute-start.1 = (f32[1,2,110,256]{3,2,1,0:T(8,128)}, f32[1,2,110,256]{3,2,1,0:T(8,128)}, u32[]{:S(2)}, u32[]{:S(2)}) collective-permute-start(f32[1,2,110,256]{3,2,1,0:T(8,128)} %get-tuple-element.367), channel_id=1, source_target_pairs={{0,1},{1,2},{2,3},{3,4},{4,5},{5,6},{6,7},{7,8},{8,9},{9,10},{10,1... | collective-permute-start | bytes 675848 | tf_op jit(solution)/shard_map/while/body/eval_jaxpr/ppermute | solution.py:67
  315.0 7.0 %copy-start.1 = (f32[2,2,256,128]{3,2,1,0:T(8,128)S(1)}, f32[2,2,256,128]{3,2,1,0:T(8,128)}, u32[]{:S(2)}) copy-start(f32[2,2,256,128]{3,2,1,0:T(8,128)} %bitcast_negate_fusion.2) | copy-start | bytes 1572868 | tf_op jit(solution)/shard_map/while
  321.3 3.3 copy-start.4
  370.8 25.3 %collective-permute-start = (f32[1,2,110,256]{3,2,1,0:T(8,128)}, f32[1,2,110,256]{3,2,1,0:T(8,128)}, u32[]{:S(2)}, u32[]{:S(2)}) collective-permute-start(f32[1,2,110,256]{3,2,1,0:T(8,128)} %get-tuple-element.367), channel_id=1, source_target_pairs={{1,0},{2,1},{3,2},{4,3},{5,4},{6,5},{7,6},{8,7},{9,8},{10,9},{11,1... | collective-permute-start | bytes 675848 | tf_op jit(solution)/shard_map/while/body/eval_jaxpr/ppermute | solution.py:68
  376.5 19.6 %collective-permute-start.1 = (f32[1,2,110,256]{3,2,1,0:T(8,128)}, f32[1,2,110,256]{3,2,1,0:T(8,128)}, u32[]{:S(2)}, u32[]{:S(2)}) collective-permute-start(f32[1,2,110,256]{3,2,1,0:T(8,128)} %get-tuple-element.367), channel_id=1, source_target_pairs={{0,1},{1,2},{2,3},{3,4},{4,5},{5,6},{6,7},{7,8},{8,9},{9,10},{10,1... | collective-permute-start | bytes 675848 | tf_op jit(solution)/shard_map/while/body/eval_jaxpr/ppermute | solution.py:67
  386.1 7.0 %copy-start.1 = (f32[2,2,256,128]{3,2,1,0:T(8,128)S(1)}, f32[2,2,256,128]{3,2,1,0:T(8,128)}, u32[]{:S(2)}) copy-start(f32[2,2,256,128]{3,2,1,0:T(8,128)} %bitcast_negate_fusion.2) | copy-start | bytes 1572868 | tf_op jit(solution)/shard_map/while
  441.9 25.3 %collective-permute-start = (f32[1,2,110,256]{3,2,1,0:T(8,128)}, f32[1,2,110,256]{3,2,1,0:T(8,128)}, u32[]{:S(2)}, u32[]{:S(2)}) collective-permute-start(f32[1,2,110,256]{3,2,1,0:T(8,128)} %get-tuple-element.367), channel_id=1, source_target_pairs={{1,0},{2,1},{3,2},{4,3},{5,4},{6,5},{7,6},{8,7},{9,8},{10,9},{11,1... | collective-permute-start | bytes 675848 | tf_op jit(solution)/shard_map/while/body/eval_jaxpr/ppermute | solution.py:68
  447.6 19.6 %collective-permute-start.1 = (f32[1,2,110,256]{3,2,1,0:T(8,128)}, f32[1,2,110,256]{3,2,1,0:T(8,128)}, u32[]{:S(2)}, u32[]{:S(2)}) collective-permute-start(f32[1,2,110,256]{3,2,1,0:T(8,128)} %get-tuple-element.367), channel_id=1, source_target_pairs={{0,1},{1,2},{2,3},{3,4},{4,5},{5,6},{6,7},{7,8},{8,9},{9,10},{10,1... | collective-permute-start | bytes 675848 | tf_op jit(solution)/shard_map/while/body/eval_jaxpr/ppermute | solution.py:67
  457.2 7.0 %copy-start.1 = (f32[2,2,256,128]{3,2,1,0:T(8,128)S(1)}, f32[2,2,256,128]{3,2,1,0:T(8,128)}, u32[]{:S(2)}) copy-start(f32[2,2,256,128]{3,2,1,0:T(8,128)} %bitcast_negate_fusion.2) | copy-start | bytes 1572868 | tf_op jit(solution)/shard_map/while
  463.5 3.3 copy-start.4
  513.0 25.3 %collective-permute-start = (f32[1,2,110,256]{3,2,1,0:T(8,128)}, f32[1,2,110,256]{3,2,1,0:T(8,128)}, u32[]{:S(2)}, u32[]{:S(2)}) collective-permute-start(f32[1,2,110,256]{3,2,1,0:T(8,128)} %get-tuple-element.367), channel_id=1, source_target_pairs={{1,0},{2,1},{3,2},{4,3},{5,4},{6,5},{7,6},{8,7},{9,8},{10,9},{11,1... | collective-permute-start | bytes 675848 | tf_op jit(solution)/shard_map/while/body/eval_jaxpr/ppermute | solution.py:68
  518.8 19.6 %collective-permute-start.1 = (f32[1,2,110,256]{3,2,1,0:T(8,128)}, f32[1,2,110,256]{3,2,1,0:T(8,128)}, u32[]{:S(2)}, u32[]{:S(2)}) collective-permute-start(f32[1,2,110,256]{3,2,1,0:T(8,128)} %get-tuple-element.367), channel_id=1, source_target_pairs={{0,1},{1,2},{2,3},{3,4},{4,5},{5,6},{6,7},{7,8},{8,9},{9,10},{10,1... | collective-permute-start | bytes 675848 | tf_op jit(solution)/shard_map/while/body/eval_jaxpr/ppermute | solution.py:67
  528.3 7.0 %copy-start.1 = (f32[2,2,256,128]{3,2,1,0:T(8,128)S(1)}, f32[2,2,256,128]{3,2,1,0:T(8,128)}, u32[]{:S(2)}) copy-start(f32[2,2,256,128]{3,2,1,0:T(8,128)} %bitcast_negate_fusion.2) | copy-start | bytes 1572868 | tf_op jit(solution)/shard_map/while
  534.6 3.3 copy-start.4
  584.1 25.3 %collective-permute-start = (f32[1,2,110,256]{3,2,1,0:T(8,128)}, f32[1,2,110,256]{3,2,1,0:T(8,128)}, u32[]{:S(2)}, u32[]{:S(2)}) collective-permute-start(f32[1,2,110,256]{3,2,1,0:T(8,128)} %get-tuple-element.367), channel_id=1, source_target_pairs={{1,0},{2,1},{3,2},{4,3},{5,4},{6,5},{7,6},{8,7},{9,8},{10,9},{11,1... | collective-permute-start | bytes 675848 | tf_op jit(solution)/shard_map/while/body/eval_jaxpr/ppermute | solution.py:68
  589.9 19.6 %collective-permute-start.1 = (f32[1,2,110,256]{3,2,1,0:T(8,128)}, f32[1,2,110,256]{3,2,1,0:T(8,128)}, u32[]{:S(2)}, u32[]{:S(2)}) collective-permute-start(f32[1,2,110,256]{3,2,1,0:T(8,128)} %get-tuple-element.367), channel_id=1, source_target_pairs={{0,1},{1,2},{2,3},{3,4},{4,5},{5,6},{6,7},{7,8},{8,9},{9,10},{10,1... | collective-permute-start | bytes 675848 | tf_op jit(solution)/shard_map/while/body/eval_jaxpr/ppermute | solution.py:67
  599.4 7.0 %copy-start.1 = (f32[2,2,256,128]{3,2,1,0:T(8,128)S(1)}, f32[2,2,256,128]{3,2,1,0:T(8,128)}, u32[]{:S(2)}) copy-start(f32[2,2,256,128]{3,2,1,0:T(8,128)} %bitcast_negate_fusion.2) | copy-start | bytes 1572868 | tf_op jit(solution)/shard_map/while
  605.7 3.3 copy-start.4
  (18 other events, 58.2 us)
Sparse Core Ops, SparseCore 0:
  9.9 74.1 all-gather.1

commit v2 on v1

v2 whole, which is shorter than its diff:
```python
import functools

import jax
import jax.numpy as jnp
from jax import lax
from jax.sharding import PartitionSpec as P
from jax.experimental import pallas as pl
from jax.experimental.pallas import tpu as pltpu

ROWS = 128
HIGHEST = lax.Precision.HIGHEST


def band(values, width):
    padded = jnp.concatenate([values, jnp.zeros((width,), jnp.float32)])
    tiled = jnp.tile(padded, width)[: width * 2 * width]
    return tiled.reshape(width, 2 * width).T


def prepare(coupling_group, impulse_group):
    half_taps = (impulse_group.shape[-1] - 1) // 2
    width = 2 * half_taps

    def toeplitz(pair):
        real_band = band(pair[0], width)
        imag_band = band(pair[1], width)
        upper = jnp.concatenate([real_band, imag_band], axis=1)
        lower = jnp.concatenate([-imag_band, real_band], axis=1)
        return jnp.concatenate([upper, lower], axis=0)

    filters = jax.vmap(jax.vmap(toeplitz))(impulse_group)
    spans, steps = filters.shape[:2]
    filters = filters.reshape((spans * steps,) + filters.shape[2:])
    channels = coupling_group.shape[-1]
    grow = ((0, 0), (0, 0), (0, ROWS - channels), (0, ROWS - channels))
    real_part = jnp.pad(coupling_group[:, :, 0], grow)
    imag_part = jnp.pad(coupling_group[:, :, 1], grow)
    upper = jnp.concatenate([real_part, -imag_part], axis=-1)
    lower = jnp.concatenate([imag_part, real_part], axis=-1)
    mixers = jnp.concatenate([upper, lower], axis=-2)
    return (filters, mixers.reshape((spans * steps,) + mixers.shape[2:]))


def group_kernel(origin_ref, nonlinear_ref, left_ref, mid_ref, right_ref, filter_ref, mixer_ref,
                 amplifier_ref, out_ref, *, spans, steps, half_taps, length):
    width = 2 * half_taps
    halo = spans * steps * half_taps
    extent = mid_ref.shape[-1]
    origin = origin_ref[0]
    parts = []
    for part in range(2):
        parts.append(jnp.concatenate(
            [left_ref[part, :, extent - halo:], mid_ref[part], right_ref[part, :, :halo]], axis=1))
    real, imag = parts
    offset = -halo
    for span_index in range(spans):
        for step_index in range(steps):
            index = span_index * steps + step_index
            blocks = real.shape[1] // width - 1
            windows = jnp.concatenate(
                [jnp.concatenate([real[:, b * width:(b + 2) * width], imag[:, b * width:(b + 2) * width]], axis=1)
                 for b in range(blocks)], axis=0)
            product = jnp.dot(windows, filter_ref[index], precision=HIGHEST,
                              preferred_element_type=jnp.float32)
            real = jnp.concatenate([product[b * ROWS:(b + 1) * ROWS, :width] for b in range(blocks)], axis=1)
            imag = jnp.concatenate([product[b * ROWS:(b + 1) * ROWS, width:] for b in range(blocks)], axis=1)
            offset = offset + half_taps
            dispersed = jnp.concatenate([real, imag], axis=0)
            mixed = jnp.dot(mixer_ref[index], dispersed, precision=HIGHEST,
                            preferred_element_type=jnp.float32)
            where = origin + offset + lax.broadcasted_iota(jnp.int32, (1, mixed.shape[1]), 1)
            inside = (where >= 0) & (where < length)
            mixed = jnp.where(inside, mixed, 0.0)
            power = jnp.sum(mixed * mixed, axis=0, keepdims=True)
            phase = nonlinear_ref[index] * power
            cosine = jnp.cos(phase)
            sine = jnp.sin(phase)
            real_mixed = mixed[:ROWS]
            imag_mixed = mixed[ROWS:]
            real = real_mixed * cosine - imag_mixed * sine
            imag = real_mixed * sine + imag_mixed * cosine
        gain = amplifier_ref[span_index]
        real = real * gain
        imag = imag * gain
    out_ref[0] = real
    out_ref[1] = imag


def group_pass(signal, filters, mixers, amplifier_group, nonlinear_group, origin, length):
    spans, steps = nonlinear_group.shape
    half_taps = filters.shape[-1] // 4
    halo = spans * steps * half_taps
    count = lax.axis_size("tm")
    forward = [(i, i + 1) for i in range(count - 1)]
    backward = [(i + 1, i) for i in range(count - 1)]
    left = lax.ppermute(signal, "tm", forward)
    right = lax.ppermute(signal, "tm", backward)
    gain = jnp.pad(amplifier_group, ((0, 0), (0, ROWS - amplifier_group.shape[-1])))[:, :, None]
    vmem = pl.BlockSpec(memory_space=pltpu.VMEM)
    smem = pl.BlockSpec(memory_space=pltpu.SMEM)
    blocks = (signal.shape[-1] + 2 * halo) // (2 * half_taps)
    flops = 2 * spans * steps * ROWS * (blocks * 4 * half_taps * 4 * half_taps + 4 * ROWS * signal.shape[-1] * 2)
    kernel = pl.pallas_call(
        functools.partial(group_kernel, spans=spans, steps=steps, half_taps=half_taps, length=length),
        out_shape=jax.ShapeDtypeStruct(signal.shape, jnp.float32),
        in_specs=[smem, smem, vmem, vmem, vmem, vmem, vmem, vmem],
        out_specs=vmem,
        cost_estimate=pl.CostEstimate(flops=6 * flops, transcendentals=0,
                                      bytes_accessed=4 * (4 * signal.size + filters.size + mixers.size)),
    )
    return kernel(origin.reshape(1), nonlinear_group.reshape(-1), left, signal, right, filters, mixers, gain)


def shards(launched, coupling, impulse, amplifier, nonlinear):
    sections = lax.axis_size("span")
    section_index = lax.axis_index("span")
    frames_count, _, _, extent = launched.shape
    per_section = frames_count // sections
    length = extent * lax.axis_size("tm")
    origin = lax.axis_index("tm") * extent

    coupling_all = lax.all_gather(coupling, "span", axis=0, tiled=True)
    impulse_all = lax.all_gather(impulse, "span", axis=0, tiled=True)
    amplifier_all = lax.all_gather(amplifier, "span", axis=0, tiled=True)
    nonlinear_all = lax.all_gather(nonlinear, "span", axis=0, tiled=True)

    channels = launched.shape[2]
    signal = lax.dynamic_slice_in_dim(launched, section_index * per_section, per_section, 0)
    signal = jnp.pad(signal, ((0, 0), (0, 0), (0, ROWS - channels), (0, 0)))

    def advance(signal, params):
        coupling_group, impulse_group, amplifier_group, nonlinear_group = params
        filters, mixers = prepare(coupling_group, impulse_group)
        signal = jnp.stack([
            group_pass(signal[frame], filters, mixers, amplifier_group, nonlinear_group, origin, length)
            for frame in range(signal.shape[0])])
        return signal, signal

    _, stacked = lax.scan(advance, signal, (coupling_all, impulse_all, amplifier_all, nonlinear_all))
    stacked = stacked[:, :, :, :channels]
    return lax.all_to_all(stacked, "span", 0, 1, tiled=True)


def solution(mesh):
    placed = (
        P(None, None, None, "tm"),
        P("span", None, None, None, None, None),
        P("span", None, None, None, None),
        P("span", None, None),
        P("span", None, None),
    )
    return jax.shard_map(
        shards,
        mesh=mesh,
        in_specs=placed,
        out_specs=P("span", None, None, None, "tm"),
        check_vma=False,
    )
```

time: 698 us -> 436 us (0.62)
  local copies, waits for them, and re-layouts: 275 us -> 129 us
  other arithmetic: 132 us -> 29.1 us
  matrix products: 98.7 us -> 0 us
  Pallas kernels: 0 us -> 96.2 us
    dot_general x64 -> x0, matrix products: 98.7 us -> none  [the longest x32 59.1 us: disperse(): jnp.einsum('fcbu,uv->fcbv', stacked, matrix, precision=lax.Precision.HIGH...]
    pallas_call x0 -> x8, Pallas kernels: none -> 96.2 us  [group_pass(): kernel(origin.reshape(1), nonlinear_group.reshape(-1), left, signal, righ...]
    mul x56 -> x0, other arithmetic: 33.8 us -> none  [the longest x32 26.3 us: group_pass(): signal = signal * inside]
    slice x120 -> x1, local copies, waits for them, and re-layouts: 34.9 us -> 2.11 us  [shards(): stacked = stacked[:, :, :, :channels]]
    mul x56 -> x0, local copies, waits for them, and re-layouts: 26.2 us -> none  [the longest x48 26.1 us: group_pass(): signal = signal * inside]
    while x80 -> x24, local copies, waits for them, and re-layouts: 28.2 us -> 5.57 us
    another operation x64 -> x0, local copies, waits for them, and re-layouts: 22 us -> none  [couple(): jnp.stack([real_part * cosine - imag_part * sine, real_part * sine + imag...]
    cos x32 -> x0, other arithmetic: 21.1 us -> none  [couple(): cosine = jnp.cos(phase)]
  transfers between devices with their start and end apart: 17 -> 17, of which waited for: 0 -> 0; matrix products, arithmetic and copies ran while one was open for 20% -> 32% of each run, Pallas kernels for 0% -> 0%
where the time goes in v2:
time: 436 us; the launch traced here: 434 us
  local copies, waits for them, and re-layouts  129 us (30%)
  blocking collectives  103 us (24%)
  Pallas kernels  96.2 us (22%)
  starting transfers between devices  61.3 us (14%)
  other arithmetic  29.1 us (7%)
  between operations  13.4 us (3%)
    pallas_call x8, Pallas kernels, group_pass(): kernel(origin.reshape(1), nonlinear_group.reshape(-1), left, signal, righ...  96.2 us
    ppermute x8, starting transfers between devices, group_pass(): right = lax.ppermute(signal, 'tm', backward)  46 us
    all_gather x1, blocking collectives, shards(): impulse_all = lax.all_gather(impulse, 'span', axis=0, tiled=True)  35.2 us
    all_to_all x1, blocking collectives, shards(): return lax.all_to_all(stacked, 'span', 0, 1, tiled=True)  26.7 us
    reshape x16, local copies, waits for them, and re-layouts, band(): return tiled.reshape(width, 2 * width).T  23.9 us
    concatenate x8, local copies, waits for them, and re-layouts, toeplitz(): return jnp.concatenate([upper, lower], axis=0)  23.4 us
    all_gather x1, blocking collectives, shards(): nonlinear_all = lax.all_gather(nonlinear, 'span', axis=0, tiled=True)  23 us
    slice x16, local copies, waits for them, and re-layouts, band(): tiled = jnp.tile(padded, width)[:width * 2 * width]  22.1 us
  transfers between devices with their start and end apart: 17, of which 0 were waited for; matrix products, arithmetic and copies ran while one was open for 32% of the time, Pallas kernels for 0%

profile of v2, /device:TPU:2, one launch (start us, length us, event | category | flops | bytes accessed | tf_op | source)
XLA Modules:
  0.0 434.0 jit_solution(5105731247629355653)
XLA Ops:
  8.1 23.0 %all_gather.12 = f32[8,2,2]{2,1,0:T(2,128)S(1)} all-gather(f32[1,2,2]{2,1,0:T(2,128)} %param.11), channel_id=1, replica_groups=mesh['span'=8,'tm'=32] {'span'}, dimensions={0}, use_global_device_ids=true | all-gather | bytes 144 | tf_op jit(solution)/shard_map/all_gather | solution.py:125
  31.1 18.4 %all_gather.15 = f32[8,2,110]{2,1,0:T(2,128)S(1)} all-gather(f32[1,2,110]{2,1,0:T(2,128)} %param.10), channel_id=1, replica_groups=mesh['span'=8,'tm'=32] {'span'}, dimensions={0}, use_global_device_ids=true | all-gather | bytes 7920 | tf_op jit(solution)/shard_map/all_gather | solution.py:124
  49.5 35.2 %all_gather.13 = f32[8,2,2,2,129]{4,3,2,1,0:T(2,128)S(1)} all-gather(f32[1,2,2,2,129]{4,3,2,1,0:T(2,128)} %param.9), channel_id=1, replica_groups=mesh['span'=8,'tm'=32] {'span'}, dimensions={0}, use_global_device_ids=true | all-gather | bytes 37152 | tf_op jit(solution)/shard_map/all_gather | solution.py:123
  84.7 312.4 %while.14 = (s32[]{:T(128)}, f32[1,2,128,256]{3,2,1,0:T(8,128)S(1)}, f32[8,1,2,128,256]{4,2,3,1,0:T(2,128)}, s32[]{:T(128)}, f32[8,2,2]{2,1,0:T(2,128)S(1)}, /*i...) while((s32[]{:T(128)}, ...), condition=%wide.region_1.2_spmd, body=%wide.region_0.1_spmd.sunk | while | flops 4029087744 | bytes 31085608 | solution.py:139
  87.3 5.8 %collective-permute-start.1 = (f32[2,128,256]{2,1,0:T(8,128)}, f32[2,128,256]{2,1,0:T(8,128)}, u32[]{:S(2)}, u32[]{:S(2)}) collective-permute-start(f32[2,128,256]{2,1,0:T(8,128)} %copy.53.mid_ref), channel_id=1, source_target_pairs={{1,0},{2,1},{3,2},{4,3},{5,4},{6,5},{7,6},{8,7},{9,8},{10,9},{11,1... | collective-permute-start | bytes 786440 | tf_op jit(solution)/shard_map/while/body/eval_jaxpr/ppermute | solution.py:97
  99.0 1.9 slice.56
  104.1 2.9 copy.39
  110.8 12.0 %eval_jaxpr.4 = f32[2,128,256]{2,1,0:T(8,128)S(1)} custom-call(s32[1]{0:T(128)} %bitcast.52.origin_ref, f32[4]{0:T(128)} %reshape.40.nonlinear_ref, f32[2,128,256]{2,1,0:T(8,128)} %collective-permute-done.left_ref, f32[2,128,256]{2,1,0:T(8,128)} %copy.53.mid_ref, f32[2,128,256]{2,1,0:T(8,128)} %collective-permute-done.1.right_ref, f32[4,512,256]{2,1,0:T(8,128)} %bitcast.64, ...), custom_call_target="tpu_custom_call" | custom-call | flops 4026531840 | bytes 4194304 | tf_op jit(solution)/shard_map/while/body/eval_jaxpr/pallas_call | solution.py:111
  126.3 5.8 %collective-permute-start.1 = (f32[2,128,256]{2,1,0:T(8,128)}, f32[2,128,256]{2,1,0:T(8,128)}, u32[]{:S(2)}, u32[]{:S(2)}) collective-permute-start(f32[2,128,256]{2,1,0:T(8,128)} %copy.53.mid_ref), channel_id=1, source_target_pairs={{1,0},{2,1},{3,2},{4,3},{5,4},{6,5},{7,6},{8,7},{9,8},{10,9},{11,1... | collective-permute-start | bytes 786440 | tf_op jit(solution)/shard_map/while/body/eval_jaxpr/ppermute | solution.py:97
  138.0 1.9 slice.56
  143.2 2.9 copy.39
  149.8 12.0 %eval_jaxpr.4 = f32[2,128,256]{2,1,0:T(8,128)S(1)} custom-call(s32[1]{0:T(128)} %bitcast.52.origin_ref, f32[4]{0:T(128)} %reshape.40.nonlinear_ref, f32[2,128,256]{2,1,0:T(8,128)} %collective-permute-done.left_ref, f32[2,128,256]{2,1,0:T(8,128)} %copy.53.mid_ref, f32[2,128,256]{2,1,0:T(8,128)} %collective-permute-done.1.right_ref, f32[4,512,256]{2,1,0:T(8,128)} %bitcast.64, ...), custom_call_target="tpu_custom_call" | custom-call | flops 4026531840 | bytes 4194304 | tf_op jit(solution)/shard_map/while/body/eval_jaxpr/pallas_call | solution.py:111
  165.4 5.8 %collective-permute-start.1 = (f32[2,128,256]{2,1,0:T(8,128)}, f32[2,128,256]{2,1,0:T(8,128)}, u32[]{:S(2)}, u32[]{:S(2)}) collective-permute-start(f32[2,128,256]{2,1,0:T(8,128)} %copy.53.mid_ref), channel_id=1, source_target_pairs={{1,0},{2,1},{3,2},{4,3},{5,4},{6,5},{7,6},{8,7},{9,8},{10,9},{11,1... | collective-permute-start | bytes 786440 | tf_op jit(solution)/shard_map/while/body/eval_jaxpr/ppermute | solution.py:97
  182.2 2.9 copy.39
  188.9 12.0 %eval_jaxpr.4 = f32[2,128,256]{2,1,0:T(8,128)S(1)} custom-call(s32[1]{0:T(128)} %bitcast.52.origin_ref, f32[4]{0:T(128)} %reshape.40.nonlinear_ref, f32[2,128,256]{2,1,0:T(8,128)} %collective-permute-done.left_ref, f32[2,128,256]{2,1,0:T(8,128)} %copy.53.mid_ref, f32[2,128,256]{2,1,0:T(8,128)} %collective-permute-done.1.right_ref, f32[4,512,256]{2,1,0:T(8,128)} %bitcast.64, ...), custom_call_target="tpu_custom_call" | custom-call | flops 4026531840 | bytes 4194304 | tf_op jit(solution)/shard_map/while/body/eval_jaxpr/pallas_call | solution.py:111
  204.4 5.8 %collective-permute-start.1 = (f32[2,128,256]{2,1,0:T(8,128)}, f32[2,128,256]{2,1,0:T(8,128)}, u32[]{:S(2)}, u32[]{:S(2)}) collective-permute-start(f32[2,128,256]{2,1,0:T(8,128)} %copy.53.mid_ref), channel_id=1, source_target_pairs={{1,0},{2,1},{3,2},{4,3},{5,4},{6,5},{7,6},{8,7},{9,8},{10,9},{11,1... | collective-permute-start | bytes 786440 | tf_op jit(solution)/shard_map/while/body/eval_jaxpr/ppermute | solution.py:97
  221.3 2.9 copy.39
  227.9 12.0 %eval_jaxpr.4 = f32[2,128,256]{2,1,0:T(8,128)S(1)} custom-call(s32[1]{0:T(128)} %bitcast.52.origin_ref, f32[4]{0:T(128)} %reshape.40.nonlinear_ref, f32[2,128,256]{2,1,0:T(8,128)} %collective-permute-done.left_ref, f32[2,128,256]{2,1,0:T(8,128)} %copy.53.mid_ref, f32[2,128,256]{2,1,0:T(8,128)} %collective-permute-done.1.right_ref, f32[4,512,256]{2,1,0:T(8,128)} %bitcast.64, ...), custom_call_target="tpu_custom_call" | custom-call | flops 4026531840 | bytes 4194304 | tf_op jit(solution)/shard_map/while/body/eval_jaxpr/pallas_call | solution.py:111
  243.5 5.8 %collective-permute-start.1 = (f32[2,128,256]{2,1,0:T(8,128)}, f32[2,128,256]{2,1,0:T(8,128)}, u32[]{:S(2)}, u32[]{:S(2)}) collective-permute-start(f32[2,128,256]{2,1,0:T(8,128)} %copy.53.mid_ref), channel_id=1, source_target_pairs={{1,0},{2,1},{3,2},{4,3},{5,4},{6,5},{7,6},{8,7},{9,8},{10,9},{11,1... | collective-permute-start | bytes 786440 | tf_op jit(solution)/shard_map/while/body/eval_jaxpr/ppermute | solution.py:97
  260.3 2.9 copy.39
  267.0 12.0 %eval_jaxpr.4 = f32[2,128,256]{2,1,0:T(8,128)S(1)} custom-call(s32[1]{0:T(128)} %bitcast.52.origin_ref, f32[4]{0:T(128)} %reshape.40.nonlinear_ref, f32[2,128,256]{2,1,0:T(8,128)} %collective-permute-done.left_ref, f32[2,128,256]{2,1,0:T(8,128)} %copy.53.mid_ref, f32[2,128,256]{2,1,0:T(8,128)} %collective-permute-done.1.right_ref, f32[4,512,256]{2,1,0:T(8,128)} %bitcast.64, ...), custom_call_target="tpu_custom_call" | custom-call | flops 4026531840 | bytes 4194304 | tf_op jit(solution)/shard_map/while/body/eval_jaxpr/pallas_call | solution.py:111
  282.5 5.8 %collective-permute-start.1 = (f32[2,128,256]{2,1,0:T(8,128)}, f32[2,128,256]{2,1,0:T(8,128)}, u32[]{:S(2)}, u32[]{:S(2)}) collective-permute-start(f32[2,128,256]{2,1,0:T(8,128)} %copy.53.mid_ref), channel_id=1, source_target_pairs={{1,0},{2,1},{3,2},{4,3},{5,4},{6,5},{7,6},{8,7},{9,8},{10,9},{11,1... | collective-permute-start | bytes 786440 | tf_op jit(solution)/shard_map/while/body/eval_jaxpr/ppermute | solution.py:97
  299.4 2.9 copy.39
  306.0 12.0 %eval_jaxpr.4 = f32[2,128,256]{2,1,0:T(8,128)S(1)} custom-call(s32[1]{0:T(128)} %bitcast.52.origin_ref, f32[4]{0:T(128)} %reshape.40.nonlinear_ref, f32[2,128,256]{2,1,0:T(8,128)} %collective-permute-done.left_ref, f32[2,128,256]{2,1,0:T(8,128)} %copy.53.mid_ref, f32[2,128,256]{2,1,0:T(8,128)} %collective-permute-done.1.right_ref, f32[4,512,256]{2,1,0:T(8,128)} %bitcast.64, ...), custom_call_target="tpu_custom_call" | custom-call | flops 4026531840 | bytes 4194304 | tf_op jit(solution)/shard_map/while/body/eval_jaxpr/pallas_call | solution.py:111
  321.6 5.8 %collective-permute-start.1 = (f32[2,128,256]{2,1,0:T(8,128)}, f32[2,128,256]{2,1,0:T(8,128)}, u32[]{:S(2)}, u32[]{:S(2)}) collective-permute-start(f32[2,128,256]{2,1,0:T(8,128)} %copy.53.mid_ref), channel_id=1, source_target_pairs={{1,0},{2,1},{3,2},{4,3},{5,4},{6,5},{7,6},{8,7},{9,8},{10,9},{11,1... | collective-permute-start | bytes 786440 | tf_op jit(solution)/shard_map/while/body/eval_jaxpr/ppermute | solution.py:97
  338.5 2.9 copy.39
  345.1 12.0 %eval_jaxpr.4 = f32[2,128,256]{2,1,0:T(8,128)S(1)} custom-call(s32[1]{0:T(128)} %bitcast.52.origin_ref, f32[4]{0:T(128)} %reshape.40.nonlinear_ref, f32[2,128,256]{2,1,0:T(8,128)} %collective-permute-done.left_ref, f32[2,128,256]{2,1,0:T(8,128)} %copy.53.mid_ref, f32[2,128,256]{2,1,0:T(8,128)} %collective-permute-done.1.right_ref, f32[4,512,256]{2,1,0:T(8,128)} %bitcast.64, ...), custom_call_target="tpu_custom_call" | custom-call | flops 4026531840 | bytes 4194304 | tf_op jit(solution)/shard_map/while/body/eval_jaxpr/pallas_call | solution.py:111
  360.7 5.8 %collective-permute-start.1 = (f32[2,128,256]{2,1,0:T(8,128)}, f32[2,128,256]{2,1,0:T(8,128)}, u32[]{:S(2)}, u32[]{:S(2)}) collective-permute-start(f32[2,128,256]{2,1,0:T(8,128)} %copy.53.mid_ref), channel_id=1, source_target_pairs={{1,0},{2,1},{3,2},{4,3},{5,4},{6,5},{7,6},{8,7},{9,8},{10,9},{11,1... | collective-permute-start | bytes 786440 | tf_op jit(solution)/shard_map/while/body/eval_jaxpr/ppermute | solution.py:97
  377.5 2.9 copy.39
  384.2 12.0 %eval_jaxpr.4 = f32[2,128,256]{2,1,0:T(8,128)S(1)} custom-call(s32[1]{0:T(128)} %bitcast.52.origin_ref, f32[4]{0:T(128)} %reshape.40.nonlinear_ref, f32[2,128,256]{2,1,0:T(8,128)} %collective-permute-done.left_ref, f32[2,128,256]{2,1,0:T(8,128)} %copy.53.mid_ref, f32[2,128,256]{2,1,0:T(8,128)} %collective-permute-done.1.right_ref, f32[4,512,256]{2,1,0:T(8,128)} %bitcast.64, ...), custom_call_target="tpu_custom_call" | custom-call | flops 4026531840 | bytes 4194304 | tf_op jit(solution)/shard_map/while/body/eval_jaxpr/pallas_call | solution.py:111
  397.1 2.1 slice.39
  399.2 26.7 %all_to_all.12 = f32[8,1,2,110,256]{4,2,3,1,0:T(2,128)S(1)} all-to-all(f32[8,1,2,110,256]{4,2,3,1,0:T(2,128)S(1)} %slice.39), channel_id=1, replica_groups=mesh['span'=8,'tm'=32] {'span'}, dimensions={0} | all-to-all | bytes 3604480 | tf_op jit(solution)/shard_map/all_to_all | solution.py:141
  (272 shorter events, 144.5 us)
Async XLA Ops:
  6.5 1.5 copy-start
  6.5 78.1 %all-gather.2.cloned.1.call-start = ((), (), s32[]{:S(2)}) async-start(), calls=%async_computation.1 | async-start | bytes 4055040 | tf_op jit(solution)/shard_map/all_gather | solution.py:122
  85.4 25.4 %collective-permute-start = (f32[2,128,256]{2,1,0:T(8,128)}, f32[2,128,256]{2,1,0:T(8,128)}, u32[]{:S(2)}, u32[]{:S(2)}) collective-permute-start(f32[2,128,256]{2,1,0:T(8,128)} %copy.53.mid_ref), channel_id=1, source_target_pairs={{0,1},{1,2},{2,3},{3,4},{4,5},{5,6},{6,7},{7,8},{8,9},{9,10},{10,1... | collective-permute-start | bytes 786440 | tf_op jit(solution)/shard_map/while/body/eval_jaxpr/ppermute | solution.py:96
  87.3 23.5 %collective-permute-start.1 = (f32[2,128,256]{2,1,0:T(8,128)}, f32[2,128,256]{2,1,0:T(8,128)}, u32[]{:S(2)}, u32[]{:S(2)}) collective-permute-start(f32[2,128,256]{2,1,0:T(8,128)} %copy.53.mid_ref), channel_id=1, source_target_pairs={{1,0},{2,1},{3,2},{4,3},{5,4},{6,5},{7,6},{8,7},{9,8},{10,9},{11,1... | collective-permute-start | bytes 786440 | tf_op jit(solution)/shard_map/while/body/eval_jaxpr/ppermute | solution.py:97
  99.0 3.4 copy-start.1
  124.4 25.4 %collective-permute-start = (f32[2,128,256]{2,1,0:T(8,128)}, f32[2,128,256]{2,1,0:T(8,128)}, u32[]{:S(2)}, u32[]{:S(2)}) collective-permute-start(f32[2,128,256]{2,1,0:T(8,128)} %copy.53.mid_ref), channel_id=1, source_target_pairs={{0,1},{1,2},{2,3},{3,4},{4,5},{5,6},{6,7},{7,8},{8,9},{9,10},{10,1... | collective-permute-start | bytes 786440 | tf_op jit(solution)/shard_map/while/body/eval_jaxpr/ppermute | solution.py:96
  126.3 23.5 %collective-permute-start.1 = (f32[2,128,256]{2,1,0:T(8,128)}, f32[2,128,256]{2,1,0:T(8,128)}, u32[]{:S(2)}, u32[]{:S(2)}) collective-permute-start(f32[2,128,256]{2,1,0:T(8,128)} %copy.53.mid_ref), channel_id=1, source_target_pairs={{1,0},{2,1},{3,2},{4,3},{5,4},{6,5},{7,6},{8,7},{9,8},{10,9},{11,1... | collective-permute-start | bytes 786440 | tf_op jit(solution)/shard_map/while/body/eval_jaxpr/ppermute | solution.py:97
  138.0 3.4 copy-start.1
  163.5 25.4 %collective-permute-start = (f32[2,128,256]{2,1,0:T(8,128)}, f32[2,128,256]{2,1,0:T(8,128)}, u32[]{:S(2)}, u32[]{:S(2)}) collective-permute-start(f32[2,128,256]{2,1,0:T(8,128)} %copy.53.mid_ref), channel_id=1, source_target_pairs={{0,1},{1,2},{2,3},{3,4},{4,5},{5,6},{6,7},{7,8},{8,9},{9,10},{10,1... | collective-permute-start | bytes 786440 | tf_op jit(solution)/shard_map/while/body/eval_jaxpr/ppermute | solution.py:96
  165.4 23.5 %collective-permute-start.1 = (f32[2,128,256]{2,1,0:T(8,128)}, f32[2,128,256]{2,1,0:T(8,128)}, u32[]{:S(2)}, u32[]{:S(2)}) collective-permute-start(f32[2,128,256]{2,1,0:T(8,128)} %copy.53.mid_ref), channel_id=1, source_target_pairs={{1,0},{2,1},{3,2},{4,3},{5,4},{6,5},{7,6},{8,7},{9,8},{10,9},{11,1... | collective-permute-start | bytes 786440 | tf_op jit(solution)/shard_map/while/body/eval_jaxpr/ppermute | solution.py:97
  177.1 3.4 copy-start.1
  202.5 25.4 %collective-permute-start = (f32[2,128,256]{2,1,0:T(8,128)}, f32[2,128,256]{2,1,0:T(8,128)}, u32[]{:S(2)}, u32[]{:S(2)}) collective-permute-start(f32[2,128,256]{2,1,0:T(8,128)} %copy.53.mid_ref), channel_id=1, source_target_pairs={{0,1},{1,2},{2,3},{3,4},{4,5},{5,6},{6,7},{7,8},{8,9},{9,10},{10,1... | collective-permute-start | bytes 786440 | tf_op jit(solution)/shard_map/while/body/eval_jaxpr/ppermute | solution.py:96
  204.4 23.5 %collective-permute-start.1 = (f32[2,128,256]{2,1,0:T(8,128)}, f32[2,128,256]{2,1,0:T(8,128)}, u32[]{:S(2)}, u32[]{:S(2)}) collective-permute-start(f32[2,128,256]{2,1,0:T(8,128)} %copy.53.mid_ref), channel_id=1, source_target_pairs={{1,0},{2,1},{3,2},{4,3},{5,4},{6,5},{7,6},{8,7},{9,8},{10,9},{11,1... | collective-permute-start | bytes 786440 | tf_op jit(solution)/shard_map/while/body/eval_jaxpr/ppermute | solution.py:97
  216.1 3.4 copy-start.1
  241.6 25.4 %collective-permute-start = (f32[2,128,256]{2,1,0:T(8,128)}, f32[2,128,256]{2,1,0:T(8,128)}, u32[]{:S(2)}, u32[]{:S(2)}) collective-permute-start(f32[2,128,256]{2,1,0:T(8,128)} %copy.53.mid_ref), channel_id=1, source_target_pairs={{0,1},{1,2},{2,3},{3,4},{4,5},{5,6},{6,7},{7,8},{8,9},{9,10},{10,1... | collective-permute-start | bytes 786440 | tf_op jit(solution)/shard_map/while/body/eval_jaxpr/ppermute | solution.py:96
  243.5 23.5 %collective-permute-start.1 = (f32[2,128,256]{2,1,0:T(8,128)}, f32[2,128,256]{2,1,0:T(8,128)}, u32[]{:S(2)}, u32[]{:S(2)}) collective-permute-start(f32[2,128,256]{2,1,0:T(8,128)} %copy.53.mid_ref), channel_id=1, source_target_pairs={{1,0},{2,1},{3,2},{4,3},{5,4},{6,5},{7,6},{8,7},{9,8},{10,9},{11,1... | collective-permute-start | bytes 786440 | tf_op jit(solution)/shard_map/while/body/eval_jaxpr/ppermute | solution.py:97
  255.2 3.4 copy-start.1
  280.6 25.4 %collective-permute-start = (f32[2,128,256]{2,1,0:T(8,128)}, f32[2,128,256]{2,1,0:T(8,128)}, u32[]{:S(2)}, u32[]{:S(2)}) collective-permute-start(f32[2,128,256]{2,1,0:T(8,128)} %copy.53.mid_ref), channel_id=1, source_target_pairs={{0,1},{1,2},{2,3},{3,4},{4,5},{5,6},{6,7},{7,8},{8,9},{9,10},{10,1... | collective-permute-start | bytes 786440 | tf_op jit(solution)/shard_map/while/body/eval_jaxpr/ppermute | solution.py:96
  282.5 23.5 %collective-permute-start.1 = (f32[2,128,256]{2,1,0:T(8,128)}, f32[2,128,256]{2,1,0:T(8,128)}, u32[]{:S(2)}, u32[]{:S(2)}) collective-permute-start(f32[2,128,256]{2,1,0:T(8,128)} %copy.53.mid_ref), channel_id=1, source_target_pairs={{1,0},{2,1},{3,2},{4,3},{5,4},{6,5},{7,6},{8,7},{9,8},{10,9},{11,1... | collective-permute-start | bytes 786440 | tf_op jit(solution)/shard_map/while/body/eval_jaxpr/ppermute | solution.py:97
  294.2 3.4 copy-start.1
  319.7 25.4 %collective-permute-start = (f32[2,128,256]{2,1,0:T(8,128)}, f32[2,128,256]{2,1,0:T(8,128)}, u32[]{:S(2)}, u32[]{:S(2)}) collective-permute-start(f32[2,128,256]{2,1,0:T(8,128)} %copy.53.mid_ref), channel_id=1, source_target_pairs={{0,1},{1,2},{2,3},{3,4},{4,5},{5,6},{6,7},{7,8},{8,9},{9,10},{10,1... | collective-permute-start | bytes 786440 | tf_op jit(solution)/shard_map/while/body/eval_jaxpr/ppermute | solution.py:96
  321.6 23.5 %collective-permute-start.1 = (f32[2,128,256]{2,1,0:T(8,128)}, f32[2,128,256]{2,1,0:T(8,128)}, u32[]{:S(2)}, u32[]{:S(2)}) collective-permute-start(f32[2,128,256]{2,1,0:T(8,128)} %copy.53.mid_ref), channel_id=1, source_target_pairs={{1,0},{2,1},{3,2},{4,3},{5,4},{6,5},{7,6},{8,7},{9,8},{10,9},{11,1... | collective-permute-start | bytes 786440 | tf_op jit(solution)/shard_map/while/body/eval_jaxpr/ppermute | solution.py:97
  333.3 3.4 copy-start.1
  358.7 25.4 %collective-permute-start = (f32[2,128,256]{2,1,0:T(8,128)}, f32[2,128,256]{2,1,0:T(8,128)}, u32[]{:S(2)}, u32[]{:S(2)}) collective-permute-start(f32[2,128,256]{2,1,0:T(8,128)} %copy.53.mid_ref), channel_id=1, source_target_pairs={{0,1},{1,2},{2,3},{3,4},{4,5},{5,6},{6,7},{7,8},{8,9},{9,10},{10,1... | collective-permute-start | bytes 786440 | tf_op jit(solution)/shard_map/while/body/eval_jaxpr/ppermute | solution.py:96
  360.7 23.5 %collective-permute-start.1 = (f32[2,128,256]{2,1,0:T(8,128)}, f32[2,128,256]{2,1,0:T(8,128)}, u32[]{:S(2)}, u32[]{:S(2)}) collective-permute-start(f32[2,128,256]{2,1,0:T(8,128)} %copy.53.mid_ref), channel_id=1, source_target_pairs={{1,0},{2,1},{3,2},{4,3},{5,4},{6,5},{7,6},{8,7},{9,8},{10,9},{11,1... | collective-permute-start | bytes 786440 | tf_op jit(solution)/shard_map/while/body/eval_jaxpr/ppermute | solution.py:97
  372.4 3.4 copy-start.1
Sparse Core Ops, SparseCore 0:
  9.9 74.1 all-gather.1

commit v3 on v2

v3 whole, which is shorter than its diff:
```python
import functools

import jax
import jax.numpy as jnp
from jax import lax
from jax.sharding import PartitionSpec as P
from jax.experimental import pallas as pl
from jax.experimental.pallas import tpu as pltpu

ROWS = 128
HIGHEST = lax.Precision.HIGHEST


def banded(row, width):
    grid = jnp.broadcast_to(row, (width, 2 * width))
    return pltpu.roll(grid, 0, 1, stride=1, stride_axis=0).T


def group_kernel(origin_ref, nonlinear_ref, left_ref, mid_ref, right_ref, taps_ref, coupling_ref,
                 amplifier_ref, out_ref, *, spans, steps, half_taps, length):
    width = 2 * half_taps
    halo = spans * steps * half_taps
    extent = mid_ref.shape[-1]
    origin = origin_ref[0]
    parts = []
    for part in range(2):
        parts.append(jnp.concatenate(
            [left_ref[part, :, extent - halo:], mid_ref[part], right_ref[part, :, :halo]], axis=1))
    real, imag = parts
    offset = -halo
    for span_index in range(spans):
        for step_index in range(steps):
            index = span_index * steps + step_index
            blocks = real.shape[1] // width - 1
            windows = jnp.concatenate(
                [jnp.concatenate([real[:, b * width:(b + 2) * width], imag[:, b * width:(b + 2) * width]], axis=1)
                 for b in range(blocks)], axis=0)
            real_band = banded(taps_ref[2 * index], width)
            imag_band = banded(taps_ref[2 * index + 1], width)
            response = jnp.concatenate([
                jnp.concatenate([real_band, imag_band], axis=1),
                jnp.concatenate([-imag_band, real_band], axis=1)], axis=0)
            product = jnp.dot(windows, response, precision=HIGHEST,
                              preferred_element_type=jnp.float32)
            real = jnp.concatenate([product[b * ROWS:(b + 1) * ROWS, :width] for b in range(blocks)], axis=1)
            imag = jnp.concatenate([product[b * ROWS:(b + 1) * ROWS, width:] for b in range(blocks)], axis=1)
            offset = offset + half_taps
            dispersed = jnp.concatenate([real, imag], axis=0)
            real_coupling = coupling_ref[2 * index]
            imag_coupling = coupling_ref[2 * index + 1]
            mixer = jnp.concatenate([
                jnp.concatenate([real_coupling, -imag_coupling], axis=1),
                jnp.concatenate([imag_coupling, real_coupling], axis=1)], axis=0)
            mixed = jnp.dot(mixer, dispersed, precision=HIGHEST,
                            preferred_element_type=jnp.float32)
            where = origin + offset + lax.broadcasted_iota(jnp.int32, (1, mixed.shape[1]), 1)
            inside = (where >= 0) & (where < length)
            mixed = jnp.where(inside, mixed, 0.0)
            power = jnp.sum(mixed * mixed, axis=0, keepdims=True)
            phase = nonlinear_ref[index] * power
            cosine = jnp.cos(phase)
            sine = jnp.sin(phase)
            real_mixed = mixed[:ROWS]
            imag_mixed = mixed[ROWS:]
            real = real_mixed * cosine - imag_mixed * sine
            imag = real_mixed * sine + imag_mixed * cosine
        gain = amplifier_ref[span_index]
        real = real * gain
        imag = imag * gain
    out_ref[0] = real
    out_ref[1] = imag


def group_pass(signal, taps, coupling, gain, nonlinear_group, origin, length, spans, steps, half_taps):
    halo = spans * steps * half_taps
    count = lax.axis_size("tm")
    forward = [(i, i + 1) for i in range(count - 1)]
    backward = [(i + 1, i) for i in range(count - 1)]
    left = lax.ppermute(signal, "tm", forward)
    right = lax.ppermute(signal, "tm", backward)
    vmem = pl.BlockSpec(memory_space=pltpu.VMEM)
    smem = pl.BlockSpec(memory_space=pltpu.SMEM)
    blocks = (signal.shape[-1] + 2 * halo) // (2 * half_taps)
    flops = 2 * spans * steps * ROWS * (blocks * 4 * half_taps * 4 * half_taps + 4 * ROWS * signal.shape[-1] * 2)
    kernel = pl.pallas_call(
        functools.partial(group_kernel, spans=spans, steps=steps, half_taps=half_taps, length=length),
        out_shape=jax.ShapeDtypeStruct(signal.shape, jnp.float32),
        in_specs=[smem, smem, vmem, vmem, vmem, vmem, vmem, vmem],
        out_specs=vmem,
        cost_estimate=pl.CostEstimate(flops=6 * flops, transcendentals=0,
                                      bytes_accessed=4 * (4 * signal.size + taps.size + coupling.size)),
    )
    return kernel(origin.reshape(1), nonlinear_group, left, signal, right, taps, coupling, gain)


def shards(launched, coupling, impulse, amplifier, nonlinear):
    sections = lax.axis_size("span")
    section_index = lax.axis_index("span")
    frames_count, _, _, extent = launched.shape
    per_section = frames_count // sections
    length = extent * lax.axis_size("tm")
    origin = lax.axis_index("tm") * extent

    pieces = (coupling, impulse, amplifier, nonlinear)
    packed = jnp.concatenate([piece.reshape(piece.shape[0], -1) for piece in pieces], axis=1)
    gathered = lax.all_gather(packed, "span", axis=0, tiled=True)
    unpacked = []
    start = 0
    for piece in pieces:
        size = piece[0].size
        unpacked.append(gathered[:, start : start + size].reshape((-1,) + piece.shape[1:]))
        start = start + size
    coupling_all, impulse_all, amplifier_all, nonlinear_all = unpacked
    groups, spans, steps, _, taps_count = impulse_all.shape
    half_taps = (taps_count - 1) // 2
    channels = launched.shape[2]
    grow = ROWS - channels
    coupling_all = jnp.pad(coupling_all, ((0, 0),) * 4 + ((0, grow), (0, grow)))
    coupling_all = coupling_all.reshape(groups, spans * steps * 2, ROWS, ROWS)
    taps_all = jnp.pad(impulse_all, ((0, 0),) * 4 + ((0, 4 * half_taps - taps_count),))
    taps_all = taps_all.reshape(groups, spans * steps * 2, 1, 4 * half_taps)
    gain_all = jnp.pad(amplifier_all, ((0, 0), (0, 0), (0, grow)))[..., None]
    nonlinear_all = nonlinear_all.reshape(groups, spans * steps)

    signal = lax.dynamic_slice_in_dim(launched, section_index * per_section, per_section, 0)
    signal = jnp.pad(signal, ((0, 0), (0, 0), (0, grow), (0, 0)))

    def advance(signal, params):
        taps, coupling_group, gain, nonlinear_group = params
        signal = jnp.stack([
            group_pass(signal[frame], taps, coupling_group, gain, nonlinear_group, origin, length,
                       spans, steps, half_taps)
            for frame in range(signal.shape[0])])
        return signal, signal

    _, stacked = lax.scan(advance, signal, (taps_all, coupling_all, gain_all, nonlinear_all))
    stacked = stacked[:, :, :, :channels]
    return lax.all_to_all(stacked, "span", 0, 1, tiled=True)


def solution(mesh):
    placed = (
        P(None, None, None, "tm"),
        P("span", None, None, None, None, None),
        P("span", None, None, None, None),
        P("span", None, None),
        P("span", None, None),
    )
    return jax.shard_map(
        shards,
        mesh=mesh,
        in_specs=placed,
        out_specs=P("span", None, None, None, "tm"),
        check_vma=False,
    )
```

time: 436 us -> 340 us (0.78)
  waiting for transfers between devices: 0.75 us -> 98.3 us
  blocking collectives: 103 us -> 24.6 us
  local copies, waits for them, and re-layouts: 129 us -> 73.2 us
  other arithmetic: 29.1 us -> 0.01 us
  starting transfers between devices: 61.3 us -> 37 us
  Pallas kernels: 96.2 us -> 91.5 us
    all_gather x3 -> x0, blocking collectives: 76.6 us -> none  [the longest x1 35.2 us: shards(): impulse_all = lax.all_gather(impulse, 'span', axis=0, tiled=True)]
    all_gather x1, waiting for transfers between devices: 0.01 us -> 69.3 us  [shards(): gathered = lax.all_gather(packed, 'span', axis=0, tiled=True)]
    squeeze x24 -> x40, local copies, waits for them, and re-layouts: 0.36 us -> 30.6 us  [shards(): lax.scan(advance, signal, (taps_all, coupling_all, gain_all, nonlinear_all))]
    ppermute x8, waiting for transfers between devices: 0.02 us -> 29 us  [group_pass(): left = lax.ppermute(signal, 'tm', forward)]
    ppermute x8, starting transfers between devices: 46 us -> 18.3 us  [group_pass(): right = lax.ppermute(signal, 'tm', backward)]
    concatenate x24 -> x1, local copies, waits for them, and re-layouts: 23.5 us -> 0.25 us  [shards(): jnp.concatenate([piece.reshape(piece.shape[0], -1) for piece in pieces],...]
    concatenate x16 -> x0, other arithmetic: 22.1 us -> none  [the longest x8 13.7 us: toeplitz(): return jnp.concatenate([upper, lower], axis=0)]
    another operation x32 -> x0, local copies, waits for them, and re-layouts: 21.5 us -> none  [band(): tiled = jnp.tile(padded, width)[:width * 2 * width]]
  transfers between devices with their start and end apart: 17 -> 17, of which waited for: 0 -> 9; matrix products, arithmetic and copies ran while one was open for 32% -> 9% of each run, Pallas kernels for 0% -> 0%
where the time goes in v3:
time: 340 us; the launch traced here: 339 us
  waiting for transfers between devices  98.3 us (29%)
  Pallas kernels  91.5 us (27%)
  local copies, waits for them, and re-layouts  73.2 us (22%)
  starting transfers between devices  37 us (11%)
  blocking collectives  24.6 us (7%)
  between operations  13.5 us (4%)
    pallas_call x8, Pallas kernels, group_pass(): kernel(origin.reshape(1), nonlinear_group, left, signal, right, taps, cou...  91.5 us
    all_gather x1, waiting for transfers between devices, shards(): gathered = lax.all_gather(packed, 'span', axis=0, tiled=True)  69.3 us
    squeeze x40, local copies, waits for them, and re-layouts, shards(): lax.scan(advance, signal, (taps_all, coupling_all, gain_all, nonlinear_all))  30.6 us
    ppermute x8, waiting for transfers between devices, group_pass(): left = lax.ppermute(signal, 'tm', forward)  29 us
    all_to_all x1, blocking collectives, shards(): return lax.all_to_all(stacked, 'span', 0, 1, tiled=True)  24.6 us
    ppermute x8, starting transfers between devices, group_pass(): left = lax.ppermute(signal, 'tm', forward)  18.8 us
    ppermute x8, starting transfers between devices, group_pass(): right = lax.ppermute(signal, 'tm', backward)  18.3 us
    unnamed x11, local copies, waits for them, and re-layouts  9.86 us
  transfers between devices with their start and end apart: 17, of which 9 were waited for; matrix products, arithmetic and copies ran while one was open for 9% of the time, Pallas kernels for 0%

profile of v3, /device:TPU:2, one launch (start us, length us, event | category | flops | bytes accessed | tf_op | source)
XLA Modules:
  0.0 338.6 jit_solution(9532355282094216579)
XLA Ops:
  10.8 4.1 %dynamic-update-slice = f32[1,98056]{1,0:T(1,128)S(1)} dynamic-update-slice(f32[1,98056]{1,0:T(1,128)S(1)} %custom-call, f32[1,96800]{1,0:T(1,128)S(1)} %reshape.34, s32[]{} %constant.45, s32[]{} %constant.45) | dynamic-update-slice | bytes 774404
  16.7 69.3 %all-gather.3.cloned.1.call-done = f32[8,1,98056]{2,1,0:T(1,128)} async-done(((f32[1,1,98056]{2,1,0:T(1,128)}), f32[8,1,98056]{2,1,0:T(1,128)}) %all-gather.3.cloned.1.call-update) | async-done | bytes 3137808 | tf_op jit(solution)/shard_map/all_gather | solution.py:106
  86.0 2.1 copy.26
  90.5 7.0 %reshape.40 = f32[8,2,2,2,110,110]{5,4,3,2,1,0:T(8,128)} reshape(f32[8,96800]{1,0:T(8,128)} %slice.22) | data formatting | bytes 6195200 | tf_op jit(solution)/shard_map/reshape | solution.py:111
  97.5 4.5 %pad.18 = f32[8,2,2,2,128,128]{5,4,3,2,1,0:T(8,128)} pad(f32[8,2,2,2,110,110]{5,4,3,2,1,0:T(8,128)} %reshape.40, f32[]{:T(128)} %constant.30.clone.1), padding=0_0x0_0x0_0x0_0x0_18x0_18 | pad | bytes 7291908 | tf_op jit(solution)/shard_map/jit(_pad)/pad | solution.py:118
  102.0 201.7 %while.12 = (s32[]{:T(128)}, f32[1,2,128,256]{3,2,1,0:T(8,128)S(1)}, f32[8,1,2,128,256]{4,2,3,1,0:T(2,128)}, s32[]{:T(128)}, f32[8,4]{1,0:T(8,128)S(1)}, /*index...) while((s32[]{:T(128)}, ...), condition=%wide.region_1.2_spmd, body=%wide.region_0.1_spmd.sunk | while | flops 4026531840 | bytes 8941885 | solution.py:136
  102.1 4.8 %collective-permute-start.1 = (f32[2,128,256]{2,1,0:T(8,128)S(1)}, f32[2,128,256]{2,1,0:T(8,128)S(1)}, u32[]{:S(2)}, u32[]{:S(2)}) collective-permute-start(f32[2,128,256]{2,1,0:T(8,128)S(1)} %copy.46.mid_ref), channel_id=1, source_target_pairs={{1,0},{2,1},{3,2},{4,3},{5,4},{6,5},{7,6},{8,7},{9,8},{10,9},{11,1... | collective-permute-start | bytes 786440 | tf_op jit(solution)/shard_map/while/body/eval_jaxpr/ppermute | solution.py:80
  112.7 4.0 %collective-permute-done.left_ref = f32[2,128,256]{2,1,0:T(8,128)S(1)} collective-permute-done((f32[2,128,256]{2,1,0:T(8,128)S(1)}, f32[2,128,256]{2,1,0:T(8,128)S(1)}, u32[]{:S(2)}, u32[]{:S(2)}) %collective-permute-start) | collective-permute-done | bytes 262176 | tf_op jit(solution)/shard_map/while/body/eval_jaxpr/ppermute | solution.py:79
  117.4 11.4 %eval_jaxpr.1 = f32[2,128,256]{2,1,0:T(8,128)S(1)} custom-call(s32[1]{0:T(128)} %bitcast.32.origin_ref, f32[4]{0:T(128)} %fusion.4.nonlinear_ref, f32[2,128,256]{2,1,0:T(8,128)} %copy-done.4, f32[2,128,256]{2,1,0:T(8,128)} %copy-done.1, f32[2,128,256]{2,1,0:T(8,128)} %copy-done.3, f32[8,1,256]{2,1,0:T(1,128)} %dynamic-slice_bitcast_fusion.4.taps_ref, ...), custom_call_target="tpu_custom_call" | custom-call | flops 4026531840 | bytes 1581056 | tf_op jit(solution)/shard_map/while/body/eval_jaxpr/pallas_call | solution.py:93
  131.7 2.4 collective-permute-start
  138.0 3.6 %collective-permute-done.left_ref = f32[2,128,256]{2,1,0:T(8,128)S(1)} collective-permute-done((f32[2,128,256]{2,1,0:T(8,128)S(1)}, f32[2,128,256]{2,1,0:T(8,128)S(1)}, u32[]{:S(2)}, u32[]{:S(2)}) %collective-permute-start) | collective-permute-done | bytes 262176 | tf_op jit(solution)/shard_map/while/body/eval_jaxpr/ppermute | solution.py:79
  142.3 11.4 %eval_jaxpr.1 = f32[2,128,256]{2,1,0:T(8,128)S(1)} custom-call(s32[1]{0:T(128)} %bitcast.32.origin_ref, f32[4]{0:T(128)} %fusion.4.nonlinear_ref, f32[2,128,256]{2,1,0:T(8,128)} %copy-done.4, f32[2,128,256]{2,1,0:T(8,128)} %copy-done.1, f32[2,128,256]{2,1,0:T(8,128)} %copy-done.3, f32[8,1,256]{2,1,0:T(1,128)} %dynamic-slice_bitcast_fusion.4.taps_ref, ...), custom_call_target="tpu_custom_call" | custom-call | flops 4026531840 | bytes 1581056 | tf_op jit(solution)/shard_map/while/body/eval_jaxpr/pallas_call | solution.py:93
  156.6 2.4 collective-permute-start
  162.9 3.6 %collective-permute-done.left_ref = f32[2,128,256]{2,1,0:T(8,128)S(1)} collective-permute-done((f32[2,128,256]{2,1,0:T(8,128)S(1)}, f32[2,128,256]{2,1,0:T(8,128)S(1)}, u32[]{:S(2)}, u32[]{:S(2)}) %collective-permute-start) | collective-permute-done | bytes 262176 | tf_op jit(solution)/shard_map/while/body/eval_jaxpr/ppermute | solution.py:79
  167.1 11.4 %eval_jaxpr.1 = f32[2,128,256]{2,1,0:T(8,128)S(1)} custom-call(s32[1]{0:T(128)} %bitcast.32.origin_ref, f32[4]{0:T(128)} %fusion.4.nonlinear_ref, f32[2,128,256]{2,1,0:T(8,128)} %copy-done.4, f32[2,128,256]{2,1,0:T(8,128)} %copy-done.1, f32[2,128,256]{2,1,0:T(8,128)} %copy-done.3, f32[8,1,256]{2,1,0:T(1,128)} %dynamic-slice_bitcast_fusion.4.taps_ref, ...), custom_call_target="tpu_custom_call" | custom-call | flops 4026531840 | bytes 1581056 | tf_op jit(solution)/shard_map/while/body/eval_jaxpr/pallas_call | solution.py:93
  181.5 2.4 collective-permute-start
  187.7 3.6 %collective-permute-done.left_ref = f32[2,128,256]{2,1,0:T(8,128)S(1)} collective-permute-done((f32[2,128,256]{2,1,0:T(8,128)S(1)}, f32[2,128,256]{2,1,0:T(8,128)S(1)}, u32[]{:S(2)}, u32[]{:S(2)}) %collective-permute-start) | collective-permute-done | bytes 262176 | tf_op jit(solution)/shard_map/while/body/eval_jaxpr/ppermute | solution.py:79
  192.0 11.4 %eval_jaxpr.1 = f32[2,128,256]{2,1,0:T(8,128)S(1)} custom-call(s32[1]{0:T(128)} %bitcast.32.origin_ref, f32[4]{0:T(128)} %fusion.4.nonlinear_ref, f32[2,128,256]{2,1,0:T(8,128)} %copy-done.4, f32[2,128,256]{2,1,0:T(8,128)} %copy-done.1, f32[2,128,256]{2,1,0:T(8,128)} %copy-done.3, f32[8,1,256]{2,1,0:T(1,128)} %dynamic-slice_bitcast_fusion.4.taps_ref, ...), custom_call_target="tpu_custom_call" | custom-call | flops 4026531840 | bytes 1581056 | tf_op jit(solution)/shard_map/while/body/eval_jaxpr/pallas_call | solution.py:93
  206.3 2.4 collective-permute-start
  212.6 3.6 %collective-permute-done.left_ref = f32[2,128,256]{2,1,0:T(8,128)S(1)} collective-permute-done((f32[2,128,256]{2,1,0:T(8,128)S(1)}, f32[2,128,256]{2,1,0:T(8,128)S(1)}, u32[]{:S(2)}, u32[]{:S(2)}) %collective-permute-start) | collective-permute-done | bytes 262176 | tf_op jit(solution)/shard_map/while/body/eval_jaxpr/ppermute | solution.py:79
  216.8 11.4 %eval_jaxpr.1 = f32[2,128,256]{2,1,0:T(8,128)S(1)} custom-call(s32[1]{0:T(128)} %bitcast.32.origin_ref, f32[4]{0:T(128)} %fusion.4.nonlinear_ref, f32[2,128,256]{2,1,0:T(8,128)} %copy-done.4, f32[2,128,256]{2,1,0:T(8,128)} %copy-done.1, f32[2,128,256]{2,1,0:T(8,128)} %copy-done.3, f32[8,1,256]{2,1,0:T(1,128)} %dynamic-slice_bitcast_fusion.4.taps_ref, ...), custom_call_target="tpu_custom_call" | custom-call | flops 4026531840 | bytes 1581056 | tf_op jit(solution)/shard_map/while/body/eval_jaxpr/pallas_call | solution.py:93
  231.2 2.4 collective-permute-start
  237.4 3.6 %collective-permute-done.left_ref = f32[2,128,256]{2,1,0:T(8,128)S(1)} collective-permute-done((f32[2,128,256]{2,1,0:T(8,128)S(1)}, f32[2,128,256]{2,1,0:T(8,128)S(1)}, u32[]{:S(2)}, u32[]{:S(2)}) %collective-permute-start) | collective-permute-done | bytes 262176 | tf_op jit(solution)/shard_map/while/body/eval_jaxpr/ppermute | solution.py:79
  241.7 11.4 %eval_jaxpr.1 = f32[2,128,256]{2,1,0:T(8,128)S(1)} custom-call(s32[1]{0:T(128)} %bitcast.32.origin_ref, f32[4]{0:T(128)} %fusion.4.nonlinear_ref, f32[2,128,256]{2,1,0:T(8,128)} %copy-done.4, f32[2,128,256]{2,1,0:T(8,128)} %copy-done.1, f32[2,128,256]{2,1,0:T(8,128)} %copy-done.3, f32[8,1,256]{2,1,0:T(1,128)} %dynamic-slice_bitcast_fusion.4.taps_ref, ...), custom_call_target="tpu_custom_call" | custom-call | flops 4026531840 | bytes 1581056 | tf_op jit(solution)/shard_map/while/body/eval_jaxpr/pallas_call | solution.py:93
  256.0 2.4 collective-permute-start
  262.2 3.6 %collective-permute-done.left_ref = f32[2,128,256]{2,1,0:T(8,128)S(1)} collective-permute-done((f32[2,128,256]{2,1,0:T(8,128)S(1)}, f32[2,128,256]{2,1,0:T(8,128)S(1)}, u32[]{:S(2)}, u32[]{:S(2)}) %collective-permute-start) | collective-permute-done | bytes 262176 | tf_op jit(solution)/shard_map/while/body/eval_jaxpr/ppermute | solution.py:79
  266.5 11.4 %eval_jaxpr.1 = f32[2,128,256]{2,1,0:T(8,128)S(1)} custom-call(s32[1]{0:T(128)} %bitcast.32.origin_ref, f32[4]{0:T(128)} %fusion.4.nonlinear_ref, f32[2,128,256]{2,1,0:T(8,128)} %copy-done.4, f32[2,128,256]{2,1,0:T(8,128)} %copy-done.1, f32[2,128,256]{2,1,0:T(8,128)} %copy-done.3, f32[8,1,256]{2,1,0:T(1,128)} %dynamic-slice_bitcast_fusion.4.taps_ref, ...), custom_call_target="tpu_custom_call" | custom-call | flops 4026531840 | bytes 1581056 | tf_op jit(solution)/shard_map/while/body/eval_jaxpr/pallas_call | solution.py:93
  280.8 2.4 collective-permute-start
  287.1 3.6 %collective-permute-done.left_ref = f32[2,128,256]{2,1,0:T(8,128)S(1)} collective-permute-done((f32[2,128,256]{2,1,0:T(8,128)S(1)}, f32[2,128,256]{2,1,0:T(8,128)S(1)}, u32[]{:S(2)}, u32[]{:S(2)}) %collective-permute-start) | collective-permute-done | bytes 262176 | tf_op jit(solution)/shard_map/while/body/eval_jaxpr/ppermute | solution.py:79
  291.4 11.4 %eval_jaxpr.1 = f32[2,128,256]{2,1,0:T(8,128)S(1)} custom-call(s32[1]{0:T(128)} %bitcast.32.origin_ref, f32[4]{0:T(128)} %fusion.4.nonlinear_ref, f32[2,128,256]{2,1,0:T(8,128)} %copy-done.4, f32[2,128,256]{2,1,0:T(8,128)} %copy-done.1, f32[2,128,256]{2,1,0:T(8,128)} %copy-done.3, f32[8,1,256]{2,1,0:T(1,128)} %dynamic-slice_bitcast_fusion.4.taps_ref, ...), custom_call_target="tpu_custom_call" | custom-call | flops 4026531840 | bytes 1581056 | tf_op jit(solution)/shard_map/while/body/eval_jaxpr/pallas_call | solution.py:93
  303.8 2.1 slice.19
  305.9 24.6 %all_to_all.12 = f32[8,1,2,110,256]{4,2,3,1,0:T(2,128)S(1)} all-to-all(f32[8,1,2,110,256]{4,2,3,1,0:T(2,128)S(1)} %slice.19), channel_id=1, replica_groups=mesh['span'=8,'tm'=32] {'span'}, dimensions={0} | all-to-all | bytes 3604480 | tf_op jit(solution)/shard_map/all_to_all | solution.py:138
  (149 shorter events, 68.8 us)
Async XLA Ops:
  6.5 10.0 %copy-start = (f32[8,2,110,256]{3,1,2,0:T(2,128)S(1)}, f32[8,2,110,256]{3,1,2,0:T(2,128)}, u32[]{:S(2)}) copy-start(f32[8,2,110,256]{3,1,2,0:T(2,128)} %param.7) | copy-start | bytes 5406724
  6.5 79.4 %all-gather.3.cloned.1.call-start = ((), (), s32[]{:S(2)}) async-start(), calls=%async_computation.1 | async-start | bytes 3534336 | tf_op jit(solution)/shard_map/all_gather | solution.py:106
  102.1 14.7 %copy-start.1 = (f32[2,128,256]{2,1,0:T(8,128)}, f32[2,128,256]{2,1,0:T(8,128)S(1)}, u32[]{:S(2)}) copy-start(f32[2,128,256]{2,1,0:T(8,128)S(1)} %copy.46.mid_ref) | copy-start | bytes 786436 | tf_op jit(solution)/shard_map/while
  102.1 10.6 %collective-permute-start.1 = (f32[2,128,256]{2,1,0:T(8,128)S(1)}, f32[2,128,256]{2,1,0:T(8,128)S(1)}, u32[]{:S(2)}, u32[]{:S(2)}) collective-permute-start(f32[2,128,256]{2,1,0:T(8,128)S(1)} %copy.46.mid_ref), channel_id=1, source_target_pairs={{1,0},{2,1},{3,2},{4,3},{5,4},{6,5},{7,6},{8,7},{9,8},{10,9},{11,1... | collective-permute-start | bytes 786440 | tf_op jit(solution)/shard_map/while/body/eval_jaxpr/ppermute | solution.py:80
  106.9 9.8 %collective-permute-start = (f32[2,128,256]{2,1,0:T(8,128)S(1)}, f32[2,128,256]{2,1,0:T(8,128)S(1)}, u32[]{:S(2)}, u32[]{:S(2)}) collective-permute-start(f32[2,128,256]{2,1,0:T(8,128)S(1)} %copy.46.mid_ref), channel_id=1, source_target_pairs={{0,1},{1,2},{2,3},{3,4},{4,5},{5,6},{6,7},{7,8},{8,9},{9,10},{10,1... | collective-permute-start | bytes 786440 | tf_op jit(solution)/shard_map/while/body/eval_jaxpr/ppermute | solution.py:79
  112.7 4.0 %copy-start.3 = (f32[2,128,256]{2,1,0:T(8,128)}, f32[2,128,256]{2,1,0:T(8,128)S(1)}, u32[]{:S(2)}) copy-start(f32[2,128,256]{2,1,0:T(8,128)S(1)} %collective-permute-done.1.right_ref) | copy-start | bytes 786436 | tf_op jit(solution)/shard_map/while
  129.8 11.7 %copy-start.1 = (f32[2,128,256]{2,1,0:T(8,128)}, f32[2,128,256]{2,1,0:T(8,128)S(1)}, u32[]{:S(2)}) copy-start(f32[2,128,256]{2,1,0:T(8,128)S(1)} %copy.46.mid_ref) | copy-start | bytes 786436 | tf_op jit(solution)/shard_map/while
  129.8 8.2 %collective-permute-start.1 = (f32[2,128,256]{2,1,0:T(8,128)S(1)}, f32[2,128,256]{2,1,0:T(8,128)S(1)}, u32[]{:S(2)}, u32[]{:S(2)}) collective-permute-start(f32[2,128,256]{2,1,0:T(8,128)S(1)} %copy.46.mid_ref), channel_id=1, source_target_pairs={{1,0},{2,1},{3,2},{4,3},{5,4},{6,5},{7,6},{8,7},{9,8},{10,9},{11,1... | collective-permute-start | bytes 786440 | tf_op jit(solution)/shard_map/while/body/eval_jaxpr/ppermute | solution.py:80
  131.7 9.8 %collective-permute-start = (f32[2,128,256]{2,1,0:T(8,128)S(1)}, f32[2,128,256]{2,1,0:T(8,128)S(1)}, u32[]{:S(2)}, u32[]{:S(2)}) collective-permute-start(f32[2,128,256]{2,1,0:T(8,128)S(1)} %copy.46.mid_ref), channel_id=1, source_target_pairs={{0,1},{1,2},{2,3},{3,4},{4,5},{5,6},{6,7},{7,8},{8,9},{9,10},{10,1... | collective-permute-start | bytes 786440 | tf_op jit(solution)/shard_map/while/body/eval_jaxpr/ppermute | solution.py:79
  138.0 3.6 %copy-start.3 = (f32[2,128,256]{2,1,0:T(8,128)}, f32[2,128,256]{2,1,0:T(8,128)S(1)}, u32[]{:S(2)}) copy-start(f32[2,128,256]{2,1,0:T(8,128)S(1)} %collective-permute-done.1.right_ref) | copy-start | bytes 786436 | tf_op jit(solution)/shard_map/while
  154.7 11.7 %copy-start.1 = (f32[2,128,256]{2,1,0:T(8,128)}, f32[2,128,256]{2,1,0:T(8,128)S(1)}, u32[]{:S(2)}) copy-start(f32[2,128,256]{2,1,0:T(8,128)S(1)} %copy.46.mid_ref) | copy-start | bytes 786436 | tf_op jit(solution)/shard_map/while
  154.7 8.2 %collective-permute-start.1 = (f32[2,128,256]{2,1,0:T(8,128)S(1)}, f32[2,128,256]{2,1,0:T(8,128)S(1)}, u32[]{:S(2)}, u32[]{:S(2)}) collective-permute-start(f32[2,128,256]{2,1,0:T(8,128)S(1)} %copy.46.mid_ref), channel_id=1, source_target_pairs={{1,0},{2,1},{3,2},{4,3},{5,4},{6,5},{7,6},{8,7},{9,8},{10,9},{11,1... | collective-permute-start | bytes 786440 | tf_op jit(solution)/shard_map/while/body/eval_jaxpr/ppermute | solution.py:80
  156.6 9.8 %collective-permute-start = (f32[2,128,256]{2,1,0:T(8,128)S(1)}, f32[2,128,256]{2,1,0:T(8,128)S(1)}, u32[]{:S(2)}, u32[]{:S(2)}) collective-permute-start(f32[2,128,256]{2,1,0:T(8,128)S(1)} %copy.46.mid_ref), channel_id=1, source_target_pairs={{0,1},{1,2},{2,3},{3,4},{4,5},{5,6},{6,7},{7,8},{8,9},{9,10},{10,1... | collective-permute-start | bytes 786440 | tf_op jit(solution)/shard_map/while/body/eval_jaxpr/ppermute | solution.py:79
  162.8 3.6 %copy-start.3 = (f32[2,128,256]{2,1,0:T(8,128)}, f32[2,128,256]{2,1,0:T(8,128)S(1)}, u32[]{:S(2)}) copy-start(f32[2,128,256]{2,1,0:T(8,128)S(1)} %collective-permute-done.1.right_ref) | copy-start | bytes 786436 | tf_op jit(solution)/shard_map/while
  179.5 11.7 %copy-start.1 = (f32[2,128,256]{2,1,0:T(8,128)}, f32[2,128,256]{2,1,0:T(8,128)S(1)}, u32[]{:S(2)}) copy-start(f32[2,128,256]{2,1,0:T(8,128)S(1)} %copy.46.mid_ref) | copy-start | bytes 786436 | tf_op jit(solution)/shard_map/while
  179.6 8.2 %collective-permute-start.1 = (f32[2,128,256]{2,1,0:T(8,128)S(1)}, f32[2,128,256]{2,1,0:T(8,128)S(1)}, u32[]{:S(2)}, u32[]{:S(2)}) collective-permute-start(f32[2,128,256]{2,1,0:T(8,128)S(1)} %copy.46.mid_ref), channel_id=1, source_target_pairs={{1,0},{2,1},{3,2},{4,3},{5,4},{6,5},{7,6},{8,7},{9,8},{10,9},{11,1... | collective-permute-start | bytes 786440 | tf_op jit(solution)/shard_map/while/body/eval_jaxpr/ppermute | solution.py:80
  181.5 9.8 %collective-permute-start = (f32[2,128,256]{2,1,0:T(8,128)S(1)}, f32[2,128,256]{2,1,0:T(8,128)S(1)}, u32[]{:S(2)}, u32[]{:S(2)}) collective-permute-start(f32[2,128,256]{2,1,0:T(8,128)S(1)} %copy.46.mid_ref), channel_id=1, source_target_pairs={{0,1},{1,2},{2,3},{3,4},{4,5},{5,6},{6,7},{7,8},{8,9},{9,10},{10,1... | collective-permute-start | bytes 786440 | tf_op jit(solution)/shard_map/while/body/eval_jaxpr/ppermute | solution.py:79
  187.7 3.6 %copy-start.3 = (f32[2,128,256]{2,1,0:T(8,128)}, f32[2,128,256]{2,1,0:T(8,128)S(1)}, u32[]{:S(2)}) copy-start(f32[2,128,256]{2,1,0:T(8,128)S(1)} %collective-permute-done.1.right_ref) | copy-start | bytes 786436 | tf_op jit(solution)/shard_map/while
  204.4 11.7 %copy-start.1 = (f32[2,128,256]{2,1,0:T(8,128)}, f32[2,128,256]{2,1,0:T(8,128)S(1)}, u32[]{:S(2)}) copy-start(f32[2,128,256]{2,1,0:T(8,128)S(1)} %copy.46.mid_ref) | copy-start | bytes 786436 | tf_op jit(solution)/shard_map/while
  204.4 8.2 %collective-permute-start.1 = (f32[2,128,256]{2,1,0:T(8,128)S(1)}, f32[2,128,256]{2,1,0:T(8,128)S(1)}, u32[]{:S(2)}, u32[]{:S(2)}) collective-permute-start(f32[2,128,256]{2,1,0:T(8,128)S(1)} %copy.46.mid_ref), channel_id=1, source_target_pairs={{1,0},{2,1},{3,2},{4,3},{5,4},{6,5},{7,6},{8,7},{9,8},{10,9},{11,1... | collective-permute-start | bytes 786440 | tf_op jit(solution)/shard_map/while/body/eval_jaxpr/ppermute | solution.py:80
  206.3 9.8 %collective-permute-start = (f32[2,128,256]{2,1,0:T(8,128)S(1)}, f32[2,128,256]{2,1,0:T(8,128)S(1)}, u32[]{:S(2)}, u32[]{:S(2)}) collective-permute-start(f32[2,128,256]{2,1,0:T(8,128)S(1)} %copy.46.mid_ref), channel_id=1, source_target_pairs={{0,1},{1,2},{2,3},{3,4},{4,5},{5,6},{6,7},{7,8},{8,9},{9,10},{10,1... | collective-permute-start | bytes 786440 | tf_op jit(solution)/shard_map/while/body/eval_jaxpr/ppermute | solution.py:79
  229.2 11.7 %copy-start.1 = (f32[2,128,256]{2,1,0:T(8,128)}, f32[2,128,256]{2,1,0:T(8,128)S(1)}, u32[]{:S(2)}) copy-start(f32[2,128,256]{2,1,0:T(8,128)S(1)} %copy.46.mid_ref) | copy-start | bytes 786436 | tf_op jit(solution)/shard_map/while
  229.2 8.2 %collective-permute-start.1 = (f32[2,128,256]{2,1,0:T(8,128)S(1)}, f32[2,128,256]{2,1,0:T(8,128)S(1)}, u32[]{:S(2)}, u32[]{:S(2)}) collective-permute-start(f32[2,128,256]{2,1,0:T(8,128)S(1)} %copy.46.mid_ref), channel_id=1, source_target_pairs={{1,0},{2,1},{3,2},{4,3},{5,4},{6,5},{7,6},{8,7},{9,8},{10,9},{11,1... | collective-permute-start | bytes 786440 | tf_op jit(solution)/shard_map/while/body/eval_jaxpr/ppermute | solution.py:80
  231.2 9.8 %collective-permute-start = (f32[2,128,256]{2,1,0:T(8,128)S(1)}, f32[2,128,256]{2,1,0:T(8,128)S(1)}, u32[]{:S(2)}, u32[]{:S(2)}) collective-permute-start(f32[2,128,256]{2,1,0:T(8,128)S(1)} %copy.46.mid_ref), channel_id=1, source_target_pairs={{0,1},{1,2},{2,3},{3,4},{4,5},{5,6},{6,7},{7,8},{8,9},{9,10},{10,1... | collective-permute-start | bytes 786440 | tf_op jit(solution)/shard_map/while/body/eval_jaxpr/ppermute | solution.py:79
  254.1 11.7 %copy-start.1 = (f32[2,128,256]{2,1,0:T(8,128)}, f32[2,128,256]{2,1,0:T(8,128)S(1)}, u32[]{:S(2)}) copy-start(f32[2,128,256]{2,1,0:T(8,128)S(1)} %copy.46.mid_ref) | copy-start | bytes 786436 | tf_op jit(solution)/shard_map/while
  254.1 8.2 %collective-permute-start.1 = (f32[2,128,256]{2,1,0:T(8,128)S(1)}, f32[2,128,256]{2,1,0:T(8,128)S(1)}, u32[]{:S(2)}, u32[]{:S(2)}) collective-permute-start(f32[2,128,256]{2,1,0:T(8,128)S(1)} %copy.46.mid_ref), channel_id=1, source_target_pairs={{1,0},{2,1},{3,2},{4,3},{5,4},{6,5},{7,6},{8,7},{9,8},{10,9},{11,1... | collective-permute-start | bytes 786440 | tf_op jit(solution)/shard_map/while/body/eval_jaxpr/ppermute | solution.py:80
  256.0 9.8 %collective-permute-start = (f32[2,128,256]{2,1,0:T(8,128)S(1)}, f32[2,128,256]{2,1,0:T(8,128)S(1)}, u32[]{:S(2)}, u32[]{:S(2)}) collective-permute-start(f32[2,128,256]{2,1,0:T(8,128)S(1)} %copy.46.mid_ref), channel_id=1, source_target_pairs={{0,1},{1,2},{2,3},{3,4},{4,5},{5,6},{6,7},{7,8},{8,9},{9,10},{10,1... | collective-permute-start | bytes 786440 | tf_op jit(solution)/shard_map/while/body/eval_jaxpr/ppermute | solution.py:79
  262.2 3.6 %copy-start.3 = (f32[2,128,256]{2,1,0:T(8,128)}, f32[2,128,256]{2,1,0:T(8,128)S(1)}, u32[]{:S(2)}) copy-start(f32[2,128,256]{2,1,0:T(8,128)S(1)} %collective-permute-done.1.right_ref) | copy-start | bytes 786436 | tf_op jit(solution)/shard_map/while
  278.9 11.8 %copy-start.1 = (f32[2,128,256]{2,1,0:T(8,128)}, f32[2,128,256]{2,1,0:T(8,128)S(1)}, u32[]{:S(2)}) copy-start(f32[2,128,256]{2,1,0:T(8,128)S(1)} %copy.46.mid_ref) | copy-start | bytes 786436 | tf_op jit(solution)/shard_map/while
  278.9 8.2 %collective-permute-start.1 = (f32[2,128,256]{2,1,0:T(8,128)S(1)}, f32[2,128,256]{2,1,0:T(8,128)S(1)}, u32[]{:S(2)}, u32[]{:S(2)}) collective-permute-start(f32[2,128,256]{2,1,0:T(8,128)S(1)} %copy.46.mid_ref), channel_id=1, source_target_pairs={{1,0},{2,1},{3,2},{4,3},{5,4},{6,5},{7,6},{8,7},{9,8},{10,9},{11,1... | collective-permute-start | bytes 786440 | tf_op jit(solution)/shard_map/while/body/eval_jaxpr/ppermute | solution.py:80
  280.8 9.9 %collective-permute-start = (f32[2,128,256]{2,1,0:T(8,128)S(1)}, f32[2,128,256]{2,1,0:T(8,128)S(1)}, u32[]{:S(2)}, u32[]{:S(2)}) collective-permute-start(f32[2,128,256]{2,1,0:T(8,128)S(1)} %copy.46.mid_ref), channel_id=1, source_target_pairs={{0,1},{1,2},{2,3},{3,4},{4,5},{5,6},{6,7},{7,8},{8,9},{9,10},{10,1... | collective-permute-start | bytes 786440 | tf_op jit(solution)/shard_map/while/body/eval_jaxpr/ppermute | solution.py:79
  287.1 3.7 %copy-start.3 = (f32[2,128,256]{2,1,0:T(8,128)}, f32[2,128,256]{2,1,0:T(8,128)S(1)}, u32[]{:S(2)}) copy-start(f32[2,128,256]{2,1,0:T(8,128)S(1)} %collective-permute-done.1.right_ref) | copy-start | bytes 786436 | tf_op jit(solution)/shard_map/while
  (11 other events, 13.6 us)
Sparse Core Ops, SparseCore 0:
  16.7 69.2 all-gather.2

commit v4 on v3

v4 whole, which is shorter than its diff:
```python
import functools

import jax
import jax.numpy as jnp
from jax import lax
from jax.sharding import PartitionSpec as P
from jax.experimental import pallas as pl
from jax.experimental.pallas import tpu as pltpu

ROWS = 128
HIGHEST = lax.Precision.HIGHEST


def banded(row, width):
    grid = jnp.broadcast_to(row, (width, 2 * width))
    return pltpu.roll(grid, 0, 1, stride=1, stride_axis=0).T


def group_kernel(origin_ref, nonlinear_ref, left_ref, mid_ref, right_ref, params_ref, out_ref, *,
                 spans, steps, half_taps, length):
    width = 2 * half_taps
    halo = spans * steps * half_taps
    extent = mid_ref.shape[-1]
    origin = origin_ref[0]
    matrices = 2 * spans * steps
    table = params_ref[matrices]

    def taps_row(row):
        pair = table[2 * row:2 * row + 2]
        return jnp.concatenate([pair[0:1], pair[1:2]], axis=1)

    gains = table[2 * matrices:2 * matrices + 8].T
    parts = []
    for part in range(2):
        parts.append(jnp.concatenate(
            [left_ref[part, :, extent - halo:], mid_ref[part], right_ref[part, :, :halo]], axis=1))
    real, imag = parts
    offset = -halo
    for span_index in range(spans):
        for step_index in range(steps):
            index = span_index * steps + step_index
            blocks = real.shape[1] // width - 1
            windows = jnp.concatenate(
                [jnp.concatenate([real[:, b * width:(b + 2) * width], imag[:, b * width:(b + 2) * width]], axis=1)
                 for b in range(blocks)], axis=0)
            real_band = banded(taps_row(2 * index), width)
            imag_band = banded(taps_row(2 * index + 1), width)
            response = jnp.concatenate([
                jnp.concatenate([real_band, imag_band], axis=1),
                jnp.concatenate([-imag_band, real_band], axis=1)], axis=0)
            product = jnp.dot(windows, response, precision=HIGHEST,
                              preferred_element_type=jnp.float32)
            real = jnp.concatenate([product[b * ROWS:(b + 1) * ROWS, :width] for b in range(blocks)], axis=1)
            imag = jnp.concatenate([product[b * ROWS:(b + 1) * ROWS, width:] for b in range(blocks)], axis=1)
            offset = offset + half_taps
            dispersed = jnp.concatenate([real, imag], axis=0)
            real_coupling = params_ref[2 * index]
            imag_coupling = params_ref[2 * index + 1]
            mixer = jnp.concatenate([
                jnp.concatenate([real_coupling, -imag_coupling], axis=1),
                jnp.concatenate([imag_coupling, real_coupling], axis=1)], axis=0)
            mixed = jnp.dot(mixer, dispersed, precision=HIGHEST,
                            preferred_element_type=jnp.float32)
            where = origin + offset + lax.broadcasted_iota(jnp.int32, (1, mixed.shape[1]), 1)
            inside = (where >= 0) & (where < length)
            mixed = jnp.where(inside, mixed, 0.0)
            power = jnp.sum(mixed * mixed, axis=0, keepdims=True)
            phase = nonlinear_ref[index] * power
            cosine = jnp.cos(phase)
            sine = jnp.sin(phase)
            real_mixed = mixed[:ROWS]
            imag_mixed = mixed[ROWS:]
            real = real_mixed * cosine - imag_mixed * sine
            imag = real_mixed * sine + imag_mixed * cosine
        gain = gains[:, span_index:span_index + 1]
        real = real * gain
        imag = imag * gain
    out_ref[0] = real
    out_ref[1] = imag


def group_pass(signal, params, origin, length, spans, steps, half_taps):
    halo = spans * steps * half_taps
    count = lax.axis_size("tm")
    forward = [(i, i + 1) for i in range(count - 1)]
    backward = [(i + 1, i) for i in range(count - 1)]
    left = lax.ppermute(signal, "tm", forward)
    right = lax.ppermute(signal, "tm", backward)
    matrices = 2 * spans * steps
    nonlinear_group = params[matrices, 2 * matrices + 8, : spans * steps]
    vmem = pl.BlockSpec(memory_space=pltpu.VMEM)
    smem = pl.BlockSpec(memory_space=pltpu.SMEM)
    blocks = (signal.shape[-1] + 2 * halo) // (2 * half_taps)
    flops = 2 * spans * steps * ROWS * (blocks * 4 * half_taps * 4 * half_taps + 4 * ROWS * signal.shape[-1] * 2)
    kernel = pl.pallas_call(
        functools.partial(group_kernel, spans=spans, steps=steps, half_taps=half_taps, length=length),
        out_shape=jax.ShapeDtypeStruct(signal.shape, jnp.float32),
        in_specs=[smem, smem, vmem, vmem, vmem, vmem],
        out_specs=vmem,
        cost_estimate=pl.CostEstimate(flops=6 * flops, transcendentals=0,
                                      bytes_accessed=4 * (4 * signal.size + params.size)),
    )
    return kernel(origin.reshape(1), nonlinear_group, left, signal, right, params)


def shards(launched, coupling, impulse, amplifier, nonlinear):
    sections = lax.axis_size("span")
    section_index = lax.axis_index("span")
    frames_count, _, _, extent = launched.shape
    per_section = frames_count // sections
    length = extent * lax.axis_size("tm")
    origin = lax.axis_index("tm") * extent

    local_groups, spans, steps, _, taps_count = impulse.shape
    groups = local_groups * sections
    half_taps = (taps_count - 1) // 2
    channels = launched.shape[2]
    grow = ROWS - channels
    matrices = 2 * spans * steps
    assert 4 * matrices + 16 <= ROWS and 4 * half_taps == 2 * ROWS and spans <= 8
    taps_rows = jnp.pad(impulse, ((0, 0),) * 4 + ((0, 4 * half_taps - taps_count),)).reshape(
        local_groups, 2 * matrices, ROWS)
    gain_rows = jnp.pad(amplifier, ((0, 0), (0, 8 - spans), (0, grow)))
    nonlinear_rows = jnp.pad(nonlinear.reshape(local_groups, 1, spans * steps),
                             ((0, 0), (0, 0), (0, ROWS - spans * steps)))
    table = jnp.concatenate([taps_rows, gain_rows, nonlinear_rows], axis=1)
    table = jnp.pad(table, ((0, 0), (0, ROWS - table.shape[1]), (0, 0)))
    local = jnp.concatenate([
        jnp.pad(coupling, ((0, 0),) * 4 + ((0, grow), (0, grow))).reshape(
            local_groups, matrices, ROWS, ROWS),
        table[:, None]], axis=1)

    def fetched(group):
        owner = group // local_groups
        chosen = lax.dynamic_index_in_dim(local, group % local_groups, 0, keepdims=False)
        return lax.psum(jnp.where(section_index == owner, chosen, 0.0), "span")

    signal = lax.dynamic_slice_in_dim(launched, section_index * per_section, per_section, 0)
    signal = jnp.pad(signal, ((0, 0), (0, 0), (0, grow), (0, 0)))

    def advance(carry, group):
        signal, params = carry
        upcoming = fetched(jnp.minimum(group + 1, groups - 1))
        signal = jnp.stack([
            group_pass(signal[frame], params, origin, length, spans, steps, half_taps)
            for frame in range(signal.shape[0])])
        return (signal, upcoming), signal

    start = (signal, fetched(jnp.int32(0)))
    _, stacked = lax.scan(advance, start, jnp.arange(groups, dtype=jnp.int32))
    stacked = stacked[:, :, :, :channels]
    return lax.all_to_all(stacked, "span", 0, 1, tiled=True)


def solution(mesh):
    placed = (
        P(None, None, None, "tm"),
        P("span", None, None, None, None, None),
        P("span", None, None, None, None),
        P("span", None, None),
        P("span", None, None),
    )
    return jax.shard_map(
        shards,
        mesh=mesh,
        in_specs=placed,
        out_specs=P("span", None, None, None, "tm"),
        check_vma=False,
    )
```

time: 340 us -> 929 us (2.73)
  waiting for transfers between devices: 98.3 us -> 713 us
  local copies, waits for them, and re-layouts: 73.2 us -> 38.5 us
    psum x0 -> x9, waiting for transfers between devices: none -> 671 us  [fetched(): return lax.psum(jnp.where(section_index == owner, chosen, 0.0), 'span')]
    all_gather x1 -> x0, waiting for transfers between devices: 69.3 us -> none  [shards(): gathered = lax.all_gather(packed, 'span', axis=0, tiled=True)]
    squeeze x40 -> x8, local copies, waits for them, and re-layouts: 30.6 us -> 4.67 us  [group_pass(): nonlinear_group = params[matrices, 2 * matrices + 8, :spans * steps]]
    ppermute x8, waiting for transfers between devices: 29 us -> 41.8 us  [group_pass(): left = lax.ppermute(signal, 'tm', forward)]
    while x56 -> x64, local copies, waits for them, and re-layouts: 5.87 us -> 15.7 us
    reshape x8 -> x2, local copies, waits for them, and re-layouts: 10.5 us -> 0.9 us  [the longest x1 0.89 us: shards(): nonlinear.reshape(local_groups, 1, spans * steps)]
  transfers between devices with their start and end apart: 17 -> 25, of which waited for: 9 -> 17; matrix products, arithmetic and copies ran while one was open for 9% -> 3% of each run, Pallas kernels for 0% -> 10%
where the time goes in v4:
time: 929 us; the launch traced here: 928 us
  waiting for transfers between devices  713 us (77%)
  Pallas kernels  89.8 us (10%)
  local copies, waits for them, and re-layouts  38.5 us (4%)
  starting transfers between devices  35.7 us (4%)
  blocking collectives  23.7 us (3%)
  between operations  13.1 us (1%)
    psum x9, waiting for transfers between devices, fetched(): return lax.psum(jnp.where(section_index == owner, chosen, 0.0), 'span')  671 us
    pallas_call x8, Pallas kernels, group_pass(): kernel(origin.reshape(1), nonlinear_group, left, signal, right, params)  89.8 us
    ppermute x8, waiting for transfers between devices, group_pass(): left = lax.ppermute(signal, 'tm', forward)  41.8 us
    all_to_all x1, blocking collectives, shards(): return lax.all_to_all(stacked, 'span', 0, 1, tiled=True)  23.7 us
    ppermute x8, starting transfers between devices, group_pass(): left = lax.ppermute(signal, 'tm', forward)  19.3 us
  transfers between devices with their start and end apart: 25, of which 17 were waited for; matrix products, arithmetic and copies ran while one was open for 3% of the time, Pallas kernels for 10%

profile of v4, /device:TPU:2, one launch (start us, length us, event | category | flops | bytes accessed | tf_op | source)
XLA Modules:
  0.0 928.1 jit_solution(4897644060488693960)
XLA Ops:
  11.0 94.1 %all-reduce.9.cloned.1.call-done = f32[9,128,128]{2,1,0:T(8,128)} async-done(((f32[9,128,128]{2,1,0:T(8,128)}), f32[9,128,128]{2,1,0:T(8,128)}) %all-reduce.9.cloned.1.call-update) | async-done | bytes 589840 | tf_op jit(solution)/shard_map/psum | solution.py:136
  105.1 789.3 %while.16 = (s32[]{:T(128)}, f32[1,2,128,256]{3,2,1,0:T(8,128)S(1)}, f32[9,128,128]{2,1,0:T(8,128)}, f32[8,1,2,128,256]{4,2,3,1,0:T(2,128)}, s32[]{:T(128)}, /*i...) while((s32[]{:T(128)}, ...), condition=%wide.region_3.4_spmd, body=%wide.region_1.3_spmd.sunk | while | flops 4026826752 | bytes 15139219 | solution.py:150
  107.2 2.4 collective-permute-start
  112.4 5.2 collective-permute-done.left_ref
  117.6 11.2 %eval_jaxpr.4 = f32[2,128,256]{2,1,0:T(8,128)S(1)} custom-call(s32[1]{0:T(128)} %bitcast.24.origin_ref, f32[4]{0:T(128)} %slice_bitcast_fusion.2.nonlinear_ref, f32[2,128,256]{2,1,0:T(8,128)} %collective-permute-done.left_ref, f32[2,128,256]{2,1,0:T(8,128)} %copy-done.1, f32[2,128,256]{2,1,0:T(8,128)} %copy-done.3, f32[9,128,128]{2,1,0:T(8,128)S(1)} %copy-done.2), custom_call_target="tpu_custom_call" | custom-call | flops 4026531840 | bytes 1638400 | tf_op jit(solution)/shard_map/while/body/eval_jaxpr/pallas_call | solution.py:103
  129.7 72.1 %all-reduce.11.cloned.1.call-done = f32[9,128,128]{2,1,0:T(8,128)} async-done(((f32[9,128,128]{2,1,0:T(8,128)}), f32[9,128,128]{2,1,0:T(8,128)}) %all-reduce.11.cloned.1.call-update) | async-done | bytes 589840 | tf_op jit(solution)/shard_map/while/body/eval_jaxpr/psum | solution.py:136
  205.9 2.4 collective-permute-start
  211.1 5.2 collective-permute-done.left_ref
  216.3 11.2 %eval_jaxpr.4 = f32[2,128,256]{2,1,0:T(8,128)S(1)} custom-call(s32[1]{0:T(128)} %bitcast.24.origin_ref, f32[4]{0:T(128)} %slice_bitcast_fusion.2.nonlinear_ref, f32[2,128,256]{2,1,0:T(8,128)} %collective-permute-done.left_ref, f32[2,128,256]{2,1,0:T(8,128)} %copy-done.1, f32[2,128,256]{2,1,0:T(8,128)} %copy-done.3, f32[9,128,128]{2,1,0:T(8,128)S(1)} %copy-done.2), custom_call_target="tpu_custom_call" | custom-call | flops 4026531840 | bytes 1638400 | tf_op jit(solution)/shard_map/while/body/eval_jaxpr/pallas_call | solution.py:103
  228.4 72.1 %all-reduce.11.cloned.1.call-done = f32[9,128,128]{2,1,0:T(8,128)} async-done(((f32[9,128,128]{2,1,0:T(8,128)}), f32[9,128,128]{2,1,0:T(8,128)}) %all-reduce.11.cloned.1.call-update) | async-done | bytes 589840 | tf_op jit(solution)/shard_map/while/body/eval_jaxpr/psum | solution.py:136
  304.6 2.4 collective-permute-start
  309.7 5.2 collective-permute-done.left_ref
  315.0 11.2 %eval_jaxpr.4 = f32[2,128,256]{2,1,0:T(8,128)S(1)} custom-call(s32[1]{0:T(128)} %bitcast.24.origin_ref, f32[4]{0:T(128)} %slice_bitcast_fusion.2.nonlinear_ref, f32[2,128,256]{2,1,0:T(8,128)} %collective-permute-done.left_ref, f32[2,128,256]{2,1,0:T(8,128)} %copy-done.1, f32[2,128,256]{2,1,0:T(8,128)} %copy-done.3, f32[9,128,128]{2,1,0:T(8,128)S(1)} %copy-done.2), custom_call_target="tpu_custom_call" | custom-call | flops 4026531840 | bytes 1638400 | tf_op jit(solution)/shard_map/while/body/eval_jaxpr/pallas_call | solution.py:103
  327.1 72.1 %all-reduce.11.cloned.1.call-done = f32[9,128,128]{2,1,0:T(8,128)} async-done(((f32[9,128,128]{2,1,0:T(8,128)}), f32[9,128,128]{2,1,0:T(8,128)}) %all-reduce.11.cloned.1.call-update) | async-done | bytes 589840 | tf_op jit(solution)/shard_map/while/body/eval_jaxpr/psum | solution.py:136
  408.4 5.2 collective-permute-done.left_ref
  413.6 11.2 %eval_jaxpr.4 = f32[2,128,256]{2,1,0:T(8,128)S(1)} custom-call(s32[1]{0:T(128)} %bitcast.24.origin_ref, f32[4]{0:T(128)} %slice_bitcast_fusion.2.nonlinear_ref, f32[2,128,256]{2,1,0:T(8,128)} %collective-permute-done.left_ref, f32[2,128,256]{2,1,0:T(8,128)} %copy-done.1, f32[2,128,256]{2,1,0:T(8,128)} %copy-done.3, f32[9,128,128]{2,1,0:T(8,128)S(1)} %copy-done.2), custom_call_target="tpu_custom_call" | custom-call | flops 4026531840 | bytes 1638400 | tf_op jit(solution)/shard_map/while/body/eval_jaxpr/pallas_call | solution.py:103
  425.8 72.1 %all-reduce.11.cloned.1.call-done = f32[9,128,128]{2,1,0:T(8,128)} async-done(((f32[9,128,128]{2,1,0:T(8,128)}), f32[9,128,128]{2,1,0:T(8,128)}) %all-reduce.11.cloned.1.call-update) | async-done | bytes 589840 | tf_op jit(solution)/shard_map/while/body/eval_jaxpr/psum | solution.py:136
  507.1 5.2 collective-permute-done.left_ref
  512.3 11.2 %eval_jaxpr.4 = f32[2,128,256]{2,1,0:T(8,128)S(1)} custom-call(s32[1]{0:T(128)} %bitcast.24.origin_ref, f32[4]{0:T(128)} %slice_bitcast_fusion.2.nonlinear_ref, f32[2,128,256]{2,1,0:T(8,128)} %collective-permute-done.left_ref, f32[2,128,256]{2,1,0:T(8,128)} %copy-done.1, f32[2,128,256]{2,1,0:T(8,128)} %copy-done.3, f32[9,128,128]{2,1,0:T(8,128)S(1)} %copy-done.2), custom_call_target="tpu_custom_call" | custom-call | flops 4026531840 | bytes 1638400 | tf_op jit(solution)/shard_map/while/body/eval_jaxpr/pallas_call | solution.py:103
  524.4 72.1 %all-reduce.11.cloned.1.call-done = f32[9,128,128]{2,1,0:T(8,128)} async-done(((f32[9,128,128]{2,1,0:T(8,128)}), f32[9,128,128]{2,1,0:T(8,128)}) %all-reduce.11.cloned.1.call-update) | async-done | bytes 589840 | tf_op jit(solution)/shard_map/while/body/eval_jaxpr/psum | solution.py:136
  600.6 2.4 collective-permute-start
  605.7 5.2 collective-permute-done.left_ref
  611.0 11.2 %eval_jaxpr.4 = f32[2,128,256]{2,1,0:T(8,128)S(1)} custom-call(s32[1]{0:T(128)} %bitcast.24.origin_ref, f32[4]{0:T(128)} %slice_bitcast_fusion.2.nonlinear_ref, f32[2,128,256]{2,1,0:T(8,128)} %collective-permute-done.left_ref, f32[2,128,256]{2,1,0:T(8,128)} %copy-done.1, f32[2,128,256]{2,1,0:T(8,128)} %copy-done.3, f32[9,128,128]{2,1,0:T(8,128)S(1)} %copy-done.2), custom_call_target="tpu_custom_call" | custom-call | flops 4026531840 | bytes 1638400 | tf_op jit(solution)/shard_map/while/body/eval_jaxpr/pallas_call | solution.py:103
  623.1 72.1 %all-reduce.11.cloned.1.call-done = f32[9,128,128]{2,1,0:T(8,128)} async-done(((f32[9,128,128]{2,1,0:T(8,128)}), f32[9,128,128]{2,1,0:T(8,128)}) %all-reduce.11.cloned.1.call-update) | async-done | bytes 589840 | tf_op jit(solution)/shard_map/while/body/eval_jaxpr/psum | solution.py:136
  699.2 2.4 collective-permute-start
  704.4 5.2 collective-permute-done.left_ref
  709.6 11.2 %eval_jaxpr.4 = f32[2,128,256]{2,1,0:T(8,128)S(1)} custom-call(s32[1]{0:T(128)} %bitcast.24.origin_ref, f32[4]{0:T(128)} %slice_bitcast_fusion.2.nonlinear_ref, f32[2,128,256]{2,1,0:T(8,128)} %collective-permute-done.left_ref, f32[2,128,256]{2,1,0:T(8,128)} %copy-done.1, f32[2,128,256]{2,1,0:T(8,128)} %copy-done.3, f32[9,128,128]{2,1,0:T(8,128)S(1)} %copy-done.2), custom_call_target="tpu_custom_call" | custom-call | flops 4026531840 | bytes 1638400 | tf_op jit(solution)/shard_map/while/body/eval_jaxpr/pallas_call | solution.py:103
  721.8 72.1 %all-reduce.11.cloned.1.call-done = f32[9,128,128]{2,1,0:T(8,128)} async-done(((f32[9,128,128]{2,1,0:T(8,128)}), f32[9,128,128]{2,1,0:T(8,128)}) %all-reduce.11.cloned.1.call-update) | async-done | bytes 589840 | tf_op jit(solution)/shard_map/while/body/eval_jaxpr/psum | solution.py:136
  803.1 5.2 collective-permute-done.left_ref
  808.3 11.2 %eval_jaxpr.4 = f32[2,128,256]{2,1,0:T(8,128)S(1)} custom-call(s32[1]{0:T(128)} %bitcast.24.origin_ref, f32[4]{0:T(128)} %slice_bitcast_fusion.2.nonlinear_ref, f32[2,128,256]{2,1,0:T(8,128)} %collective-permute-done.left_ref, f32[2,128,256]{2,1,0:T(8,128)} %copy-done.1, f32[2,128,256]{2,1,0:T(8,128)} %copy-done.3, f32[9,128,128]{2,1,0:T(8,128)S(1)} %copy-done.2), custom_call_target="tpu_custom_call" | custom-call | flops 4026531840 | bytes 1638400 | tf_op jit(solution)/shard_map/while/body/eval_jaxpr/pallas_call | solution.py:103
  820.4 72.1 %all-reduce.11.cloned.1.call-done = f32[9,128,128]{2,1,0:T(8,128)} async-done(((f32[9,128,128]{2,1,0:T(8,128)}), f32[9,128,128]{2,1,0:T(8,128)}) %all-reduce.11.cloned.1.call-update) | async-done | bytes 589840 | tf_op jit(solution)/shard_map/while/body/eval_jaxpr/psum | solution.py:136
  896.6 23.7 %all_to_all.12 = f32[8,1,2,110,256]{4,2,3,1,0:T(2,128)S(1)} all-to-all(f32[8,1,2,110,256]{4,2,3,1,0:T(2,128)S(1)} %slice.9), channel_id=1, replica_groups=mesh['span'=8,'tm'=32] {'span'}, dimensions={0} | all-to-all | bytes 3604480 | tf_op jit(solution)/shard_map/all_to_all | solution.py:152
  (150 shorter events, 70.8 us)
Async XLA Ops:
  6.5 98.6 %all-reduce.9.cloned.1.call-start = ((), (), s32[]{:S(2)}) async-start(), calls=%async_computation.1 | async-start | bytes 1179648 | tf_op jit(solution)/shard_map/psum | solution.py:136
  105.1 96.7 %all-reduce.11.cloned.1.call-start = ((), (), s32[]{:S(2)}) async-start(), calls=%async_computation.2 | async-start | bytes 1179648 | tf_op jit(solution)/shard_map/while/body/eval_jaxpr/psum | solution.py:136
  105.2 12.4 %copy-start.1 = (f32[2,128,256]{2,1,0:T(8,128)}, f32[2,128,256]{2,1,0:T(8,128)S(1)}, u32[]{:S(2)}) copy-start(f32[2,128,256]{2,1,0:T(8,128)S(1)} %copy.41.mid_ref) | copy-start | bytes 786436 | tf_op jit(solution)/shard_map/while
  105.2 7.2 collective-permute-start.1
  107.2 10.4 %collective-permute-start = (f32[2,128,256]{2,1,0:T(8,128)S(1)}, f32[2,128,256]{2,1,0:T(8,128)}, u32[]{:S(2)}, u32[]{:S(2)}) collective-permute-start(f32[2,128,256]{2,1,0:T(8,128)S(1)} %copy.41.mid_ref), channel_id=1, source_target_pairs={{0,1},{1,2},{2,3},{3,4},{4,5},{5,6},{6,7},{7,8},{8,9},{9,10},{10,1... | collective-permute-start | bytes 786440 | tf_op jit(solution)/shard_map/while/body/eval_jaxpr/ppermute | solution.py:87
  203.8 96.7 %all-reduce.11.cloned.1.call-start = ((), (), s32[]{:S(2)}) async-start(), calls=%async_computation.2 | async-start | bytes 1179648 | tf_op jit(solution)/shard_map/while/body/eval_jaxpr/psum | solution.py:136
  203.8 12.4 %copy-start.1 = (f32[2,128,256]{2,1,0:T(8,128)}, f32[2,128,256]{2,1,0:T(8,128)S(1)}, u32[]{:S(2)}) copy-start(f32[2,128,256]{2,1,0:T(8,128)S(1)} %copy.41.mid_ref) | copy-start | bytes 786436 | tf_op jit(solution)/shard_map/while
  203.8 7.2 collective-permute-start.1
  205.9 10.4 %collective-permute-start = (f32[2,128,256]{2,1,0:T(8,128)S(1)}, f32[2,128,256]{2,1,0:T(8,128)}, u32[]{:S(2)}, u32[]{:S(2)}) collective-permute-start(f32[2,128,256]{2,1,0:T(8,128)S(1)} %copy.41.mid_ref), channel_id=1, source_target_pairs={{0,1},{1,2},{2,3},{3,4},{4,5},{5,6},{6,7},{7,8},{8,9},{9,10},{10,1... | collective-permute-start | bytes 786440 | tf_op jit(solution)/shard_map/while/body/eval_jaxpr/ppermute | solution.py:87
  302.5 96.7 %all-reduce.11.cloned.1.call-start = ((), (), s32[]{:S(2)}) async-start(), calls=%async_computation.2 | async-start | bytes 1179648 | tf_op jit(solution)/shard_map/while/body/eval_jaxpr/psum | solution.py:136
  302.5 12.4 %copy-start.1 = (f32[2,128,256]{2,1,0:T(8,128)}, f32[2,128,256]{2,1,0:T(8,128)S(1)}, u32[]{:S(2)}) copy-start(f32[2,128,256]{2,1,0:T(8,128)S(1)} %copy.41.mid_ref) | copy-start | bytes 786436 | tf_op jit(solution)/shard_map/while
  302.5 7.2 collective-permute-start.1
  304.6 10.4 %collective-permute-start = (f32[2,128,256]{2,1,0:T(8,128)S(1)}, f32[2,128,256]{2,1,0:T(8,128)}, u32[]{:S(2)}, u32[]{:S(2)}) collective-permute-start(f32[2,128,256]{2,1,0:T(8,128)S(1)} %copy.41.mid_ref), channel_id=1, source_target_pairs={{0,1},{1,2},{2,3},{3,4},{4,5},{5,6},{6,7},{7,8},{8,9},{9,10},{10,1... | collective-permute-start | bytes 786440 | tf_op jit(solution)/shard_map/while/body/eval_jaxpr/ppermute | solution.py:87
  401.1 96.7 %all-reduce.11.cloned.1.call-start = ((), (), s32[]{:S(2)}) async-start(), calls=%async_computation.2 | async-start | bytes 1179648 | tf_op jit(solution)/shard_map/while/body/eval_jaxpr/psum | solution.py:136
  401.2 12.4 %copy-start.1 = (f32[2,128,256]{2,1,0:T(8,128)}, f32[2,128,256]{2,1,0:T(8,128)S(1)}, u32[]{:S(2)}) copy-start(f32[2,128,256]{2,1,0:T(8,128)S(1)} %copy.41.mid_ref) | copy-start | bytes 786436 | tf_op jit(solution)/shard_map/while
  401.2 7.2 collective-permute-start.1
  403.2 10.4 %collective-permute-start = (f32[2,128,256]{2,1,0:T(8,128)S(1)}, f32[2,128,256]{2,1,0:T(8,128)}, u32[]{:S(2)}, u32[]{:S(2)}) collective-permute-start(f32[2,128,256]{2,1,0:T(8,128)S(1)} %copy.41.mid_ref), channel_id=1, source_target_pairs={{0,1},{1,2},{2,3},{3,4},{4,5},{5,6},{6,7},{7,8},{8,9},{9,10},{10,1... | collective-permute-start | bytes 786440 | tf_op jit(solution)/shard_map/while/body/eval_jaxpr/ppermute | solution.py:87
  499.8 96.7 %all-reduce.11.cloned.1.call-start = ((), (), s32[]{:S(2)}) async-start(), calls=%async_computation.2 | async-start | bytes 1179648 | tf_op jit(solution)/shard_map/while/body/eval_jaxpr/psum | solution.py:136
  499.8 12.4 %copy-start.1 = (f32[2,128,256]{2,1,0:T(8,128)}, f32[2,128,256]{2,1,0:T(8,128)S(1)}, u32[]{:S(2)}) copy-start(f32[2,128,256]{2,1,0:T(8,128)S(1)} %copy.41.mid_ref) | copy-start | bytes 786436 | tf_op jit(solution)/shard_map/while
  499.8 7.2 collective-permute-start.1
  501.9 10.4 %collective-permute-start = (f32[2,128,256]{2,1,0:T(8,128)S(1)}, f32[2,128,256]{2,1,0:T(8,128)}, u32[]{:S(2)}, u32[]{:S(2)}) collective-permute-start(f32[2,128,256]{2,1,0:T(8,128)S(1)} %copy.41.mid_ref), channel_id=1, source_target_pairs={{0,1},{1,2},{2,3},{3,4},{4,5},{5,6},{6,7},{7,8},{8,9},{9,10},{10,1... | collective-permute-start | bytes 786440 | tf_op jit(solution)/shard_map/while/body/eval_jaxpr/ppermute | solution.py:87
  598.5 96.7 %all-reduce.11.cloned.1.call-start = ((), (), s32[]{:S(2)}) async-start(), calls=%async_computation.2 | async-start | bytes 1179648 | tf_op jit(solution)/shard_map/while/body/eval_jaxpr/psum | solution.py:136
  598.5 12.4 %copy-start.1 = (f32[2,128,256]{2,1,0:T(8,128)}, f32[2,128,256]{2,1,0:T(8,128)S(1)}, u32[]{:S(2)}) copy-start(f32[2,128,256]{2,1,0:T(8,128)S(1)} %copy.41.mid_ref) | copy-start | bytes 786436 | tf_op jit(solution)/shard_map/while
  598.5 7.2 collective-permute-start.1
  600.6 10.4 %collective-permute-start = (f32[2,128,256]{2,1,0:T(8,128)S(1)}, f32[2,128,256]{2,1,0:T(8,128)}, u32[]{:S(2)}, u32[]{:S(2)}) collective-permute-start(f32[2,128,256]{2,1,0:T(8,128)S(1)} %copy.41.mid_ref), channel_id=1, source_target_pairs={{0,1},{1,2},{2,3},{3,4},{4,5},{5,6},{6,7},{7,8},{8,9},{9,10},{10,1... | collective-permute-start | bytes 786440 | tf_op jit(solution)/shard_map/while/body/eval_jaxpr/ppermute | solution.py:87
  697.2 96.7 %all-reduce.11.cloned.1.call-start = ((), (), s32[]{:S(2)}) async-start(), calls=%async_computation.2 | async-start | bytes 1179648 | tf_op jit(solution)/shard_map/while/body/eval_jaxpr/psum | solution.py:136
  697.2 12.4 %copy-start.1 = (f32[2,128,256]{2,1,0:T(8,128)}, f32[2,128,256]{2,1,0:T(8,128)S(1)}, u32[]{:S(2)}) copy-start(f32[2,128,256]{2,1,0:T(8,128)S(1)} %copy.41.mid_ref) | copy-start | bytes 786436 | tf_op jit(solution)/shard_map/while
  697.2 7.2 collective-permute-start.1
  699.2 10.4 %collective-permute-start = (f32[2,128,256]{2,1,0:T(8,128)S(1)}, f32[2,128,256]{2,1,0:T(8,128)}, u32[]{:S(2)}, u32[]{:S(2)}) collective-permute-start(f32[2,128,256]{2,1,0:T(8,128)S(1)} %copy.41.mid_ref), channel_id=1, source_target_pairs={{0,1},{1,2},{2,3},{3,4},{4,5},{5,6},{6,7},{7,8},{8,9},{9,10},{10,1... | collective-permute-start | bytes 786440 | tf_op jit(solution)/shard_map/while/body/eval_jaxpr/ppermute | solution.py:87
  795.8 96.7 %all-reduce.11.cloned.1.call-start = ((), (), s32[]{:S(2)}) async-start(), calls=%async_computation.2 | async-start | bytes 1179648 | tf_op jit(solution)/shard_map/while/body/eval_jaxpr/psum | solution.py:136
  795.9 7.2 collective-permute-start.1
  797.9 10.4 %collective-permute-start = (f32[2,128,256]{2,1,0:T(8,128)S(1)}, f32[2,128,256]{2,1,0:T(8,128)}, u32[]{:S(2)}, u32[]{:S(2)}) collective-permute-start(f32[2,128,256]{2,1,0:T(8,128)S(1)} %copy.41.mid_ref), channel_id=1, source_target_pairs={{0,1},{1,2},{2,3},{3,4},{4,5},{5,6},{6,7},{7,8},{8,9},{9,10},{10,1... | collective-permute-start | bytes 786440 | tf_op jit(solution)/shard_map/while/body/eval_jaxpr/ppermute | solution.py:87
  (18 other events, 111.8 us)
Sparse Core Ops, SparseCore 0:
  11.0 94.0 all-reduce.8
  111.9 89.9 all-reduce.10
  210.6 89.9 all-reduce.10
  309.2 89.9 all-reduce.10
  407.9 89.9 all-reduce.10
  506.6 89.9 all-reduce.10
  605.2 89.9 all-reduce.10
  703.9 89.9 all-reduce.10
  802.6 89.9 all-reduce.10

commit v5 on v3

--- a/solution.py
+++ b/solution.py
@@ -16,12 +16,13 @@
     return pltpu.roll(grid, 0, 1, stride=1, stride_axis=0).T
 
 
-def group_kernel(origin_ref, nonlinear_ref, left_ref, mid_ref, right_ref, taps_ref, coupling_ref,
+def group_kernel(scalar_ref, nonlinear_ref, left_ref, mid_ref, right_ref, taps_ref, coupling_ref,
                  amplifier_ref, out_ref, *, spans, steps, half_taps, length):
     width = 2 * half_taps
     halo = spans * steps * half_taps
     extent = mid_ref.shape[-1]
-    origin = origin_ref[0]
+    group = scalar_ref[0]
+    origin = scalar_ref[1]
     parts = []
     for part in range(2):
         parts.append(jnp.concatenate(
@@ -35,8 +36,8 @@
             windows = jnp.concatenate(
                 [jnp.concatenate([real[:, b * width:(b + 2) * width], imag[:, b * width:(b + 2) * width]], axis=1)
                  for b in range(blocks)], axis=0)
-            real_band = banded(taps_ref[2 * index], width)
-            imag_band = banded(taps_ref[2 * index + 1], width)
+            real_band = banded(taps_ref[0, 2 * index], width)
+            imag_band = banded(taps_ref[0, 2 * index + 1], width)
             response = jnp.concatenate([
                 jnp.concatenate([real_band, imag_band], axis=1),
                 jnp.concatenate([-imag_band, real_band], axis=1)], axis=0)
@@ -46,8 +47,8 @@
             imag = jnp.concatenate([product[b * ROWS:(b + 1) * ROWS, width:] for b in range(blocks)], axis=1)
             offset = offset + half_taps
             dispersed = jnp.concatenate([real, imag], axis=0)
-            real_coupling = coupling_ref[2 * index]
-            imag_coupling = coupling_ref[2 * index + 1]
+            real_coupling = coupling_ref[0, 2 * index]
+            imag_coupling = coupling_ref[0, 2 * index + 1]
             mixer = jnp.concatenate([
                 jnp.concatenate([real_coupling, -imag_coupling], axis=1),
                 jnp.concatenate([imag_coupling, real_coupling], axis=1)], axis=0)
@@ -57,40 +58,54 @@
             inside = (where >= 0) & (where < length)
             mixed = jnp.where(inside, mixed, 0.0)
             power = jnp.sum(mixed * mixed, axis=0, keepdims=True)
-            phase = nonlinear_ref[index] * power
+            phase = nonlinear_ref[group, index] * power
             cosine = jnp.cos(phase)
             sine = jnp.sin(phase)
             real_mixed = mixed[:ROWS]
             imag_mixed = mixed[ROWS:]
             real = real_mixed * cosine - imag_mixed * sine
             imag = real_mixed * sine + imag_mixed * cosine
-        gain = amplifier_ref[span_index]
+        gain = amplifier_ref[0, span_index]
         real = real * gain
         imag = imag * gain
     out_ref[0] = real
     out_ref[1] = imag
 
 
-def group_pass(signal, taps, coupling, gain, nonlinear_group, origin, length, spans, steps, half_taps):
+def group_pass(signal, group, taps, coupling, gain, nonlinear, origin, length, spans, steps, half_taps):
     halo = spans * steps * half_taps
     count = lax.axis_size("tm")
     forward = [(i, i + 1) for i in range(count - 1)]
     backward = [(i + 1, i) for i in range(count - 1)]
     left = lax.ppermute(signal, "tm", forward)
     right = lax.ppermute(signal, "tm", backward)
-    vmem = pl.BlockSpec(memory_space=pltpu.VMEM)
     smem = pl.BlockSpec(memory_space=pltpu.SMEM)
+
+    def whole(shape):
+        return pl.BlockSpec(shape, lambda i, scalars: (0,) * len(shape))
+
+    def chosen(array):
+        shape = (1,) + array.shape[1:]
+        return pl.BlockSpec(shape, lambda i, scalars: (scalars[0],) + (0,) * (len(shape) - 1))
+
     blocks = (signal.shape[-1] + 2 * halo) // (2 * half_taps)
     flops = 2 * spans * steps * ROWS * (blocks * 4 * half_taps * 4 * half_taps + 4 * ROWS * signal.shape[-1] * 2)
+    grid_spec = pltpu.PrefetchScalarGridSpec(
+        num_scalar_prefetch=1,
+        grid=(1,),
+        in_specs=[smem, whole(signal.shape), whole(signal.shape), whole(signal.shape),
+                  chosen(taps), chosen(coupling), chosen(gain)],
+        out_specs=whole(signal.shape),
+    )
     kernel = pl.pallas_call(
         functools.partial(group_kernel, spans=spans, steps=steps, half_taps=half_taps, length=length),
         out_shape=jax.ShapeDtypeStruct(signal.shape, jnp.float32),
-        in_specs=[smem, smem, vmem, vmem, vmem, vmem, vmem, vmem],
-        out_specs=vmem,
+        grid_spec=grid_spec,
         cost_estimate=pl.CostEstimate(flops=6 * flops, transcendentals=0,
-                                      bytes_accessed=4 * (4 * signal.size + taps.size + coupling.size)),
+                                      bytes_accessed=4 * (4 * signal.size + taps[0].size + coupling[0].size)),
     )
-    return kernel(origin.reshape(1), nonlinear_group, left, signal, right, taps, coupling, gain)
+    scalars = jnp.stack([group, origin]).astype(jnp.int32)
+    return kernel(scalars, nonlinear, left, signal, right, taps, coupling, gain)
 
 
 def shards(launched, coupling, impulse, amplifier, nonlinear):
@@ -125,15 +140,14 @@
     signal = lax.dynamic_slice_in_dim(launched, section_index * per_section, per_section, 0)
     signal = jnp.pad(signal, ((0, 0), (0, 0), (0, grow), (0, 0)))
 
-    def advance(signal, params):
-        taps, coupling_group, gain, nonlinear_group = params
+    def advance(signal, group):
         signal = jnp.stack([
-            group_pass(signal[frame], taps, coupling_group, gain, nonlinear_group, origin, length,
-                       spans, steps, half_taps)
+            group_pass(signal[frame], group, taps_all, coupling_all, gain_all, nonlinear_all, origin,
+                       length, spans, steps, half_taps)
             for frame in range(signal.shape[0])])
         return signal, signal
 
-    _, stacked = lax.scan(advance, signal, (taps_all, coupling_all, gain_all, nonlinear_all))
+    _, stacked = lax.scan(advance, signal, jnp.arange(groups, dtype=jnp.int32))
     stacked = stacked[:, :, :, :channels]
     return lax.all_to_all(stacked, "span", 0, 1, tiled=True)
 

time: 340 us -> 340 us (level)
  local copies, waits for them, and re-layouts: 73.2 us -> 42.1 us
  waiting for transfers between devices: 98.3 us -> 116 us
  other arithmetic: 0.01 us -> 9.43 us
  Pallas kernels: 91.5 us -> 96.6 us
    squeeze x40 -> x0, local copies, waits for them, and re-layouts: 30.6 us -> none  [shards(): lax.scan(advance, signal, (taps_all, coupling_all, gain_all, nonlinear_all))]
    ppermute x8, waiting for transfers between devices: 29 us -> 46.1 us  [group_pass(): left = lax.ppermute(signal, 'tm', forward)]
    another operation x0 -> x8, other arithmetic: none -> 9.42 us  [group_pass(): scalars = jnp.stack([group, origin]).astype(jnp.int32)]
    while x56 -> x41, local copies, waits for them, and re-layouts: 5.87 us -> 0.59 us  [the longest x1 0.36 us: shards(): _, stacked = lax.scan(advance, signal, jnp.arange(groups, dtype=jnp.int32))]
    pallas_call x8, Pallas kernels: 91.5 us -> 96.6 us  [group_pass(): return kernel(scalars, nonlinear, left, signal, right, taps, coupling, gain)]
    dynamic_slice x0 -> x8, local copies, waits for them, and re-layouts: none -> 4.77 us  [shards(): _, stacked = lax.scan(advance, signal, jnp.arange(groups, dtype=jnp.int32))]
  transfers between devices with their start and end apart: 17 -> 17, of which waited for: 9 -> 10; matrix products, arithmetic and copies ran while one was open for 9% -> 4% of each run, Pallas kernels for 0% -> 0%
where the time goes in v5:
time: 340 us; the launch traced here: 339 us
  waiting for transfers between devices  116 us (34%)
  Pallas kernels  96.6 us (28%)
  local copies, waits for them, and re-layouts  42.1 us (12%)
  starting transfers between devices  37 us (11%)
  blocking collectives  23.9 us (7%)
  between operations  13.5 us (4%)
  other arithmetic  9.43 us (3%)
    pallas_call x8, Pallas kernels, group_pass(): return kernel(scalars, nonlinear, left, signal, right, taps, coupling, gain)  96.6 us
    all_gather x1, waiting for transfers between devices, shards(): gathered = lax.all_gather(packed, 'span', axis=0, tiled=True)  69.3 us
    ppermute x8, waiting for transfers between devices, group_pass(): left = lax.ppermute(signal, 'tm', forward)  46.1 us
    all_to_all x1, blocking collectives, shards(): return lax.all_to_all(stacked, 'span', 0, 1, tiled=True)  23.9 us
    ppermute x8, starting transfers between devices, group_pass(): left = lax.ppermute(signal, 'tm', forward)  18.8 us
    ppermute x8, starting transfers between devices, group_pass(): right = lax.ppermute(signal, 'tm', backward)  18.3 us
    unnamed x11, local copies, waits for them, and re-layouts  9.86 us
    another operation x8, other arithmetic, group_pass(): scalars = jnp.stack([group, origin]).astype(jnp.int32)  9.42 us
  transfers between devices with their start and end apart: 17, of which 10 were waited for; matrix products, arithmetic and copies ran while one was open for 4% of the time, Pallas kernels for 0%

profile of v5, /device:TPU:2, one launch (start us, length us, event | category | flops | bytes accessed | tf_op | source)
XLA Modules:
  0.0 338.7 jit_solution(499869795460265213)
XLA Ops:
  10.8 4.1 %dynamic-update-slice = f32[1,98056]{1,0:T(1,128)S(1)} dynamic-update-slice(f32[1,98056]{1,0:T(1,128)S(1)} %custom-call, f32[1,96800]{1,0:T(1,128)S(1)} %reshape.31, s32[]{} %constant.38, s32[]{} %constant.38) | dynamic-update-slice | bytes 774404
  16.7 69.3 %all-gather.3.cloned.1.call-done = f32[8,1,98056]{2,1,0:T(1,128)} async-done(((f32[1,1,98056]{2,1,0:T(1,128)}), f32[8,1,98056]{2,1,0:T(1,128)}) %all-gather.3.cloned.1.call-update) | async-done | bytes 3137808 | tf_op jit(solution)/shard_map/all_gather | solution.py:121
  86.0 2.1 copy.34
  90.5 7.0 %reshape.37 = f32[8,2,2,2,110,110]{5,4,3,2,1,0:T(8,128)} reshape(f32[8,96800]{1,0:T(8,128)} %slice.22) | data formatting | bytes 6195200 | tf_op jit(solution)/shard_map/reshape | solution.py:126
  97.5 4.5 %pad.18 = f32[8,2,2,2,128,128]{5,4,3,2,1,0:T(8,128)} pad(f32[8,2,2,2,110,110]{5,4,3,2,1,0:T(8,128)} %reshape.37, f32[]{:T(128)} %constant.22.clone.1), padding=0_0x0_0x0_0x0_0x0_18x0_18 | pad | bytes 7291908 | tf_op jit(solution)/shard_map/jit(_pad)/pad | solution.py:133
  102.4 202.2 %while.12 = (s32[]{:T(128)}, f32[1,2,128,256]{3,2,1,0:T(8,128)S(1)}, f32[8,1,2,128,256]{4,2,3,1,0:T(2,128)}, s32[8]{0:T(128)S(1)}, s32[]{:T(128)}, /*index=5*/f3...) while((s32[]{:T(128)}, ...), condition=%wide.region_1.2_spmd, body=%wide.region_0.1_spmd.sunk | while | flops 4026531840 | bytes 6824213 | solution.py:150
  102.6 4.8 %collective-permute-start.1 = (f32[2,128,256]{2,1,0:T(8,128)S(1)}, f32[2,128,256]{2,1,0:T(8,128)S(1)}, u32[]{:S(2)}, u32[]{:S(2)}) collective-permute-start(f32[2,128,256]{2,1,0:T(8,128)S(1)} %copy.52.mid_ref), channel_id=1, source_target_pairs={{1,0},{2,1},{3,2},{4,3},{5,4},{6,5},{7,6},{8,7},{9,8},{10,9},{11,1... | collective-permute-start | bytes 786440 | tf_op jit(solution)/shard_map/while/body/eval_jaxpr/ppermute | solution.py:81
  111.4 6.0 %collective-permute-done.left_ref = f32[2,128,256]{2,1,0:T(8,128)} collective-permute-done((f32[2,128,256]{2,1,0:T(8,128)S(1)}, f32[2,128,256]{2,1,0:T(8,128)}, u32[]{:S(2)}, u32[]{:S(2)}) %collective-permute-start) | collective-permute-done | bytes 262176 | tf_op jit(solution)/shard_map/while/body/eval_jaxpr/ppermute | solution.py:80
  117.4 12.1 %eval_jaxpr.1 = f32[2,128,256]{2,1,0:T(8,128)S(1)} custom-call(s32[2]{0:T(128)} %pad_add_fusion.2.scalar_ref, f32[8,4]{1,0:T(8,128)S(1)} %get-tuple-element.178.nonlinear_ref, f32[2,128,256]{2,1,0:T(8,128)} %collective-permute-done.left_ref, f32[2,128,256]{2,1,0:T(8,128)} %copy-done.1, f32[2,128,256]{2,1,0:T(8,128)} %copy-done.3, ...), custom_call_target="tpu_custom_call" | custom-call | flops 4026531840 | bytes 1581056 | tf_op jit(solution)/shard_map/while/body/eval_jaxpr/pallas_call | solution.py:108
  132.3 2.4 collective-permute-start
  136.5 5.7 %collective-permute-done.left_ref = f32[2,128,256]{2,1,0:T(8,128)} collective-permute-done((f32[2,128,256]{2,1,0:T(8,128)S(1)}, f32[2,128,256]{2,1,0:T(8,128)}, u32[]{:S(2)}, u32[]{:S(2)}) %collective-permute-start) | collective-permute-done | bytes 262176 | tf_op jit(solution)/shard_map/while/body/eval_jaxpr/ppermute | solution.py:80
  142.2 12.1 %eval_jaxpr.1 = f32[2,128,256]{2,1,0:T(8,128)S(1)} custom-call(s32[2]{0:T(128)} %pad_add_fusion.2.scalar_ref, f32[8,4]{1,0:T(8,128)S(1)} %get-tuple-element.178.nonlinear_ref, f32[2,128,256]{2,1,0:T(8,128)} %collective-permute-done.left_ref, f32[2,128,256]{2,1,0:T(8,128)} %copy-done.1, f32[2,128,256]{2,1,0:T(8,128)} %copy-done.3, ...), custom_call_target="tpu_custom_call" | custom-call | flops 4026531840 | bytes 1581056 | tf_op jit(solution)/shard_map/while/body/eval_jaxpr/pallas_call | solution.py:108
  157.2 2.4 collective-permute-start
  161.4 5.7 %collective-permute-done.left_ref = f32[2,128,256]{2,1,0:T(8,128)} collective-permute-done((f32[2,128,256]{2,1,0:T(8,128)S(1)}, f32[2,128,256]{2,1,0:T(8,128)}, u32[]{:S(2)}, u32[]{:S(2)}) %collective-permute-start) | collective-permute-done | bytes 262176 | tf_op jit(solution)/shard_map/while/body/eval_jaxpr/ppermute | solution.py:80
  167.1 12.1 %eval_jaxpr.1 = f32[2,128,256]{2,1,0:T(8,128)S(1)} custom-call(s32[2]{0:T(128)} %pad_add_fusion.2.scalar_ref, f32[8,4]{1,0:T(8,128)S(1)} %get-tuple-element.178.nonlinear_ref, f32[2,128,256]{2,1,0:T(8,128)} %collective-permute-done.left_ref, f32[2,128,256]{2,1,0:T(8,128)} %copy-done.1, f32[2,128,256]{2,1,0:T(8,128)} %copy-done.3, ...), custom_call_target="tpu_custom_call" | custom-call | flops 4026531840 | bytes 1581056 | tf_op jit(solution)/shard_map/while/body/eval_jaxpr/pallas_call | solution.py:108
  182.1 2.4 collective-permute-start
  186.3 5.7 %collective-permute-done.left_ref = f32[2,128,256]{2,1,0:T(8,128)} collective-permute-done((f32[2,128,256]{2,1,0:T(8,128)S(1)}, f32[2,128,256]{2,1,0:T(8,128)}, u32[]{:S(2)}, u32[]{:S(2)}) %collective-permute-start) | collective-permute-done | bytes 262176 | tf_op jit(solution)/shard_map/while/body/eval_jaxpr/ppermute | solution.py:80
  192.0 12.1 %eval_jaxpr.1 = f32[2,128,256]{2,1,0:T(8,128)S(1)} custom-call(s32[2]{0:T(128)} %pad_add_fusion.2.scalar_ref, f32[8,4]{1,0:T(8,128)S(1)} %get-tuple-element.178.nonlinear_ref, f32[2,128,256]{2,1,0:T(8,128)} %collective-permute-done.left_ref, f32[2,128,256]{2,1,0:T(8,128)} %copy-done.1, f32[2,128,256]{2,1,0:T(8,128)} %copy-done.3, ...), custom_call_target="tpu_custom_call" | custom-call | flops 4026531840 | bytes 1581056 | tf_op jit(solution)/shard_map/while/body/eval_jaxpr/pallas_call | solution.py:108
  207.0 2.4 collective-permute-start
  211.2 5.7 %collective-permute-done.left_ref = f32[2,128,256]{2,1,0:T(8,128)} collective-permute-done((f32[2,128,256]{2,1,0:T(8,128)S(1)}, f32[2,128,256]{2,1,0:T(8,128)}, u32[]{:S(2)}, u32[]{:S(2)}) %collective-permute-start) | collective-permute-done | bytes 262176 | tf_op jit(solution)/shard_map/while/body/eval_jaxpr/ppermute | solution.py:80
  216.9 12.1 %eval_jaxpr.1 = f32[2,128,256]{2,1,0:T(8,128)S(1)} custom-call(s32[2]{0:T(128)} %pad_add_fusion.2.scalar_ref, f32[8,4]{1,0:T(8,128)S(1)} %get-tuple-element.178.nonlinear_ref, f32[2,128,256]{2,1,0:T(8,128)} %collective-permute-done.left_ref, f32[2,128,256]{2,1,0:T(8,128)} %copy-done.1, f32[2,128,256]{2,1,0:T(8,128)} %copy-done.3, ...), custom_call_target="tpu_custom_call" | custom-call | flops 4026531840 | bytes 1581056 | tf_op jit(solution)/shard_map/while/body/eval_jaxpr/pallas_call | solution.py:108
  231.9 2.4 collective-permute-start
  236.1 5.7 %collective-permute-done.left_ref = f32[2,128,256]{2,1,0:T(8,128)} collective-permute-done((f32[2,128,256]{2,1,0:T(8,128)S(1)}, f32[2,128,256]{2,1,0:T(8,128)}, u32[]{:S(2)}, u32[]{:S(2)}) %collective-permute-start) | collective-permute-done | bytes 262176 | tf_op jit(solution)/shard_map/while/body/eval_jaxpr/ppermute | solution.py:80
  241.8 12.1 %eval_jaxpr.1 = f32[2,128,256]{2,1,0:T(8,128)S(1)} custom-call(s32[2]{0:T(128)} %pad_add_fusion.2.scalar_ref, f32[8,4]{1,0:T(8,128)S(1)} %get-tuple-element.178.nonlinear_ref, f32[2,128,256]{2,1,0:T(8,128)} %collective-permute-done.left_ref, f32[2,128,256]{2,1,0:T(8,128)} %copy-done.1, f32[2,128,256]{2,1,0:T(8,128)} %copy-done.3, ...), custom_call_target="tpu_custom_call" | custom-call | flops 4026531840 | bytes 1581056 | tf_op jit(solution)/shard_map/while/body/eval_jaxpr/pallas_call | solution.py:108
  256.8 2.4 collective-permute-start
  260.9 5.7 %collective-permute-done.left_ref = f32[2,128,256]{2,1,0:T(8,128)} collective-permute-done((f32[2,128,256]{2,1,0:T(8,128)S(1)}, f32[2,128,256]{2,1,0:T(8,128)}, u32[]{:S(2)}, u32[]{:S(2)}) %collective-permute-start) | collective-permute-done | bytes 262176 | tf_op jit(solution)/shard_map/while/body/eval_jaxpr/ppermute | solution.py:80
  266.7 12.1 %eval_jaxpr.1 = f32[2,128,256]{2,1,0:T(8,128)S(1)} custom-call(s32[2]{0:T(128)} %pad_add_fusion.2.scalar_ref, f32[8,4]{1,0:T(8,128)S(1)} %get-tuple-element.178.nonlinear_ref, f32[2,128,256]{2,1,0:T(8,128)} %collective-permute-done.left_ref, f32[2,128,256]{2,1,0:T(8,128)} %copy-done.1, f32[2,128,256]{2,1,0:T(8,128)} %copy-done.3, ...), custom_call_target="tpu_custom_call" | custom-call | flops 4026531840 | bytes 1581056 | tf_op jit(solution)/shard_map/while/body/eval_jaxpr/pallas_call | solution.py:108
  281.6 2.4 collective-permute-start
  285.8 5.8 %collective-permute-done.left_ref = f32[2,128,256]{2,1,0:T(8,128)} collective-permute-done((f32[2,128,256]{2,1,0:T(8,128)S(1)}, f32[2,128,256]{2,1,0:T(8,128)}, u32[]{:S(2)}, u32[]{:S(2)}) %collective-permute-start) | collective-permute-done | bytes 262176 | tf_op jit(solution)/shard_map/while/body/eval_jaxpr/ppermute | solution.py:80
  291.6 12.1 %eval_jaxpr.1 = f32[2,128,256]{2,1,0:T(8,128)S(1)} custom-call(s32[2]{0:T(128)} %pad_add_fusion.2.scalar_ref, f32[8,4]{1,0:T(8,128)S(1)} %get-tuple-element.178.nonlinear_ref, f32[2,128,256]{2,1,0:T(8,128)} %collective-permute-done.left_ref, f32[2,128,256]{2,1,0:T(8,128)} %copy-done.1, f32[2,128,256]{2,1,0:T(8,128)} %copy-done.3, ...), custom_call_target="tpu_custom_call" | custom-call | flops 4026531840 | bytes 1581056 | tf_op jit(solution)/shard_map/while/body/eval_jaxpr/pallas_call | solution.py:108
  304.6 2.1 slice.19
  306.7 23.9 %all_to_all.12 = f32[8,1,2,110,256]{4,2,3,1,0:T(2,128)S(1)} all-to-all(f32[8,1,2,110,256]{4,2,3,1,0:T(2,128)S(1)} %slice.19), channel_id=1, replica_groups=mesh['span'=8,'tm'=32] {'span'}, dimensions={0} | all-to-all | bytes 3604480 | tf_op jit(solution)/shard_map/all_to_all | solution.py:152
  (111 shorter events, 47.3 us)
Async XLA Ops:
  6.5 10.0 %copy-start = (f32[8,2,110,256]{3,1,2,0:T(2,128)S(1)}, f32[8,2,110,256]{3,1,2,0:T(2,128)}, u32[]{:S(2)}) copy-start(f32[8,2,110,256]{3,1,2,0:T(2,128)} %param.7) | copy-start | bytes 5406724
  6.5 79.4 %all-gather.3.cloned.1.call-start = ((), (), s32[]{:S(2)}) async-start(), calls=%async_computation.1 | async-start | bytes 3534336 | tf_op jit(solution)/shard_map/all_gather | solution.py:121
  102.6 14.8 %copy-start.1 = (f32[2,128,256]{2,1,0:T(8,128)}, f32[2,128,256]{2,1,0:T(8,128)S(1)}, u32[]{:S(2)}) copy-start(f32[2,128,256]{2,1,0:T(8,128)S(1)} %copy.52.mid_ref) | copy-start | bytes 786436 | tf_op jit(solution)/shard_map/while
  102.6 8.7 %collective-permute-start.1 = (f32[2,128,256]{2,1,0:T(8,128)S(1)}, f32[2,128,256]{2,1,0:T(8,128)S(1)}, u32[]{:S(2)}, u32[]{:S(2)}) collective-permute-start(f32[2,128,256]{2,1,0:T(8,128)S(1)} %copy.52.mid_ref), channel_id=1, source_target_pairs={{1,0},{2,1},{3,2},{4,3},{5,4},{6,5},{7,6},{8,7},{9,8},{10,9},{11,1... | collective-permute-start | bytes 786440 | tf_op jit(solution)/shard_map/while/body/eval_jaxpr/ppermute | solution.py:81
  107.5 9.9 %collective-permute-start = (f32[2,128,256]{2,1,0:T(8,128)S(1)}, f32[2,128,256]{2,1,0:T(8,128)}, u32[]{:S(2)}, u32[]{:S(2)}) collective-permute-start(f32[2,128,256]{2,1,0:T(8,128)S(1)} %copy.52.mid_ref), channel_id=1, source_target_pairs={{0,1},{1,2},{2,3},{3,4},{4,5},{5,6},{6,7},{7,8},{8,9},{9,10},{10,1... | collective-permute-start | bytes 786440 | tf_op jit(solution)/shard_map/while/body/eval_jaxpr/ppermute | solution.py:80
  111.3 6.0 %copy-start.3 = (f32[2,128,256]{2,1,0:T(8,128)}, f32[2,128,256]{2,1,0:T(8,128)S(1)}, u32[]{:S(2)}) copy-start(f32[2,128,256]{2,1,0:T(8,128)S(1)} %collective-permute-done.1.right_ref) | copy-start | bytes 786436 | tf_op jit(solution)/shard_map/while
  130.4 11.9 %copy-start.1 = (f32[2,128,256]{2,1,0:T(8,128)}, f32[2,128,256]{2,1,0:T(8,128)S(1)}, u32[]{:S(2)}) copy-start(f32[2,128,256]{2,1,0:T(8,128)S(1)} %copy.52.mid_ref) | copy-start | bytes 786436 | tf_op jit(solution)/shard_map/while
  130.4 6.1 %collective-permute-start.1 = (f32[2,128,256]{2,1,0:T(8,128)S(1)}, f32[2,128,256]{2,1,0:T(8,128)S(1)}, u32[]{:S(2)}, u32[]{:S(2)}) collective-permute-start(f32[2,128,256]{2,1,0:T(8,128)S(1)} %copy.52.mid_ref), channel_id=1, source_target_pairs={{1,0},{2,1},{3,2},{4,3},{5,4},{6,5},{7,6},{8,7},{9,8},{10,9},{11,1... | collective-permute-start | bytes 786440 | tf_op jit(solution)/shard_map/while/body/eval_jaxpr/ppermute | solution.py:81
  132.3 9.9 %collective-permute-start = (f32[2,128,256]{2,1,0:T(8,128)S(1)}, f32[2,128,256]{2,1,0:T(8,128)}, u32[]{:S(2)}, u32[]{:S(2)}) collective-permute-start(f32[2,128,256]{2,1,0:T(8,128)S(1)} %copy.52.mid_ref), channel_id=1, source_target_pairs={{0,1},{1,2},{2,3},{3,4},{4,5},{5,6},{6,7},{7,8},{8,9},{9,10},{10,1... | collective-permute-start | bytes 786440 | tf_op jit(solution)/shard_map/while/body/eval_jaxpr/ppermute | solution.py:80
  136.5 5.7 %copy-start.3 = (f32[2,128,256]{2,1,0:T(8,128)}, f32[2,128,256]{2,1,0:T(8,128)S(1)}, u32[]{:S(2)}) copy-start(f32[2,128,256]{2,1,0:T(8,128)S(1)} %collective-permute-done.1.right_ref) | copy-start | bytes 786436 | tf_op jit(solution)/shard_map/while
  155.3 11.9 %copy-start.1 = (f32[2,128,256]{2,1,0:T(8,128)}, f32[2,128,256]{2,1,0:T(8,128)S(1)}, u32[]{:S(2)}) copy-start(f32[2,128,256]{2,1,0:T(8,128)S(1)} %copy.52.mid_ref) | copy-start | bytes 786436 | tf_op jit(solution)/shard_map/while
  155.3 6.1 %collective-permute-start.1 = (f32[2,128,256]{2,1,0:T(8,128)S(1)}, f32[2,128,256]{2,1,0:T(8,128)S(1)}, u32[]{:S(2)}, u32[]{:S(2)}) collective-permute-start(f32[2,128,256]{2,1,0:T(8,128)S(1)} %copy.52.mid_ref), channel_id=1, source_target_pairs={{1,0},{2,1},{3,2},{4,3},{5,4},{6,5},{7,6},{8,7},{9,8},{10,9},{11,1... | collective-permute-start | bytes 786440 | tf_op jit(solution)/shard_map/while/body/eval_jaxpr/ppermute | solution.py:81
  157.2 9.9 %collective-permute-start = (f32[2,128,256]{2,1,0:T(8,128)S(1)}, f32[2,128,256]{2,1,0:T(8,128)}, u32[]{:S(2)}, u32[]{:S(2)}) collective-permute-start(f32[2,128,256]{2,1,0:T(8,128)S(1)} %copy.52.mid_ref), channel_id=1, source_target_pairs={{0,1},{1,2},{2,3},{3,4},{4,5},{5,6},{6,7},{7,8},{8,9},{9,10},{10,1... | collective-permute-start | bytes 786440 | tf_op jit(solution)/shard_map/while/body/eval_jaxpr/ppermute | solution.py:80
  180.2 11.9 %copy-start.1 = (f32[2,128,256]{2,1,0:T(8,128)}, f32[2,128,256]{2,1,0:T(8,128)S(1)}, u32[]{:S(2)}) copy-start(f32[2,128,256]{2,1,0:T(8,128)S(1)} %copy.52.mid_ref) | copy-start | bytes 786436 | tf_op jit(solution)/shard_map/while
  180.2 6.1 %collective-permute-start.1 = (f32[2,128,256]{2,1,0:T(8,128)S(1)}, f32[2,128,256]{2,1,0:T(8,128)S(1)}, u32[]{:S(2)}, u32[]{:S(2)}) collective-permute-start(f32[2,128,256]{2,1,0:T(8,128)S(1)} %copy.52.mid_ref), channel_id=1, source_target_pairs={{1,0},{2,1},{3,2},{4,3},{5,4},{6,5},{7,6},{8,7},{9,8},{10,9},{11,1... | collective-permute-start | bytes 786440 | tf_op jit(solution)/shard_map/while/body/eval_jaxpr/ppermute | solution.py:81
  182.1 9.9 %collective-permute-start = (f32[2,128,256]{2,1,0:T(8,128)S(1)}, f32[2,128,256]{2,1,0:T(8,128)}, u32[]{:S(2)}, u32[]{:S(2)}) collective-permute-start(f32[2,128,256]{2,1,0:T(8,128)S(1)} %copy.52.mid_ref), channel_id=1, source_target_pairs={{0,1},{1,2},{2,3},{3,4},{4,5},{5,6},{6,7},{7,8},{8,9},{9,10},{10,1... | collective-permute-start | bytes 786440 | tf_op jit(solution)/shard_map/while/body/eval_jaxpr/ppermute | solution.py:80
  186.3 5.7 %copy-start.3 = (f32[2,128,256]{2,1,0:T(8,128)}, f32[2,128,256]{2,1,0:T(8,128)S(1)}, u32[]{:S(2)}) copy-start(f32[2,128,256]{2,1,0:T(8,128)S(1)} %collective-permute-done.1.right_ref) | copy-start | bytes 786436 | tf_op jit(solution)/shard_map/while
  205.1 11.9 %copy-start.1 = (f32[2,128,256]{2,1,0:T(8,128)}, f32[2,128,256]{2,1,0:T(8,128)S(1)}, u32[]{:S(2)}) copy-start(f32[2,128,256]{2,1,0:T(8,128)S(1)} %copy.52.mid_ref) | copy-start | bytes 786436 | tf_op jit(solution)/shard_map/while
  205.1 6.1 %collective-permute-start.1 = (f32[2,128,256]{2,1,0:T(8,128)S(1)}, f32[2,128,256]{2,1,0:T(8,128)S(1)}, u32[]{:S(2)}, u32[]{:S(2)}) collective-permute-start(f32[2,128,256]{2,1,0:T(8,128)S(1)} %copy.52.mid_ref), channel_id=1, source_target_pairs={{1,0},{2,1},{3,2},{4,3},{5,4},{6,5},{7,6},{8,7},{9,8},{10,9},{11,1... | collective-permute-start | bytes 786440 | tf_op jit(solution)/shard_map/while/body/eval_jaxpr/ppermute | solution.py:81
  207.0 9.9 %collective-permute-start = (f32[2,128,256]{2,1,0:T(8,128)S(1)}, f32[2,128,256]{2,1,0:T(8,128)}, u32[]{:S(2)}, u32[]{:S(2)}) collective-permute-start(f32[2,128,256]{2,1,0:T(8,128)S(1)} %copy.52.mid_ref), channel_id=1, source_target_pairs={{0,1},{1,2},{2,3},{3,4},{4,5},{5,6},{6,7},{7,8},{8,9},{9,10},{10,1... | collective-permute-start | bytes 786440 | tf_op jit(solution)/shard_map/while/body/eval_jaxpr/ppermute | solution.py:80
  211.2 5.7 %copy-start.3 = (f32[2,128,256]{2,1,0:T(8,128)}, f32[2,128,256]{2,1,0:T(8,128)S(1)}, u32[]{:S(2)}) copy-start(f32[2,128,256]{2,1,0:T(8,128)S(1)} %collective-permute-done.1.right_ref) | copy-start | bytes 786436 | tf_op jit(solution)/shard_map/while
  229.9 11.9 %copy-start.1 = (f32[2,128,256]{2,1,0:T(8,128)}, f32[2,128,256]{2,1,0:T(8,128)S(1)}, u32[]{:S(2)}) copy-start(f32[2,128,256]{2,1,0:T(8,128)S(1)} %copy.52.mid_ref) | copy-start | bytes 786436 | tf_op jit(solution)/shard_map/while
  230.0 6.1 %collective-permute-start.1 = (f32[2,128,256]{2,1,0:T(8,128)S(1)}, f32[2,128,256]{2,1,0:T(8,128)S(1)}, u32[]{:S(2)}, u32[]{:S(2)}) collective-permute-start(f32[2,128,256]{2,1,0:T(8,128)S(1)} %copy.52.mid_ref), channel_id=1, source_target_pairs={{1,0},{2,1},{3,2},{4,3},{5,4},{6,5},{7,6},{8,7},{9,8},{10,9},{11,1... | collective-permute-start | bytes 786440 | tf_op jit(solution)/shard_map/while/body/eval_jaxpr/ppermute | solution.py:81
  231.9 9.9 %collective-permute-start = (f32[2,128,256]{2,1,0:T(8,128)S(1)}, f32[2,128,256]{2,1,0:T(8,128)}, u32[]{:S(2)}, u32[]{:S(2)}) collective-permute-start(f32[2,128,256]{2,1,0:T(8,128)S(1)} %copy.52.mid_ref), channel_id=1, source_target_pairs={{0,1},{1,2},{2,3},{3,4},{4,5},{5,6},{6,7},{7,8},{8,9},{9,10},{10,1... | collective-permute-start | bytes 786440 | tf_op jit(solution)/shard_map/while/body/eval_jaxpr/ppermute | solution.py:80
  236.1 5.7 %copy-start.3 = (f32[2,128,256]{2,1,0:T(8,128)}, f32[2,128,256]{2,1,0:T(8,128)S(1)}, u32[]{:S(2)}) copy-start(f32[2,128,256]{2,1,0:T(8,128)S(1)} %collective-permute-done.1.right_ref) | copy-start | bytes 786436 | tf_op jit(solution)/shard_map/while
  254.8 11.9 %copy-start.1 = (f32[2,128,256]{2,1,0:T(8,128)}, f32[2,128,256]{2,1,0:T(8,128)S(1)}, u32[]{:S(2)}) copy-start(f32[2,128,256]{2,1,0:T(8,128)S(1)} %copy.52.mid_ref) | copy-start | bytes 786436 | tf_op jit(solution)/shard_map/while
  254.8 6.1 %collective-permute-start.1 = (f32[2,128,256]{2,1,0:T(8,128)S(1)}, f32[2,128,256]{2,1,0:T(8,128)S(1)}, u32[]{:S(2)}, u32[]{:S(2)}) collective-permute-start(f32[2,128,256]{2,1,0:T(8,128)S(1)} %copy.52.mid_ref), channel_id=1, source_target_pairs={{1,0},{2,1},{3,2},{4,3},{5,4},{6,5},{7,6},{8,7},{9,8},{10,9},{11,1... | collective-permute-start | bytes 786440 | tf_op jit(solution)/shard_map/while/body/eval_jaxpr/ppermute | solution.py:81
  256.8 9.9 %collective-permute-start = (f32[2,128,256]{2,1,0:T(8,128)S(1)}, f32[2,128,256]{2,1,0:T(8,128)}, u32[]{:S(2)}, u32[]{:S(2)}) collective-permute-start(f32[2,128,256]{2,1,0:T(8,128)S(1)} %copy.52.mid_ref), channel_id=1, source_target_pairs={{0,1},{1,2},{2,3},{3,4},{4,5},{5,6},{6,7},{7,8},{8,9},{9,10},{10,1... | collective-permute-start | bytes 786440 | tf_op jit(solution)/shard_map/while/body/eval_jaxpr/ppermute | solution.py:80
  279.7 12.0 %copy-start.1 = (f32[2,128,256]{2,1,0:T(8,128)}, f32[2,128,256]{2,1,0:T(8,128)S(1)}, u32[]{:S(2)}) copy-start(f32[2,128,256]{2,1,0:T(8,128)S(1)} %copy.52.mid_ref) | copy-start | bytes 786436 | tf_op jit(solution)/shard_map/while
  279.7 6.1 %collective-permute-start.1 = (f32[2,128,256]{2,1,0:T(8,128)S(1)}, f32[2,128,256]{2,1,0:T(8,128)S(1)}, u32[]{:S(2)}, u32[]{:S(2)}) collective-permute-start(f32[2,128,256]{2,1,0:T(8,128)S(1)} %copy.52.mid_ref), channel_id=1, source_target_pairs={{1,0},{2,1},{3,2},{4,3},{5,4},{6,5},{7,6},{8,7},{9,8},{10,9},{11,1... | collective-permute-start | bytes 786440 | tf_op jit(solution)/shard_map/while/body/eval_jaxpr/ppermute | solution.py:81
  281.6 10.0 %collective-permute-start = (f32[2,128,256]{2,1,0:T(8,128)S(1)}, f32[2,128,256]{2,1,0:T(8,128)}, u32[]{:S(2)}, u32[]{:S(2)}) collective-permute-start(f32[2,128,256]{2,1,0:T(8,128)S(1)} %copy.52.mid_ref), channel_id=1, source_target_pairs={{0,1},{1,2},{2,3},{3,4},{4,5},{5,6},{6,7},{7,8},{8,9},{9,10},{10,1... | collective-permute-start | bytes 786440 | tf_op jit(solution)/shard_map/while/body/eval_jaxpr/ppermute | solution.py:80
  285.8 5.8 %copy-start.3 = (f32[2,128,256]{2,1,0:T(8,128)}, f32[2,128,256]{2,1,0:T(8,128)S(1)}, u32[]{:S(2)}) copy-start(f32[2,128,256]{2,1,0:T(8,128)S(1)} %collective-permute-done.1.right_ref) | copy-start | bytes 786436 | tf_op jit(solution)/shard_map/while
  (3 other events, 12.2 us)
Sparse Core Ops, SparseCore 0:
  16.7 69.2 all-gather.2

commit v6 on v5

--- a/solution.py
+++ b/solution.py
@@ -72,13 +72,16 @@
     out_ref[1] = imag
 
 
-def group_pass(signal, group, taps, coupling, gain, nonlinear, origin, length, spans, steps, half_taps):
-    halo = spans * steps * half_taps
+def exchanged(signal):
     count = lax.axis_size("tm")
     forward = [(i, i + 1) for i in range(count - 1)]
     backward = [(i + 1, i) for i in range(count - 1)]
-    left = lax.ppermute(signal, "tm", forward)
-    right = lax.ppermute(signal, "tm", backward)
+    return lax.ppermute(signal, "tm", forward), lax.ppermute(signal, "tm", backward)
+
+
+def group_pass(signal, left, right, group, taps, coupling, gain, nonlinear, origin, length, spans,
+               steps, half_taps):
+    halo = spans * steps * half_taps
     smem = pl.BlockSpec(memory_space=pltpu.SMEM)
 
     def whole(shape):
@@ -140,14 +143,24 @@
     signal = lax.dynamic_slice_in_dim(launched, section_index * per_section, per_section, 0)
     signal = jnp.pad(signal, ((0, 0), (0, 0), (0, grow), (0, 0)))
 
-    def advance(signal, group):
-        signal = jnp.stack([
-            group_pass(signal[frame], group, taps_all, coupling_all, gain_all, nonlinear_all, origin,
-                       length, spans, steps, half_taps)
-            for frame in range(signal.shape[0])])
-        return signal, signal
+    def passed(signal, left, right, group):
+        return group_pass(signal, left, right, group, taps_all, coupling_all, gain_all, nonlinear_all,
+                          origin, length, spans, steps, half_taps)
 
-    _, stacked = lax.scan(advance, signal, jnp.arange(groups, dtype=jnp.int32))
+    signal = signal[0]
+    assert per_section == 1
+    left, right = exchanged(signal)
+
+    def advance(carry, group):
+        signal, left, right = carry
+        signal = passed(signal, left, right, group)
+        left, right = exchanged(signal)
+        return (signal, left, right), signal
+
+    (signal, left, right), stacked = lax.scan(
+        advance, (signal, left, right), jnp.arange(groups - 1, dtype=jnp.int32))
+    last = passed(signal, left, right, jnp.int32(groups - 1))
+    stacked = jnp.concatenate([stacked, last[None]], axis=0)[:, None]
     stacked = stacked[:, :, :, :channels]
     return lax.all_to_all(stacked, "span", 0, 1, tiled=True)
 

time: 340 us -> 342 us (level)
  waiting for transfers between devices: 116 us -> 94.2 us
  local copies, waits for them, and re-layouts: 42.1 us -> 53.2 us
  starting transfers between devices: 37 us -> 41.7 us
  Pallas kernels: 96.6 us -> 101 us
    ppermute x16, waiting for transfers between devices: 46.3 us -> 34.6 us  [the longest x8 34.6 us: exchanged(): lax.ppermute(signal, 'tm', forward)]
    all_gather x1, waiting for transfers between devices: 69.3 us -> 59.6 us  [shards(): gathered = lax.all_gather(packed, 'span', axis=0, tiled=True)]
    while x41 -> x8, local copies, waits for them, and re-layouts: 0.59 us -> 7.04 us  [the longest x1 0.36 us: shards(): _, stacked = lax.scan(advance, signal, jnp.arange(groups, dtype=jnp.int32))]
    dynamic_update_slice x8 -> x7, local copies, waits for them, and re-layouts: 7.38 us -> 13.1 us  [shards(): lax.scan(advance, (signal, left, right), jnp.arange(groups - 1, dtype=jnp...]
    ppermute x16, starting transfers between devices: 37 us -> 41.7 us  [the longest x8 23.4 us: exchanged(): lax.ppermute(signal, 'tm', backward)]
    pallas_call x8, Pallas kernels: 96.6 us -> 101 us  [group_pass(): return kernel(scalars, nonlinear, left, signal, right, taps, coupling, gain)]
    reshape x3 -> x4, local copies, waits for them, and re-layouts: 7.25 us -> 7.25 us  [shards(): gathered[:, start:start + size].reshape((-1,) + piece.shape[1:])]
  transfers between devices with their start and end apart: 17 -> 17, of which waited for: 10 -> 8; matrix products, arithmetic and copies ran while one was open for 4% -> 11% of each run, Pallas kernels for 0% -> 0%
where the time goes in v6:
time: 342 us; the launch traced here: 340 us
  Pallas kernels  101 us (30%)
  waiting for transfers between devices  94.2 us (28%)
  local copies, waits for them, and re-layouts  53.2 us (16%)
  starting transfers between devices  41.7 us (12%)
  blocking collectives  24.1 us (7%)
  between operations  13.6 us (4%)
  other arithmetic  11.7 us (3%)
    pallas_call x8, Pallas kernels, group_pass(): return kernel(scalars, nonlinear, left, signal, right, taps, coupling, gain)  101 us
    all_gather x1, waiting for transfers between devices, shards(): gathered = lax.all_gather(packed, 'span', axis=0, tiled=True)  59.6 us
    ppermute x8, waiting for transfers between devices, exchanged(): lax.ppermute(signal, 'tm', forward)  34.6 us
    all_to_all x1, blocking collectives, shards(): return lax.all_to_all(stacked, 'span', 0, 1, tiled=True)  24.1 us
    ppermute x8, starting transfers between devices, exchanged(): lax.ppermute(signal, 'tm', backward)  23.4 us
    ppermute x8, starting transfers between devices, exchanged(): lax.ppermute(signal, 'tm', forward)  18.3 us
    dynamic_update_slice x7, local copies, waits for them, and re-layouts, shards(): lax.scan(advance, (signal, left, right), jnp.arange(groups - 1, dtype=jnp...  13.1 us
    unnamed x11, local copies, waits for them, and re-layouts  9.86 us
  transfers between devices with their start and end apart: 17, of which 8 were waited for; matrix products, arithmetic and copies ran while one was open for 11% of the time, Pallas kernels for 0%

profile of v6, /device:TPU:2, one launch (start us, length us, event | category | flops | bytes accessed | tf_op | source)
XLA Modules:
  0.0 339.9 jit_solution(4456838958622232173)
XLA Ops:
  10.8 4.1 %dynamic-update-slice = f32[1,98056]{1,0:T(1,128)S(1)} dynamic-update-slice(f32[1,98056]{1,0:T(1,128)S(1)} %custom-call, f32[1,96800]{1,0:T(1,128)S(1)} %reshape.30, s32[]{} %constant.42, s32[]{} %constant.42) | dynamic-update-slice | bytes 774404
  16.6 7.2 %collective-permute-start.3 = (f32[2,128,256]{2,1,0:T(8,128)S(1)}, f32[2,128,256]{2,1,0:T(8,128)S(1)}, u32[]{:S(2)}, u32[]{:S(2)}) collective-permute-start(f32[2,128,256]{2,1,0:T(8,128)S(1)} %pad_bitcast_fusion), channel_id=1, source_target_pairs={{1,0},{2,1},{3,2},{4,3},{5,4},{6,5},{7,6},{8,7},{9,8},{10,9},{11,1... | collective-permute-start | bytes 786440 | tf_op jit(solution)/shard_map/ppermute | solution.py:79
  26.4 59.6 %all-gather.3.cloned.1.call-done = f32[8,1,98056]{2,1,0:T(1,128)} async-done(((f32[1,1,98056]{2,1,0:T(1,128)}), f32[8,1,98056]{2,1,0:T(1,128)}) %all-gather.3.cloned.1.call-update) | async-done | bytes 3137808 | tf_op jit(solution)/shard_map/all_gather | solution.py:124
  86.0 2.1 copy.33
  90.5 7.0 %reshape.36 = f32[8,2,2,2,110,110]{5,4,3,2,1,0:T(8,128)} reshape(f32[8,96800]{1,0:T(8,128)} %slice.22) | data formatting | bytes 6195200 | tf_op jit(solution)/shard_map/reshape | solution.py:129
  97.5 4.5 %pad.18 = f32[8,2,2,2,128,128]{5,4,3,2,1,0:T(8,128)} pad(f32[8,2,2,2,110,110]{5,4,3,2,1,0:T(8,128)} %reshape.36, f32[]{:T(128)} %constant.23.clone.1), padding=0_0x0_0x0_0x0_0x0_18x0_18 | pad | bytes 7291908 | tf_op jit(solution)/shard_map/jit(_pad)/pad | solution.py:136
  102.4 188.4 %while.16 = (s32[]{:T(128)}, f32[2,128,256]{2,1,0:T(8,128)S(1)}, f32[2,128,256]{2,1,0:T(8,128)}, f32[2,128,256]{2,1,0:T(8,128)S(1)}, f32[7,2,128,256]{3,1,2,0:T(...) while((s32[]{:T(128)}, f32[2,128,256]{2,1,0:T(8,128)S(1)}, ...), condition=%wide.region_1.2_spmd, body=%wide.region_0.1_spmd.sunk | while | flops 4026531840 | bytes 4727021 | solution.py:160
  104.4 12.6 %eval_jaxpr.1 = f32[2,128,256]{2,1,0:T(8,128)} custom-call(s32[2]{0:T(128)} %pad_add_fusion.3.scalar_ref, f32[8,4]{1,0:T(8,128)S(1)} %get-tuple-element.211.nonlinear_ref, f32[2,128,256]{2,1,0:T(8,128)} %get-tuple-element.194.left_ref, f32[2,128,256]{2,1,0:T(8,128)S(1)} %get-tuple-element.193.mid_ref, f32[2,128,256]{2,1,0:T(8,128)S(1)} %get-tuple-element.195.right_ref, ...), custom_call_target="tpu_custom_call" | custom-call | flops 4026531840 | bytes 1581056 | tf_op jit(solution)/shard_map/while/body/eval_jaxpr/pallas_call | solution.py:111
  117.1 4.8 %collective-permute-start.1 = (f32[2,128,256]{2,1,0:T(8,128)}, f32[2,128,256]{2,1,0:T(8,128)S(1)}, u32[]{:S(2)}, u32[]{:S(2)}) collective-permute-start(f32[2,128,256]{2,1,0:T(8,128)} %eval_jaxpr.1), channel_id=1, source_target_pairs={{1,0},{2,1},{3,2},{4,3},{5,4},{6,5},{7,6},{8,7},{9,8},{10,9},{11,1... | collective-permute-start | bytes 786440 | tf_op jit(solution)/shard_map/while/body/eval_jaxpr/ppermute | solution.py:79
  121.9 1.9 collective-permute-start
  126.6 5.4 %collective-permute-done = f32[2,128,256]{2,1,0:T(8,128)} collective-permute-done((f32[2,128,256]{2,1,0:T(8,128)}, f32[2,128,256]{2,1,0:T(8,128)}, u32[]{:S(2)}, u32[]{:S(2)}) %collective-permute-start) | collective-permute-done | bytes 262176 | tf_op jit(solution)/shard_map/while/body/eval_jaxpr/ppermute | solution.py:79
  133.8 12.6 %eval_jaxpr.1 = f32[2,128,256]{2,1,0:T(8,128)} custom-call(s32[2]{0:T(128)} %pad_add_fusion.3.scalar_ref, f32[8,4]{1,0:T(8,128)S(1)} %get-tuple-element.211.nonlinear_ref, f32[2,128,256]{2,1,0:T(8,128)} %get-tuple-element.194.left_ref, f32[2,128,256]{2,1,0:T(8,128)S(1)} %get-tuple-element.193.mid_ref, f32[2,128,256]{2,1,0:T(8,128)S(1)} %get-tuple-element.195.right_ref, ...), custom_call_target="tpu_custom_call" | custom-call | flops 4026531840 | bytes 1581056 | tf_op jit(solution)/shard_map/while/body/eval_jaxpr/pallas_call | solution.py:111
  148.4 2.4 collective-permute-start
  153.6 4.8 %collective-permute-done = f32[2,128,256]{2,1,0:T(8,128)} collective-permute-done((f32[2,128,256]{2,1,0:T(8,128)}, f32[2,128,256]{2,1,0:T(8,128)}, u32[]{:S(2)}, u32[]{:S(2)}) %collective-permute-start) | collective-permute-done | bytes 262176 | tf_op jit(solution)/shard_map/while/body/eval_jaxpr/ppermute | solution.py:79
  160.3 12.6 %eval_jaxpr.1 = f32[2,128,256]{2,1,0:T(8,128)} custom-call(s32[2]{0:T(128)} %pad_add_fusion.3.scalar_ref, f32[8,4]{1,0:T(8,128)S(1)} %get-tuple-element.211.nonlinear_ref, f32[2,128,256]{2,1,0:T(8,128)} %get-tuple-element.194.left_ref, f32[2,128,256]{2,1,0:T(8,128)S(1)} %get-tuple-element.193.mid_ref, f32[2,128,256]{2,1,0:T(8,128)S(1)} %get-tuple-element.195.right_ref, ...), custom_call_target="tpu_custom_call" | custom-call | flops 4026531840 | bytes 1581056 | tf_op jit(solution)/shard_map/while/body/eval_jaxpr/pallas_call | solution.py:111
  174.8 2.4 collective-permute-start
  180.1 4.9 %collective-permute-done = f32[2,128,256]{2,1,0:T(8,128)} collective-permute-done((f32[2,128,256]{2,1,0:T(8,128)}, f32[2,128,256]{2,1,0:T(8,128)}, u32[]{:S(2)}, u32[]{:S(2)}) %collective-permute-start) | collective-permute-done | bytes 262176 | tf_op jit(solution)/shard_map/while/body/eval_jaxpr/ppermute | solution.py:79
  186.7 12.6 %eval_jaxpr.1 = f32[2,128,256]{2,1,0:T(8,128)} custom-call(s32[2]{0:T(128)} %pad_add_fusion.3.scalar_ref, f32[8,4]{1,0:T(8,128)S(1)} %get-tuple-element.211.nonlinear_ref, f32[2,128,256]{2,1,0:T(8,128)} %get-tuple-element.194.left_ref, f32[2,128,256]{2,1,0:T(8,128)S(1)} %get-tuple-element.193.mid_ref, f32[2,128,256]{2,1,0:T(8,128)S(1)} %get-tuple-element.195.right_ref, ...), custom_call_target="tpu_custom_call" | custom-call | flops 4026531840 | bytes 1581056 | tf_op jit(solution)/shard_map/while/body/eval_jaxpr/pallas_call | solution.py:111
  201.3 2.4 collective-permute-start
  206.5 4.9 %collective-permute-done = f32[2,128,256]{2,1,0:T(8,128)} collective-permute-done((f32[2,128,256]{2,1,0:T(8,128)}, f32[2,128,256]{2,1,0:T(8,128)}, u32[]{:S(2)}, u32[]{:S(2)}) %collective-permute-start) | collective-permute-done | bytes 262176 | tf_op jit(solution)/shard_map/while/body/eval_jaxpr/ppermute | solution.py:79
  213.2 12.6 %eval_jaxpr.1 = f32[2,128,256]{2,1,0:T(8,128)} custom-call(s32[2]{0:T(128)} %pad_add_fusion.3.scalar_ref, f32[8,4]{1,0:T(8,128)S(1)} %get-tuple-element.211.nonlinear_ref, f32[2,128,256]{2,1,0:T(8,128)} %get-tuple-element.194.left_ref, f32[2,128,256]{2,1,0:T(8,128)S(1)} %get-tuple-element.193.mid_ref, f32[2,128,256]{2,1,0:T(8,128)S(1)} %get-tuple-element.195.right_ref, ...), custom_call_target="tpu_custom_call" | custom-call | flops 4026531840 | bytes 1581056 | tf_op jit(solution)/shard_map/while/body/eval_jaxpr/pallas_call | solution.py:111
  227.8 2.4 collective-permute-start
  233.0 4.9 %collective-permute-done = f32[2,128,256]{2,1,0:T(8,128)} collective-permute-done((f32[2,128,256]{2,1,0:T(8,128)}, f32[2,128,256]{2,1,0:T(8,128)}, u32[]{:S(2)}, u32[]{:S(2)}) %collective-permute-start) | collective-permute-done | bytes 262176 | tf_op jit(solution)/shard_map/while/body/eval_jaxpr/ppermute | solution.py:79
  239.7 12.6 %eval_jaxpr.1 = f32[2,128,256]{2,1,0:T(8,128)} custom-call(s32[2]{0:T(128)} %pad_add_fusion.3.scalar_ref, f32[8,4]{1,0:T(8,128)S(1)} %get-tuple-element.211.nonlinear_ref, f32[2,128,256]{2,1,0:T(8,128)} %get-tuple-element.194.left_ref, f32[2,128,256]{2,1,0:T(8,128)S(1)} %get-tuple-element.193.mid_ref, f32[2,128,256]{2,1,0:T(8,128)S(1)} %get-tuple-element.195.right_ref, ...), custom_call_target="tpu_custom_call" | custom-call | flops 4026531840 | bytes 1581056 | tf_op jit(solution)/shard_map/while/body/eval_jaxpr/pallas_call | solution.py:111
  254.2 2.4 collective-permute-start
  259.5 4.9 %collective-permute-done = f32[2,128,256]{2,1,0:T(8,128)} collective-permute-done((f32[2,128,256]{2,1,0:T(8,128)}, f32[2,128,256]{2,1,0:T(8,128)}, u32[]{:S(2)}, u32[]{:S(2)}) %collective-permute-start) | collective-permute-done | bytes 262176 | tf_op jit(solution)/shard_map/while/body/eval_jaxpr/ppermute | solution.py:79
  266.1 12.6 %eval_jaxpr.1 = f32[2,128,256]{2,1,0:T(8,128)} custom-call(s32[2]{0:T(128)} %pad_add_fusion.3.scalar_ref, f32[8,4]{1,0:T(8,128)S(1)} %get-tuple-element.211.nonlinear_ref, f32[2,128,256]{2,1,0:T(8,128)} %get-tuple-element.194.left_ref, f32[2,128,256]{2,1,0:T(8,128)S(1)} %get-tuple-element.193.mid_ref, f32[2,128,256]{2,1,0:T(8,128)S(1)} %get-tuple-element.195.right_ref, ...), custom_call_target="tpu_custom_call" | custom-call | flops 4026531840 | bytes 1581056 | tf_op jit(solution)/shard_map/while/body/eval_jaxpr/pallas_call | solution.py:111
  280.7 2.4 collective-permute-start
  285.9 4.9 %collective-permute-done = f32[2,128,256]{2,1,0:T(8,128)} collective-permute-done((f32[2,128,256]{2,1,0:T(8,128)}, f32[2,128,256]{2,1,0:T(8,128)}, u32[]{:S(2)}, u32[]{:S(2)}) %collective-permute-start) | collective-permute-done | bytes 262176 | tf_op jit(solution)/shard_map/while/body/eval_jaxpr/ppermute | solution.py:79
  290.8 12.6 %shard_map.55 = f32[2,128,256]{2,1,0:T(8,128)} custom-call(s32[2]{0:T(128)} %pad_add_fusion.1.scalar_ref, f32[8,4]{1,0:T(8,128)S(1)} %get-tuple-element.227, f32[2,128,256]{2,1,0:T(8,128)} %get-tuple-element.66.left_ref, f32[2,128,256]{2,1,0:T(8,128)S(1)} %get-tuple-element.67.mid_ref, f32[2,128,256]{2,1,0:T(8,128)S(1)} %get-tuple-element.68.right_ref, ...), custom_call_target="tpu_custom_call" | custom-call | flops 4026531840 | bytes 1581056 | tf_op jit(solution)/shard_map/pallas_call | solution.py:111
  304.6 2.6 maximum_bitcast_fusion
  307.8 24.1 %all_to_all.12 = f32[8,1,2,110,256]{4,2,3,1,0:T(2,128)S(1)} all-to-all(f32[8,1,2,110,256]{4,2,3,1,0:T(2,128)S(1)} %slice.24), channel_id=1, replica_groups=mesh['span'=8,'tm'=32] {'span'}, dimensions={0} | all-to-all | bytes 3604480 | tf_op jit(solution)/shard_map/all_to_all | solution.py:165
  (79 shorter events, 58.1 us)
Async XLA Ops:
  6.5 10.0 %copy-start = (f32[8,2,110,256]{3,1,2,0:T(2,128)S(1)}, f32[8,2,110,256]{3,1,2,0:T(2,128)}, u32[]{:S(2)}) copy-start(f32[8,2,110,256]{3,1,2,0:T(2,128)} %param.7) | copy-start | bytes 5406724
  6.5 79.4 %all-gather.3.cloned.1.call-start = ((), (), s32[]{:S(2)}) async-start(), calls=%async_computation.1 | async-start | bytes 3534336 | tf_op jit(solution)/shard_map/all_gather | solution.py:124
  15.8 0.8 copy-start.1
  16.6 85.8 %collective-permute-start.3 = (f32[2,128,256]{2,1,0:T(8,128)S(1)}, f32[2,128,256]{2,1,0:T(8,128)S(1)}, u32[]{:S(2)}, u32[]{:S(2)}) collective-permute-start(f32[2,128,256]{2,1,0:T(8,128)S(1)} %pad_bitcast_fusion), channel_id=1, source_target_pairs={{1,0},{2,1},{3,2},{4,3},{5,4},{6,5},{7,6},{8,7},{9,8},{10,9},{11,1... | collective-permute-start | bytes 786440 | tf_op jit(solution)/shard_map/ppermute | solution.py:79
  23.8 78.6 %collective-permute-start.2 = (f32[2,128,256]{2,1,0:T(8,128)S(1)}, f32[2,128,256]{2,1,0:T(8,128)}, u32[]{:S(2)}, u32[]{:S(2)}) collective-permute-start(f32[2,128,256]{2,1,0:T(8,128)S(1)} %pad_bitcast_fusion), channel_id=1, source_target_pairs={{0,1},{1,2},{2,3},{3,4},{4,5},{5,6},{6,7},{7,8},{8,9},{9,10},{10,1... | collective-permute-start | bytes 786440 | tf_op jit(solution)/shard_map/ppermute | solution.py:79
  117.1 9.6 %collective-permute-start.1 = (f32[2,128,256]{2,1,0:T(8,128)}, f32[2,128,256]{2,1,0:T(8,128)S(1)}, u32[]{:S(2)}, u32[]{:S(2)}) collective-permute-start(f32[2,128,256]{2,1,0:T(8,128)} %eval_jaxpr.1), channel_id=1, source_target_pairs={{1,0},{2,1},{3,2},{4,3},{5,4},{6,5},{7,6},{8,7},{9,8},{10,9},{11,1... | collective-permute-start | bytes 786440 | tf_op jit(solution)/shard_map/while/body/eval_jaxpr/ppermute | solution.py:79
  121.9 10.1 %collective-permute-start = (f32[2,128,256]{2,1,0:T(8,128)}, f32[2,128,256]{2,1,0:T(8,128)}, u32[]{:S(2)}, u32[]{:S(2)}) collective-permute-start(f32[2,128,256]{2,1,0:T(8,128)} %eval_jaxpr.1), channel_id=1, source_target_pairs={{0,1},{1,2},{2,3},{3,4},{4,5},{5,6},{6,7},{7,8},{8,9},{9,10},{10,1... | collective-permute-start | bytes 786440 | tf_op jit(solution)/shard_map/while/body/eval_jaxpr/ppermute | solution.py:79
  146.4 7.2 %collective-permute-start.1 = (f32[2,128,256]{2,1,0:T(8,128)}, f32[2,128,256]{2,1,0:T(8,128)S(1)}, u32[]{:S(2)}, u32[]{:S(2)}) collective-permute-start(f32[2,128,256]{2,1,0:T(8,128)} %eval_jaxpr.1), channel_id=1, source_target_pairs={{1,0},{2,1},{3,2},{4,3},{5,4},{6,5},{7,6},{8,7},{9,8},{10,9},{11,1... | collective-permute-start | bytes 786440 | tf_op jit(solution)/shard_map/while/body/eval_jaxpr/ppermute | solution.py:79
  148.4 10.1 %collective-permute-start = (f32[2,128,256]{2,1,0:T(8,128)}, f32[2,128,256]{2,1,0:T(8,128)}, u32[]{:S(2)}, u32[]{:S(2)}) collective-permute-start(f32[2,128,256]{2,1,0:T(8,128)} %eval_jaxpr.1), channel_id=1, source_target_pairs={{0,1},{1,2},{2,3},{3,4},{4,5},{5,6},{6,7},{7,8},{8,9},{9,10},{10,1... | collective-permute-start | bytes 786440 | tf_op jit(solution)/shard_map/while/body/eval_jaxpr/ppermute | solution.py:79
  172.9 7.2 %collective-permute-start.1 = (f32[2,128,256]{2,1,0:T(8,128)}, f32[2,128,256]{2,1,0:T(8,128)S(1)}, u32[]{:S(2)}, u32[]{:S(2)}) collective-permute-start(f32[2,128,256]{2,1,0:T(8,128)} %eval_jaxpr.1), channel_id=1, source_target_pairs={{1,0},{2,1},{3,2},{4,3},{5,4},{6,5},{7,6},{8,7},{9,8},{10,9},{11,1... | collective-permute-start | bytes 786440 | tf_op jit(solution)/shard_map/while/body/eval_jaxpr/ppermute | solution.py:79
  174.8 10.1 %collective-permute-start = (f32[2,128,256]{2,1,0:T(8,128)}, f32[2,128,256]{2,1,0:T(8,128)}, u32[]{:S(2)}, u32[]{:S(2)}) collective-permute-start(f32[2,128,256]{2,1,0:T(8,128)} %eval_jaxpr.1), channel_id=1, source_target_pairs={{0,1},{1,2},{2,3},{3,4},{4,5},{5,6},{6,7},{7,8},{8,9},{9,10},{10,1... | collective-permute-start | bytes 786440 | tf_op jit(solution)/shard_map/while/body/eval_jaxpr/ppermute | solution.py:79
  199.4 7.2 %collective-permute-start.1 = (f32[2,128,256]{2,1,0:T(8,128)}, f32[2,128,256]{2,1,0:T(8,128)S(1)}, u32[]{:S(2)}, u32[]{:S(2)}) collective-permute-start(f32[2,128,256]{2,1,0:T(8,128)} %eval_jaxpr.1), channel_id=1, source_target_pairs={{1,0},{2,1},{3,2},{4,3},{5,4},{6,5},{7,6},{8,7},{9,8},{10,9},{11,1... | collective-permute-start | bytes 786440 | tf_op jit(solution)/shard_map/while/body/eval_jaxpr/ppermute | solution.py:79
  201.3 10.1 %collective-permute-start = (f32[2,128,256]{2,1,0:T(8,128)}, f32[2,128,256]{2,1,0:T(8,128)}, u32[]{:S(2)}, u32[]{:S(2)}) collective-permute-start(f32[2,128,256]{2,1,0:T(8,128)} %eval_jaxpr.1), channel_id=1, source_target_pairs={{0,1},{1,2},{2,3},{3,4},{4,5},{5,6},{6,7},{7,8},{8,9},{9,10},{10,1... | collective-permute-start | bytes 786440 | tf_op jit(solution)/shard_map/while/body/eval_jaxpr/ppermute | solution.py:79
  225.8 7.2 %collective-permute-start.1 = (f32[2,128,256]{2,1,0:T(8,128)}, f32[2,128,256]{2,1,0:T(8,128)S(1)}, u32[]{:S(2)}, u32[]{:S(2)}) collective-permute-start(f32[2,128,256]{2,1,0:T(8,128)} %eval_jaxpr.1), channel_id=1, source_target_pairs={{1,0},{2,1},{3,2},{4,3},{5,4},{6,5},{7,6},{8,7},{9,8},{10,9},{11,1... | collective-permute-start | bytes 786440 | tf_op jit(solution)/shard_map/while/body/eval_jaxpr/ppermute | solution.py:79
  227.8 10.1 %collective-permute-start = (f32[2,128,256]{2,1,0:T(8,128)}, f32[2,128,256]{2,1,0:T(8,128)}, u32[]{:S(2)}, u32[]{:S(2)}) collective-permute-start(f32[2,128,256]{2,1,0:T(8,128)} %eval_jaxpr.1), channel_id=1, source_target_pairs={{0,1},{1,2},{2,3},{3,4},{4,5},{5,6},{6,7},{7,8},{8,9},{9,10},{10,1... | collective-permute-start | bytes 786440 | tf_op jit(solution)/shard_map/while/body/eval_jaxpr/ppermute | solution.py:79
  252.3 7.1 %collective-permute-start.1 = (f32[2,128,256]{2,1,0:T(8,128)}, f32[2,128,256]{2,1,0:T(8,128)S(1)}, u32[]{:S(2)}, u32[]{:S(2)}) collective-permute-start(f32[2,128,256]{2,1,0:T(8,128)} %eval_jaxpr.1), channel_id=1, source_target_pairs={{1,0},{2,1},{3,2},{4,3},{5,4},{6,5},{7,6},{8,7},{9,8},{10,9},{11,1... | collective-permute-start | bytes 786440 | tf_op jit(solution)/shard_map/while/body/eval_jaxpr/ppermute | solution.py:79
  254.2 10.1 %collective-permute-start = (f32[2,128,256]{2,1,0:T(8,128)}, f32[2,128,256]{2,1,0:T(8,128)}, u32[]{:S(2)}, u32[]{:S(2)}) collective-permute-start(f32[2,128,256]{2,1,0:T(8,128)} %eval_jaxpr.1), channel_id=1, source_target_pairs={{0,1},{1,2},{2,3},{3,4},{4,5},{5,6},{6,7},{7,8},{8,9},{9,10},{10,1... | collective-permute-start | bytes 786440 | tf_op jit(solution)/shard_map/while/body/eval_jaxpr/ppermute | solution.py:79
  278.8 7.1 %collective-permute-start.1 = (f32[2,128,256]{2,1,0:T(8,128)}, f32[2,128,256]{2,1,0:T(8,128)S(1)}, u32[]{:S(2)}, u32[]{:S(2)}) collective-permute-start(f32[2,128,256]{2,1,0:T(8,128)} %eval_jaxpr.1), channel_id=1, source_target_pairs={{1,0},{2,1},{3,2},{4,3},{5,4},{6,5},{7,6},{8,7},{9,8},{10,9},{11,1... | collective-permute-start | bytes 786440 | tf_op jit(solution)/shard_map/while/body/eval_jaxpr/ppermute | solution.py:79
  280.7 10.1 %collective-permute-start = (f32[2,128,256]{2,1,0:T(8,128)}, f32[2,128,256]{2,1,0:T(8,128)}, u32[]{:S(2)}, u32[]{:S(2)}) collective-permute-start(f32[2,128,256]{2,1,0:T(8,128)} %eval_jaxpr.1), channel_id=1, source_target_pairs={{0,1},{1,2},{2,3},{3,4},{4,5},{5,6},{6,7},{7,8},{8,9},{9,10},{10,1... | collective-permute-start | bytes 786440 | tf_op jit(solution)/shard_map/while/body/eval_jaxpr/ppermute | solution.py:79
Sparse Core Ops, SparseCore 0:
  16.7 69.2 all-gather.2

commit v7 on v5

--- a/solution.py
+++ b/solution.py
@@ -118,7 +118,13 @@
 
     pieces = (coupling, impulse, amplifier, nonlinear)
     packed = jnp.concatenate([piece.reshape(piece.shape[0], -1) for piece in pieces], axis=1)
-    gathered = lax.all_gather(packed, "span", axis=0, tiled=True)
+    parts = lax.axis_size("tm")
+    size = packed.shape[1]
+    chunk = -(-size // (parts * 128)) * 128
+    packed = jnp.pad(packed, ((0, 0), (0, chunk * parts - size))).reshape(1, parts, chunk)
+    mine = lax.dynamic_index_in_dim(packed, lax.axis_index("tm"), 1, keepdims=False)
+    across = lax.all_gather(mine, "span", axis=0, tiled=True)
+    gathered = lax.all_gather(across, "tm", axis=1, tiled=True)[:, :size]
     unpacked = []
     start = 0
     for piece in pieces:

time: 340 us -> 379 us (1.11)
  blocking collectives: 23.9 us -> 63.9 us
  waiting for transfers between devices: 116 us -> 112 us
    all_gather x0 -> x1, blocking collectives: none -> 36.6 us  [shards(): across = lax.all_gather(mine, 'span', axis=0, tiled=True)]
    unnamed x11 -> x9, local copies, waits for them, and re-layouts: 9.86 us -> 10.7 us
  transfers between devices with their start and end apart: 17 -> 17, of which waited for: 10 -> 9; matrix products, arithmetic and copies ran while one was open for 4% -> 4% of each run, Pallas kernels for 0% -> 0%
where the time goes in v7:
time: 379 us; the launch traced here: 378 us
  waiting for transfers between devices  112 us (30%)
  Pallas kernels  96.6 us (25%)
  blocking collectives  63.9 us (17%)
  local copies, waits for them, and re-layouts  44.7 us (12%)
  starting transfers between devices  36.6 us (10%)
  between operations  13.5 us (4%)
  other arithmetic  10.7 us (3%)
    pallas_call x8, Pallas kernels, group_pass(): return kernel(scalars, nonlinear, left, signal, right, taps, coupling, gain)  96.6 us
    all_gather x1, waiting for transfers between devices, shards(): gathered = lax.all_gather(across, 'tm', axis=1, tiled=True)[:, :size]  67.4 us
    ppermute x8, waiting for transfers between devices, group_pass(): left = lax.ppermute(signal, 'tm', forward)  44.3 us
    all_gather x1, blocking collectives, shards(): across = lax.all_gather(mine, 'span', axis=0, tiled=True)  36.6 us
    all_to_all x1, blocking collectives, shards(): return lax.all_to_all(stacked, 'span', 0, 1, tiled=True)  27.3 us
    ppermute x8, starting transfers between devices, group_pass(): left = lax.ppermute(signal, 'tm', forward)  18.8 us
    ppermute x8, starting transfers between devices, group_pass(): right = lax.ppermute(signal, 'tm', backward)  17.8 us
    unnamed x9, local copies, waits for them, and re-layouts  10.7 us
  transfers between devices with their start and end apart: 17, of which 9 were waited for; matrix products, arithmetic and copies ran while one was open for 4% of the time, Pallas kernels for 0%

profile of v7, /device:TPU:2, one launch (start us, length us, event | category | flops | bytes accessed | tf_op | source)
XLA Modules:
  0.0 378.3 jit_solution(14078318092807167354)
XLA Ops:
  10.8 4.1 %dynamic-update-slice = f32[1,98056]{1,0:T(1,128)S(1)} dynamic-update-slice(f32[1,98056]{1,0:T(1,128)S(1)} %custom-call, f32[1,96800]{1,0:T(1,128)S(1)} %reshape.34, s32[]{} %constant.47, s32[]{} %constant.47) | dynamic-update-slice | bytes 774404
  16.9 36.6 %all-gather = f32[8,1,3072]{2,1,0:T(1,128)} all-gather(f32[1,1,3072]{2,1,0:T(1,128)S(1)} %constant_dynamic-slice_fusion), channel_id=2, replica_groups=mesh['span'=8,'tm'=32] {'span'}, dimensions={0}, use_global_device_ids=true | all-gather | bytes 110592 | tf_op jit(solution)/shard_map/all_gather | solution.py:126
  53.6 67.4 %all-gather.4.cloned.1.call-done = f32[8,1,98304]{2,1,0:T(1,128)} async-done(((f32[8,1,3072]{2,1,0:T(1,128)}), f32[8,1,98304]{2,1,0:T(1,128)}) %all-gather.4.cloned.1.call-update) | async-done | bytes 3145744 | tf_op jit(solution)/shard_map/all_gather | solution.py:127
  121.0 3.7 copy.37
  127.2 7.0 %reshape.41 = f32[8,2,2,2,110,110]{5,4,3,2,1,0:T(8,128)} reshape(f32[8,96800]{1,0:T(8,128)} %slice.27) | data formatting | bytes 6195200 | tf_op jit(solution)/shard_map/reshape | solution.py:132
  134.2 4.5 %pad.23 = f32[8,2,2,2,128,128]{5,4,3,2,1,0:T(8,128)} pad(f32[8,2,2,2,110,110]{5,4,3,2,1,0:T(8,128)} %reshape.41, f32[]{:T(128)} %constant.26.clone.1), padding=0_0x0_0x0_0x0_0x0_18x0_18 | pad | bytes 7291908 | tf_op jit(solution)/shard_map/jit(_pad)/pad | solution.py:139
  139.1 201.7 %while.12 = (s32[]{:T(128)}, f32[1,2,128,256]{3,2,1,0:T(8,128)S(1)}, f32[8,1,2,128,256]{4,2,3,1,0:T(2,128)}, s32[8]{0:T(128)S(1)}, s32[]{:T(128)}, /*index=5*/f3...) while((s32[]{:T(128)}, ...), condition=%wide.region_1.2_spmd, body=%wide.region_0.1_spmd.sunk | while | flops 4026531840 | bytes 6824213 | solution.py:156
  139.3 4.4 %collective-permute-start.1 = (f32[2,128,256]{2,1,0:T(8,128)S(1)}, f32[2,128,256]{2,1,0:T(8,128)S(1)}, u32[]{:S(2)}, u32[]{:S(2)}) collective-permute-start(f32[2,128,256]{2,1,0:T(8,128)S(1)} %copy.55.mid_ref), channel_id=1, source_target_pairs={{1,0},{2,1},{3,2},{4,3},{5,4},{6,5},{7,6},{8,7},{9,8},{10,9},{11,1... | collective-permute-start | bytes 786440 | tf_op jit(solution)/shard_map/while/body/eval_jaxpr/ppermute | solution.py:81
  147.7 6.0 %collective-permute-done.left_ref = f32[2,128,256]{2,1,0:T(8,128)} collective-permute-done((f32[2,128,256]{2,1,0:T(8,128)S(1)}, f32[2,128,256]{2,1,0:T(8,128)}, u32[]{:S(2)}, u32[]{:S(2)}) %collective-permute-start) | collective-permute-done | bytes 262176 | tf_op jit(solution)/shard_map/while/body/eval_jaxpr/ppermute | solution.py:80
  153.6 12.1 %eval_jaxpr.1 = f32[2,128,256]{2,1,0:T(8,128)S(1)} custom-call(s32[2]{0:T(128)} %pad_add_fusion.2.scalar_ref, f32[8,4]{1,0:T(8,128)S(1)} %get-tuple-element.178.nonlinear_ref, f32[2,128,256]{2,1,0:T(8,128)} %collective-permute-done.left_ref, f32[2,128,256]{2,1,0:T(8,128)} %copy-done.1, f32[2,128,256]{2,1,0:T(8,128)} %copy-done.2, ...), custom_call_target="tpu_custom_call" | custom-call | flops 4026531840 | bytes 1581056 | tf_op jit(solution)/shard_map/while/body/eval_jaxpr/pallas_call | solution.py:108
  168.6 2.4 collective-permute-start
  173.0 5.5 %collective-permute-done.left_ref = f32[2,128,256]{2,1,0:T(8,128)} collective-permute-done((f32[2,128,256]{2,1,0:T(8,128)S(1)}, f32[2,128,256]{2,1,0:T(8,128)}, u32[]{:S(2)}, u32[]{:S(2)}) %collective-permute-start) | collective-permute-done | bytes 262176 | tf_op jit(solution)/shard_map/while/body/eval_jaxpr/ppermute | solution.py:80
  178.5 12.1 %eval_jaxpr.1 = f32[2,128,256]{2,1,0:T(8,128)S(1)} custom-call(s32[2]{0:T(128)} %pad_add_fusion.2.scalar_ref, f32[8,4]{1,0:T(8,128)S(1)} %get-tuple-element.178.nonlinear_ref, f32[2,128,256]{2,1,0:T(8,128)} %collective-permute-done.left_ref, f32[2,128,256]{2,1,0:T(8,128)} %copy-done.1, f32[2,128,256]{2,1,0:T(8,128)} %copy-done.2, ...), custom_call_target="tpu_custom_call" | custom-call | flops 4026531840 | bytes 1581056 | tf_op jit(solution)/shard_map/while/body/eval_jaxpr/pallas_call | solution.py:108
  193.5 2.4 collective-permute-start
  197.9 5.5 %collective-permute-done.left_ref = f32[2,128,256]{2,1,0:T(8,128)} collective-permute-done((f32[2,128,256]{2,1,0:T(8,128)S(1)}, f32[2,128,256]{2,1,0:T(8,128)}, u32[]{:S(2)}, u32[]{:S(2)}) %collective-permute-start) | collective-permute-done | bytes 262176 | tf_op jit(solution)/shard_map/while/body/eval_jaxpr/ppermute | solution.py:80
  203.4 12.1 %eval_jaxpr.1 = f32[2,128,256]{2,1,0:T(8,128)S(1)} custom-call(s32[2]{0:T(128)} %pad_add_fusion.2.scalar_ref, f32[8,4]{1,0:T(8,128)S(1)} %get-tuple-element.178.nonlinear_ref, f32[2,128,256]{2,1,0:T(8,128)} %collective-permute-done.left_ref, f32[2,128,256]{2,1,0:T(8,128)} %copy-done.1, f32[2,128,256]{2,1,0:T(8,128)} %copy-done.2, ...), custom_call_target="tpu_custom_call" | custom-call | flops 4026531840 | bytes 1581056 | tf_op jit(solution)/shard_map/while/body/eval_jaxpr/pallas_call | solution.py:108
  218.4 2.4 collective-permute-start
  222.8 5.5 %collective-permute-done.left_ref = f32[2,128,256]{2,1,0:T(8,128)} collective-permute-done((f32[2,128,256]{2,1,0:T(8,128)S(1)}, f32[2,128,256]{2,1,0:T(8,128)}, u32[]{:S(2)}, u32[]{:S(2)}) %collective-permute-start) | collective-permute-done | bytes 262176 | tf_op jit(solution)/shard_map/while/body/eval_jaxpr/ppermute | solution.py:80
  228.3 12.1 %eval_jaxpr.1 = f32[2,128,256]{2,1,0:T(8,128)S(1)} custom-call(s32[2]{0:T(128)} %pad_add_fusion.2.scalar_ref, f32[8,4]{1,0:T(8,128)S(1)} %get-tuple-element.178.nonlinear_ref, f32[2,128,256]{2,1,0:T(8,128)} %collective-permute-done.left_ref, f32[2,128,256]{2,1,0:T(8,128)} %copy-done.1, f32[2,128,256]{2,1,0:T(8,128)} %copy-done.2, ...), custom_call_target="tpu_custom_call" | custom-call | flops 4026531840 | bytes 1581056 | tf_op jit(solution)/shard_map/while/body/eval_jaxpr/pallas_call | solution.py:108
  243.2 2.4 collective-permute-start
  247.7 5.5 %collective-permute-done.left_ref = f32[2,128,256]{2,1,0:T(8,128)} collective-permute-done((f32[2,128,256]{2,1,0:T(8,128)S(1)}, f32[2,128,256]{2,1,0:T(8,128)}, u32[]{:S(2)}, u32[]{:S(2)}) %collective-permute-start) | collective-permute-done | bytes 262176 | tf_op jit(solution)/shard_map/while/body/eval_jaxpr/ppermute | solution.py:80
  253.2 12.1 %eval_jaxpr.1 = f32[2,128,256]{2,1,0:T(8,128)S(1)} custom-call(s32[2]{0:T(128)} %pad_add_fusion.2.scalar_ref, f32[8,4]{1,0:T(8,128)S(1)} %get-tuple-element.178.nonlinear_ref, f32[2,128,256]{2,1,0:T(8,128)} %collective-permute-done.left_ref, f32[2,128,256]{2,1,0:T(8,128)} %copy-done.1, f32[2,128,256]{2,1,0:T(8,128)} %copy-done.2, ...), custom_call_target="tpu_custom_call" | custom-call | flops 4026531840 | bytes 1581056 | tf_op jit(solution)/shard_map/while/body/eval_jaxpr/pallas_call | solution.py:108
  268.1 2.4 collective-permute-start
  272.6 5.5 %collective-permute-done.left_ref = f32[2,128,256]{2,1,0:T(8,128)} collective-permute-done((f32[2,128,256]{2,1,0:T(8,128)S(1)}, f32[2,128,256]{2,1,0:T(8,128)}, u32[]{:S(2)}, u32[]{:S(2)}) %collective-permute-start) | collective-permute-done | bytes 262176 | tf_op jit(solution)/shard_map/while/body/eval_jaxpr/ppermute | solution.py:80
  278.0 12.1 %eval_jaxpr.1 = f32[2,128,256]{2,1,0:T(8,128)S(1)} custom-call(s32[2]{0:T(128)} %pad_add_fusion.2.scalar_ref, f32[8,4]{1,0:T(8,128)S(1)} %get-tuple-element.178.nonlinear_ref, f32[2,128,256]{2,1,0:T(8,128)} %collective-permute-done.left_ref, f32[2,128,256]{2,1,0:T(8,128)} %copy-done.1, f32[2,128,256]{2,1,0:T(8,128)} %copy-done.2, ...), custom_call_target="tpu_custom_call" | custom-call | flops 4026531840 | bytes 1581056 | tf_op jit(solution)/shard_map/while/body/eval_jaxpr/pallas_call | solution.py:108
  293.0 2.4 collective-permute-start
  297.4 5.5 %collective-permute-done.left_ref = f32[2,128,256]{2,1,0:T(8,128)} collective-permute-done((f32[2,128,256]{2,1,0:T(8,128)S(1)}, f32[2,128,256]{2,1,0:T(8,128)}, u32[]{:S(2)}, u32[]{:S(2)}) %collective-permute-start) | collective-permute-done | bytes 262176 | tf_op jit(solution)/shard_map/while/body/eval_jaxpr/ppermute | solution.py:80
  302.9 12.1 %eval_jaxpr.1 = f32[2,128,256]{2,1,0:T(8,128)S(1)} custom-call(s32[2]{0:T(128)} %pad_add_fusion.2.scalar_ref, f32[8,4]{1,0:T(8,128)S(1)} %get-tuple-element.178.nonlinear_ref, f32[2,128,256]{2,1,0:T(8,128)} %collective-permute-done.left_ref, f32[2,128,256]{2,1,0:T(8,128)} %copy-done.1, f32[2,128,256]{2,1,0:T(8,128)} %copy-done.2, ...), custom_call_target="tpu_custom_call" | custom-call | flops 4026531840 | bytes 1581056 | tf_op jit(solution)/shard_map/while/body/eval_jaxpr/pallas_call | solution.py:108
  317.9 2.4 collective-permute-start
  322.3 5.5 %collective-permute-done.left_ref = f32[2,128,256]{2,1,0:T(8,128)} collective-permute-done((f32[2,128,256]{2,1,0:T(8,128)S(1)}, f32[2,128,256]{2,1,0:T(8,128)}, u32[]{:S(2)}, u32[]{:S(2)}) %collective-permute-start) | collective-permute-done | bytes 262176 | tf_op jit(solution)/shard_map/while/body/eval_jaxpr/ppermute | solution.py:80
  327.8 12.1 %eval_jaxpr.1 = f32[2,128,256]{2,1,0:T(8,128)S(1)} custom-call(s32[2]{0:T(128)} %pad_add_fusion.2.scalar_ref, f32[8,4]{1,0:T(8,128)S(1)} %get-tuple-element.178.nonlinear_ref, f32[2,128,256]{2,1,0:T(8,128)} %collective-permute-done.left_ref, f32[2,128,256]{2,1,0:T(8,128)} %copy-done.1, f32[2,128,256]{2,1,0:T(8,128)} %copy-done.2, ...), custom_call_target="tpu_custom_call" | custom-call | flops 4026531840 | bytes 1581056 | tf_op jit(solution)/shard_map/while/body/eval_jaxpr/pallas_call | solution.py:108
  342.9 27.3 %all_to_all.12 = f32[8,1,2,110,256]{4,2,3,1,0:T(2,128)S(1)} all-to-all(f32[8,1,2,110,256]{4,2,3,1,0:T(2,128)S(1)} %slice.24), channel_id=1, replica_groups=mesh['span'=8,'tm'=32] {'span'}, dimensions={0} | all-to-all | bytes 3604480 | tf_op jit(solution)/shard_map/all_to_all | solution.py:158
  (113 shorter events, 51.5 us)
Async XLA Ops:
  6.5 46.9 %copy-start = (f32[8,2,110,256]{3,1,2,0:T(2,128)S(1)}, f32[8,2,110,256]{3,1,2,0:T(2,128)}, u32[]{:S(2)}) copy-start(f32[8,2,110,256]{3,1,2,0:T(2,128)} %param.7) | copy-start | bytes 5406724
  6.5 114.5 %all-gather.4.cloned.1.call-start = ((), (), s32[]{:S(2)}) async-start(), calls=%async_computation.1 | async-start | bytes 3244032 | tf_op jit(solution)/shard_map/all_gather | solution.py:127
  139.3 14.3 %copy-start.1 = (f32[2,128,256]{2,1,0:T(8,128)}, f32[2,128,256]{2,1,0:T(8,128)S(1)}, u32[]{:S(2)}) copy-start(f32[2,128,256]{2,1,0:T(8,128)S(1)} %copy.55.mid_ref) | copy-start | bytes 786436 | tf_op jit(solution)/shard_map/while
  139.3 8.3 %collective-permute-start.1 = (f32[2,128,256]{2,1,0:T(8,128)S(1)}, f32[2,128,256]{2,1,0:T(8,128)S(1)}, u32[]{:S(2)}, u32[]{:S(2)}) collective-permute-start(f32[2,128,256]{2,1,0:T(8,128)S(1)} %copy.55.mid_ref), channel_id=1, source_target_pairs={{1,0},{2,1},{3,2},{4,3},{5,4},{6,5},{7,6},{8,7},{9,8},{10,9},{11,1... | collective-permute-start | bytes 786440 | tf_op jit(solution)/shard_map/while/body/eval_jaxpr/ppermute | solution.py:81
  143.7 9.9 %collective-permute-start = (f32[2,128,256]{2,1,0:T(8,128)S(1)}, f32[2,128,256]{2,1,0:T(8,128)}, u32[]{:S(2)}, u32[]{:S(2)}) collective-permute-start(f32[2,128,256]{2,1,0:T(8,128)S(1)} %copy.55.mid_ref), channel_id=1, source_target_pairs={{0,1},{1,2},{2,3},{3,4},{4,5},{5,6},{6,7},{7,8},{8,9},{9,10},{10,1... | collective-permute-start | bytes 786440 | tf_op jit(solution)/shard_map/while/body/eval_jaxpr/ppermute | solution.py:80
  147.7 6.0 %copy-start.2 = (f32[2,128,256]{2,1,0:T(8,128)}, f32[2,128,256]{2,1,0:T(8,128)S(1)}, u32[]{:S(2)}) copy-start(f32[2,128,256]{2,1,0:T(8,128)S(1)} %collective-permute-done.1.right_ref) | copy-start | bytes 786436 | tf_op jit(solution)/shard_map/while
  166.6 11.9 %copy-start.1 = (f32[2,128,256]{2,1,0:T(8,128)}, f32[2,128,256]{2,1,0:T(8,128)S(1)}, u32[]{:S(2)}) copy-start(f32[2,128,256]{2,1,0:T(8,128)S(1)} %copy.55.mid_ref) | copy-start | bytes 786436 | tf_op jit(solution)/shard_map/while
  166.6 6.4 %collective-permute-start.1 = (f32[2,128,256]{2,1,0:T(8,128)S(1)}, f32[2,128,256]{2,1,0:T(8,128)S(1)}, u32[]{:S(2)}, u32[]{:S(2)}) collective-permute-start(f32[2,128,256]{2,1,0:T(8,128)S(1)} %copy.55.mid_ref), channel_id=1, source_target_pairs={{1,0},{2,1},{3,2},{4,3},{5,4},{6,5},{7,6},{8,7},{9,8},{10,9},{11,1... | collective-permute-start | bytes 786440 | tf_op jit(solution)/shard_map/while/body/eval_jaxpr/ppermute | solution.py:81
  168.6 9.9 %collective-permute-start = (f32[2,128,256]{2,1,0:T(8,128)S(1)}, f32[2,128,256]{2,1,0:T(8,128)}, u32[]{:S(2)}, u32[]{:S(2)}) collective-permute-start(f32[2,128,256]{2,1,0:T(8,128)S(1)} %copy.55.mid_ref), channel_id=1, source_target_pairs={{0,1},{1,2},{2,3},{3,4},{4,5},{5,6},{6,7},{7,8},{8,9},{9,10},{10,1... | collective-permute-start | bytes 786440 | tf_op jit(solution)/shard_map/while/body/eval_jaxpr/ppermute | solution.py:80
  173.0 5.5 %copy-start.2 = (f32[2,128,256]{2,1,0:T(8,128)}, f32[2,128,256]{2,1,0:T(8,128)S(1)}, u32[]{:S(2)}) copy-start(f32[2,128,256]{2,1,0:T(8,128)S(1)} %collective-permute-done.1.right_ref) | copy-start | bytes 786436 | tf_op jit(solution)/shard_map/while
  191.5 11.9 %copy-start.1 = (f32[2,128,256]{2,1,0:T(8,128)}, f32[2,128,256]{2,1,0:T(8,128)S(1)}, u32[]{:S(2)}) copy-start(f32[2,128,256]{2,1,0:T(8,128)S(1)} %copy.55.mid_ref) | copy-start | bytes 786436 | tf_op jit(solution)/shard_map/while
  191.6 6.4 %collective-permute-start.1 = (f32[2,128,256]{2,1,0:T(8,128)S(1)}, f32[2,128,256]{2,1,0:T(8,128)S(1)}, u32[]{:S(2)}, u32[]{:S(2)}) collective-permute-start(f32[2,128,256]{2,1,0:T(8,128)S(1)} %copy.55.mid_ref), channel_id=1, source_target_pairs={{1,0},{2,1},{3,2},{4,3},{5,4},{6,5},{7,6},{8,7},{9,8},{10,9},{11,1... | collective-permute-start | bytes 786440 | tf_op jit(solution)/shard_map/while/body/eval_jaxpr/ppermute | solution.py:81
  193.5 9.9 %collective-permute-start = (f32[2,128,256]{2,1,0:T(8,128)S(1)}, f32[2,128,256]{2,1,0:T(8,128)}, u32[]{:S(2)}, u32[]{:S(2)}) collective-permute-start(f32[2,128,256]{2,1,0:T(8,128)S(1)} %copy.55.mid_ref), channel_id=1, source_target_pairs={{0,1},{1,2},{2,3},{3,4},{4,5},{5,6},{6,7},{7,8},{8,9},{9,10},{10,1... | collective-permute-start | bytes 786440 | tf_op jit(solution)/shard_map/while/body/eval_jaxpr/ppermute | solution.py:80
  197.9 5.5 %copy-start.2 = (f32[2,128,256]{2,1,0:T(8,128)}, f32[2,128,256]{2,1,0:T(8,128)S(1)}, u32[]{:S(2)}) copy-start(f32[2,128,256]{2,1,0:T(8,128)S(1)} %collective-permute-done.1.right_ref) | copy-start | bytes 786436 | tf_op jit(solution)/shard_map/while
  216.4 11.9 %copy-start.1 = (f32[2,128,256]{2,1,0:T(8,128)}, f32[2,128,256]{2,1,0:T(8,128)S(1)}, u32[]{:S(2)}) copy-start(f32[2,128,256]{2,1,0:T(8,128)S(1)} %copy.55.mid_ref) | copy-start | bytes 786436 | tf_op jit(solution)/shard_map/while
  216.4 6.4 %collective-permute-start.1 = (f32[2,128,256]{2,1,0:T(8,128)S(1)}, f32[2,128,256]{2,1,0:T(8,128)S(1)}, u32[]{:S(2)}, u32[]{:S(2)}) collective-permute-start(f32[2,128,256]{2,1,0:T(8,128)S(1)} %copy.55.mid_ref), channel_id=1, source_target_pairs={{1,0},{2,1},{3,2},{4,3},{5,4},{6,5},{7,6},{8,7},{9,8},{10,9},{11,1... | collective-permute-start | bytes 786440 | tf_op jit(solution)/shard_map/while/body/eval_jaxpr/ppermute | solution.py:81
  218.4 9.9 %collective-permute-start = (f32[2,128,256]{2,1,0:T(8,128)S(1)}, f32[2,128,256]{2,1,0:T(8,128)}, u32[]{:S(2)}, u32[]{:S(2)}) collective-permute-start(f32[2,128,256]{2,1,0:T(8,128)S(1)} %copy.55.mid_ref), channel_id=1, source_target_pairs={{0,1},{1,2},{2,3},{3,4},{4,5},{5,6},{6,7},{7,8},{8,9},{9,10},{10,1... | collective-permute-start | bytes 786440 | tf_op jit(solution)/shard_map/while/body/eval_jaxpr/ppermute | solution.py:80
  222.8 5.5 %copy-start.2 = (f32[2,128,256]{2,1,0:T(8,128)}, f32[2,128,256]{2,1,0:T(8,128)S(1)}, u32[]{:S(2)}) copy-start(f32[2,128,256]{2,1,0:T(8,128)S(1)} %collective-permute-done.1.right_ref) | copy-start | bytes 786436 | tf_op jit(solution)/shard_map/while
  241.3 11.9 %copy-start.1 = (f32[2,128,256]{2,1,0:T(8,128)}, f32[2,128,256]{2,1,0:T(8,128)S(1)}, u32[]{:S(2)}) copy-start(f32[2,128,256]{2,1,0:T(8,128)S(1)} %copy.55.mid_ref) | copy-start | bytes 786436 | tf_op jit(solution)/shard_map/while
  241.3 6.4 %collective-permute-start.1 = (f32[2,128,256]{2,1,0:T(8,128)S(1)}, f32[2,128,256]{2,1,0:T(8,128)S(1)}, u32[]{:S(2)}, u32[]{:S(2)}) collective-permute-start(f32[2,128,256]{2,1,0:T(8,128)S(1)} %copy.55.mid_ref), channel_id=1, source_target_pairs={{1,0},{2,1},{3,2},{4,3},{5,4},{6,5},{7,6},{8,7},{9,8},{10,9},{11,1... | collective-permute-start | bytes 786440 | tf_op jit(solution)/shard_map/while/body/eval_jaxpr/ppermute | solution.py:81
  243.2 9.9 %collective-permute-start = (f32[2,128,256]{2,1,0:T(8,128)S(1)}, f32[2,128,256]{2,1,0:T(8,128)}, u32[]{:S(2)}, u32[]{:S(2)}) collective-permute-start(f32[2,128,256]{2,1,0:T(8,128)S(1)} %copy.55.mid_ref), channel_id=1, source_target_pairs={{0,1},{1,2},{2,3},{3,4},{4,5},{5,6},{6,7},{7,8},{8,9},{9,10},{10,1... | collective-permute-start | bytes 786440 | tf_op jit(solution)/shard_map/while/body/eval_jaxpr/ppermute | solution.py:80
  247.7 5.5 %copy-start.2 = (f32[2,128,256]{2,1,0:T(8,128)}, f32[2,128,256]{2,1,0:T(8,128)S(1)}, u32[]{:S(2)}) copy-start(f32[2,128,256]{2,1,0:T(8,128)S(1)} %collective-permute-done.1.right_ref) | copy-start | bytes 786436 | tf_op jit(solution)/shard_map/while
  266.2 11.9 %copy-start.1 = (f32[2,128,256]{2,1,0:T(8,128)}, f32[2,128,256]{2,1,0:T(8,128)S(1)}, u32[]{:S(2)}) copy-start(f32[2,128,256]{2,1,0:T(8,128)S(1)} %copy.55.mid_ref) | copy-start | bytes 786436 | tf_op jit(solution)/shard_map/while
  266.2 6.4 %collective-permute-start.1 = (f32[2,128,256]{2,1,0:T(8,128)S(1)}, f32[2,128,256]{2,1,0:T(8,128)S(1)}, u32[]{:S(2)}, u32[]{:S(2)}) collective-permute-start(f32[2,128,256]{2,1,0:T(8,128)S(1)} %copy.55.mid_ref), channel_id=1, source_target_pairs={{1,0},{2,1},{3,2},{4,3},{5,4},{6,5},{7,6},{8,7},{9,8},{10,9},{11,1... | collective-permute-start | bytes 786440 | tf_op jit(solution)/shard_map/while/body/eval_jaxpr/ppermute | solution.py:81
  268.1 9.9 %collective-permute-start = (f32[2,128,256]{2,1,0:T(8,128)S(1)}, f32[2,128,256]{2,1,0:T(8,128)}, u32[]{:S(2)}, u32[]{:S(2)}) collective-permute-start(f32[2,128,256]{2,1,0:T(8,128)S(1)} %copy.55.mid_ref), channel_id=1, source_target_pairs={{0,1},{1,2},{2,3},{3,4},{4,5},{5,6},{6,7},{7,8},{8,9},{9,10},{10,1... | collective-permute-start | bytes 786440 | tf_op jit(solution)/shard_map/while/body/eval_jaxpr/ppermute | solution.py:80
  272.6 5.5 %copy-start.2 = (f32[2,128,256]{2,1,0:T(8,128)}, f32[2,128,256]{2,1,0:T(8,128)S(1)}, u32[]{:S(2)}) copy-start(f32[2,128,256]{2,1,0:T(8,128)S(1)} %collective-permute-done.1.right_ref) | copy-start | bytes 786436 | tf_op jit(solution)/shard_map/while
  291.1 11.9 %copy-start.1 = (f32[2,128,256]{2,1,0:T(8,128)}, f32[2,128,256]{2,1,0:T(8,128)S(1)}, u32[]{:S(2)}) copy-start(f32[2,128,256]{2,1,0:T(8,128)S(1)} %copy.55.mid_ref) | copy-start | bytes 786436 | tf_op jit(solution)/shard_map/while
  291.1 6.4 %collective-permute-start.1 = (f32[2,128,256]{2,1,0:T(8,128)S(1)}, f32[2,128,256]{2,1,0:T(8,128)S(1)}, u32[]{:S(2)}, u32[]{:S(2)}) collective-permute-start(f32[2,128,256]{2,1,0:T(8,128)S(1)} %copy.55.mid_ref), channel_id=1, source_target_pairs={{1,0},{2,1},{3,2},{4,3},{5,4},{6,5},{7,6},{8,7},{9,8},{10,9},{11,1... | collective-permute-start | bytes 786440 | tf_op jit(solution)/shard_map/while/body/eval_jaxpr/ppermute | solution.py:81
  293.0 9.9 %collective-permute-start = (f32[2,128,256]{2,1,0:T(8,128)S(1)}, f32[2,128,256]{2,1,0:T(8,128)}, u32[]{:S(2)}, u32[]{:S(2)}) collective-permute-start(f32[2,128,256]{2,1,0:T(8,128)S(1)} %copy.55.mid_ref), channel_id=1, source_target_pairs={{0,1},{1,2},{2,3},{3,4},{4,5},{5,6},{6,7},{7,8},{8,9},{9,10},{10,1... | collective-permute-start | bytes 786440 | tf_op jit(solution)/shard_map/while/body/eval_jaxpr/ppermute | solution.py:80
  315.9 11.9 %copy-start.1 = (f32[2,128,256]{2,1,0:T(8,128)}, f32[2,128,256]{2,1,0:T(8,128)S(1)}, u32[]{:S(2)}) copy-start(f32[2,128,256]{2,1,0:T(8,128)S(1)} %copy.55.mid_ref) | copy-start | bytes 786436 | tf_op jit(solution)/shard_map/while
  315.9 6.4 %collective-permute-start.1 = (f32[2,128,256]{2,1,0:T(8,128)S(1)}, f32[2,128,256]{2,1,0:T(8,128)S(1)}, u32[]{:S(2)}, u32[]{:S(2)}) collective-permute-start(f32[2,128,256]{2,1,0:T(8,128)S(1)} %copy.55.mid_ref), channel_id=1, source_target_pairs={{1,0},{2,1},{3,2},{4,3},{5,4},{6,5},{7,6},{8,7},{9,8},{10,9},{11,1... | collective-permute-start | bytes 786440 | tf_op jit(solution)/shard_map/while/body/eval_jaxpr/ppermute | solution.py:81
  317.9 9.9 %collective-permute-start = (f32[2,128,256]{2,1,0:T(8,128)S(1)}, f32[2,128,256]{2,1,0:T(8,128)}, u32[]{:S(2)}, u32[]{:S(2)}) collective-permute-start(f32[2,128,256]{2,1,0:T(8,128)S(1)} %copy.55.mid_ref), channel_id=1, source_target_pairs={{0,1},{1,2},{2,3},{3,4},{4,5},{5,6},{6,7},{7,8},{8,9},{9,10},{10,1... | collective-permute-start | bytes 786440 | tf_op jit(solution)/shard_map/while/body/eval_jaxpr/ppermute | solution.py:80
  (2 other events, 11.0 us)
Sparse Core Ops, SparseCore 0:
  53.6 67.3 all-gather.3
